TPU v7x, 512 devices: a whole 4x4x16 slice. The times are simulated.
512 devices in a mesh: pipe: 16 (over y, x), seq: 32 (over z, core).
Axes of the slice: x: 4, y: 4, z: 16, core: 2. Of those that a mesh axis runs over, the one named last changes fastest.
Arguments:
- queries: bfloat16 [16, 2, 4096, 2048], P('pipe', None, 'seq'), may hold values from -120 to 120
- keys: bfloat16 [16, 2, 4096, 512], P('pipe', None, 'seq'), may hold values from -5 to 5
- values: bfloat16 [16, 2, 4096, 512], P('pipe', None, 'seq'), may hold values from -6 to 6
- out_grad: bfloat16 [2, 4096, 2048], P(None, 'seq'), may hold values from -6 to 6
- segments: int32 [2, 4096], replicated, may hold values from 0 to 63, never falling along the last dimension, each value on 1 to 256 neighbouring positions
Outputs:
- query_grads: bfloat16 [16, 2, 4096, 2048], P('pipe', None, 'seq')
- key_grads: bfloat16 [16, 2, 4096, 512], P('pipe', None, 'seq')
- value_grads: bfloat16 [16, 2, 4096, 512], P('pipe', None, 'seq')
Inputs may be any that keep to these rules, and one draw needn't show every extreme that they name: `segments`: segment numbers never fall along a micro-batch.
All inputs are finite; a program needn't handle non-finite values.
Results may differ from a plain program's by a relative error of at most 0.014.
Values may be sent and summed in bfloat16 or wider, within the bound.
No kernel may reach another device: no remote copies, remote signals or barrier semaphores. Data moves between devices by JAX's collectives and lax.ppermute only.
A program may use at most 64 MiB of HBM per device.

v0:
```python
import jax
import jax.numpy as jnp
from jax import lax
from jax.sharding import PartitionSpec as P

DH = 128
WINDOW = 128


def from_behind(block, axis, distance):
    devices = range(lax.axis_size(axis))
    route = [(i - distance, i) for i in devices if i - distance in devices]
    return lax.ppermute(block, axis, route)


def tile_backward(query, key_rows, value_rows, grad_out, allowed):
    row_count = query.shape[0]
    key_count = key_rows.shape[0]
    kv_heads = key_rows.shape[1] // DH
    group_size = query.shape[1] // (kv_heads * DH)
    score_scale = DH ** (-0.5)
    query_heads = query.reshape(row_count, kv_heads, group_size, DH)
    grad_heads = grad_out.reshape(row_count, kv_heads, group_size, DH)
    key_heads = key_rows.reshape(key_count, kv_heads, DH)
    value_heads = value_rows.reshape(key_count, kv_heads, DH)
    scores = (
        jnp.einsum("qhgd,khd->hgqk", query_heads, key_heads, preferred_element_type=jnp.float32)
        * score_scale
    )
    masked = jnp.where(allowed, scores, -jnp.inf)
    row_max = jnp.max(masked, axis=-1, keepdims=True)
    weights = jnp.exp(masked - row_max)
    probability = weights / jnp.sum(weights, axis=-1, keepdims=True)
    prob_low = probability.astype(jnp.bfloat16)
    output = jnp.einsum("hgqk,khd->qhgd", prob_low, value_heads, preferred_element_type=jnp.float32)
    grad_prob = jnp.einsum(
        "qhgd,khd->hgqk", grad_heads, value_heads, preferred_element_type=jnp.float32
    )
    grad_dot = jnp.transpose(jnp.sum(grad_heads.astype(jnp.float32) * output, axis=-1), (1, 2, 0))[
        ..., None
    ]
    grad_score = (probability * (grad_prob - grad_dot)).astype(jnp.bfloat16)
    query_grad = (
        jnp.einsum("hgqk,khd->qhgd", grad_score, key_heads, preferred_element_type=jnp.float32)
        * score_scale
    )
    key_grad = (
        jnp.einsum("hgqk,qhgd->khd", grad_score, query_heads, preferred_element_type=jnp.float32)
        * score_scale
    )
    value_grad = jnp.einsum(
        "hgqk,qhgd->khd", prob_low, grad_heads, preferred_element_type=jnp.float32
    )
    return (
        query_grad.reshape(row_count, -1),
        key_grad.reshape(key_count, -1),
        value_grad.reshape(key_count, -1),
    )


def item_backward(query, key_rows, value_rows, grad_out, allowed):
    return tile_backward(query, key_rows, value_rows, grad_out, allowed)


def per_device(queries, keys, values, out_grad, segments):
    micro_count = queries.shape[1]
    row_count = queries.shape[2]
    query_width = queries.shape[3]
    key_width = keys.shape[3]
    section_count = lax.axis_size("pipe")
    section_index = lax.axis_index("pipe")
    seq_index = lax.axis_index("seq")
    own_query = queries[0]
    own_key = keys[0]
    own_value = values[0]
    seg_padded = jnp.concatenate(
        [jnp.full((micro_count, row_count), -1, jnp.int32), segments], axis=1
    )
    query_pos = seq_index * row_count + jnp.arange(row_count, dtype=jnp.int32)
    key_pos = seq_index * row_count - row_count + jnp.arange(2 * row_count, dtype=jnp.int32)
    seg_query = lax.dynamic_slice_in_dim(
        seg_padded, seq_index * row_count + row_count, row_count, axis=1
    )
    seg_key = lax.dynamic_slice_in_dim(seg_padded, seq_index * row_count, 2 * row_count, axis=1)
    near = (
        (key_pos[None, :] <= query_pos[:, None])
        & (query_pos[:, None] - key_pos[None, :] < WINDOW)
        & (key_pos[None, :] >= 0)
    )
    masks = near[None] & (seg_query[:, :, None] == seg_key[:, None, :])
    halo_key, halo_value = from_behind((own_key, own_value), "seq", 1)
    key_rows = jnp.concatenate([halo_key, own_key], axis=1)
    value_rows = jnp.concatenate([halo_value, own_value], axis=1)
    pieces = 1

    def pass_back(sent_grad):
        return from_behind(sent_grad, "pipe", -1)

    item_count = micro_count * pieces
    tick_count = item_count + section_count - 1
    piece_query = query_width // pieces
    piece_key = key_width // pieces

    def tick(tick_step, state_carry):
        sent_grad, query_all, key_all, value_all = state_carry
        incoming = pass_back(sent_grad)
        item_index = tick_step - (section_count - 1 - section_index)
        valid = (item_index >= 0) & (item_index < item_count)
        safe_item = jnp.clip(item_index, 0, item_count - 1)
        batch_index = safe_item // pieces
        half_index = safe_item % pieces

        def do_work(unused):
            query = lax.dynamic_slice(
                own_query, (batch_index, 0, half_index * piece_query), (1, row_count, piece_query)
            )[0]
            key_piece = lax.dynamic_slice(
                key_rows, (batch_index, 0, half_index * piece_key), (1, 2 * row_count, piece_key)
            )[0]
            value_piece = lax.dynamic_slice(
                value_rows, (batch_index, 0, half_index * piece_key), (1, 2 * row_count, piece_key)
            )[0]
            top_grad = lax.dynamic_slice(
                out_grad, (batch_index, 0, half_index * piece_query), (1, row_count, piece_query)
            )[0]
            grad_in = jnp.where(section_index == section_count - 1, top_grad, incoming)
            allowed = lax.dynamic_index_in_dim(masks, batch_index, 0, keepdims=False)
            query_grad, key_grad, value_grad = item_backward(
                query, key_piece, value_piece, grad_in, allowed
            )
            grad_next = (grad_in.astype(jnp.float32) + query_grad).astype(jnp.bfloat16)
            query_new = lax.dynamic_update_slice(
                query_all, grad_next[None], (batch_index, 0, half_index * piece_query)
            )
            key_new = lax.dynamic_update_slice(
                key_all, key_grad[None], (batch_index, 0, half_index * piece_key)
            )
            value_new = lax.dynamic_update_slice(
                value_all, value_grad[None], (batch_index, 0, half_index * piece_key)
            )
            return (grad_next, query_new, key_new, value_new)

        def keep_carry(unused):
            return (sent_grad, query_all, key_all, value_all)

        return lax.cond(valid, do_work, keep_carry, 0)

    start_state = (
        jnp.zeros((row_count, piece_query), jnp.bfloat16),
        jnp.zeros((micro_count, row_count, query_width), jnp.bfloat16),
        jnp.zeros((micro_count, 2 * row_count, key_width), jnp.float32),
        jnp.zeros((micro_count, 2 * row_count, key_width), jnp.float32),
    )
    sent_grad, query_all, key_all, value_all = lax.fori_loop(0, tick_count, tick, start_state)
    back_key, back_value = from_behind(
        (key_all[:, :row_count], value_all[:, :row_count]), "seq", -1
    )
    key_grads = (key_all[:, row_count:] + back_key).astype(jnp.bfloat16)
    value_grads = (value_all[:, row_count:] + back_value).astype(jnp.bfloat16)
    return (query_all[None], key_grads[None], value_grads[None])


def solution(mesh):
    placed = (
        P("pipe", None, "seq", None),
        P("pipe", None, "seq", None),
        P("pipe", None, "seq", None),
        P(None, "seq", None),
        P(),
    )
    return jax.shard_map(
        per_device,
        mesh=mesh,
        in_specs=placed,
        out_specs=(
            P("pipe", None, "seq", None),
            P("pipe", None, "seq", None),
            P("pipe", None, "seq", None),
        ),
        check_vma=False,
    )
```

profile of v0, /device:TPU:97, one launch (start us, length us, event | category | flops | bytes accessed | tf_op | source)
XLA Modules:
  0.0 431.1 jit_solution(320990074752381)
XLA Ops:
  0.6 1.2 copy.32
  1.9 5.3 %collective-permute-start.2 = (bf16[2,128,512]{1,2,0:T(8,128)(2,1)S(1)}, bf16[2,128,512]{1,2,0:T(8,128)(2,1)S(1)}, u32[]{:S(2)}, u32[]{:S(2)}) collective-permute-start(bf16[2,128,512]{1,2,0:T(8,128)(2,1)S(1)} %bitcast.98), channel_id=1, source_target_pairs={{0,1},{1,2},{2,3},{3,4},{4,5},{5,6},{6,7},{7,8},{8,9},{9,10},{10,1... | collective-permute-start | bytes 786440 | tf_op jit(solution)/shard_map/ppermute | solution.py:13
  7.2 1.1 copy.30
  8.3 1.9 collective-permute-start.1
  11.1 2.3 copy.31
  13.4 1.3 copy.33
  16.5 1.1 broadcast_in_dim.48
  17.6 1.1 broadcast.103.clone
  18.7 1.0 broadcast.103
  19.7 378.8 %while.22 = (s32[]{:T(128)}, bf16[128,2048]{0,1:T(8,128)(2,1)S(1)}, bf16[2,128,2048]{1,2,0:T(8,128)(2,1)}, f32[2,256,512]{1,2,0:T(8,128)}, f32[2,256,512]{1,2,0:...) while((s32[]{:T(128)}, bf16[128,2048]{0,1:T(8,128)(2,1)S(1)}, ...), condition=%wide.region_6.7_spmd.clone, body=%wide.region_0.6_spmd.clone.sunk | while | flops 812841216 | bytes 32125980 | solution.py:154
  19.7 1.3 collective-permute-start
  21.0 13.6 %collective-permute-done = bf16[128,2048]{0,1:T(8,128)(2,1)S(1)} collective-permute-done((bf16[128,2048]{0,1:T(8,128)(2,1)S(1)}, bf16[128,2048]{0,1:T(8,128)(2,1)S(1)}, u32[]{:S(2)}, u32[]{:S(2)}) %collective-permute-start) | collective-permute-done | bytes 524320 | tf_op jit(solution)/shard_map/while/body/eval_jaxpr/ppermute | solution.py:13
  34.6 1.3 collective-permute-start
  35.9 12.7 %collective-permute-done = bf16[128,2048]{0,1:T(8,128)(2,1)S(1)} collective-permute-done((bf16[128,2048]{0,1:T(8,128)(2,1)S(1)}, bf16[128,2048]{0,1:T(8,128)(2,1)S(1)}, u32[]{:S(2)}, u32[]{:S(2)}) %collective-permute-start) | collective-permute-done | bytes 524320 | tf_op jit(solution)/shard_map/while/body/eval_jaxpr/ppermute | solution.py:13
  48.6 1.3 collective-permute-start
  49.9 11.9 %collective-permute-done = bf16[128,2048]{0,1:T(8,128)(2,1)S(1)} collective-permute-done((bf16[128,2048]{0,1:T(8,128)(2,1)S(1)}, bf16[128,2048]{0,1:T(8,128)(2,1)S(1)}, u32[]{:S(2)}, u32[]{:S(2)}) %collective-permute-start) | collective-permute-done | bytes 524320 | tf_op jit(solution)/shard_map/while/body/eval_jaxpr/ppermute | solution.py:13
  61.8 1.3 collective-permute-start
  63.1 13.8 %collective-permute-done = bf16[128,2048]{0,1:T(8,128)(2,1)S(1)} collective-permute-done((bf16[128,2048]{0,1:T(8,128)(2,1)S(1)}, bf16[128,2048]{0,1:T(8,128)(2,1)S(1)}, u32[]{:S(2)}, u32[]{:S(2)}) %collective-permute-start) | collective-permute-done | bytes 524320 | tf_op jit(solution)/shard_map/while/body/eval_jaxpr/ppermute | solution.py:13
  76.8 1.3 collective-permute-start
  78.1 12.3 %collective-permute-done = bf16[128,2048]{0,1:T(8,128)(2,1)S(1)} collective-permute-done((bf16[128,2048]{0,1:T(8,128)(2,1)S(1)}, bf16[128,2048]{0,1:T(8,128)(2,1)S(1)}, u32[]{:S(2)}, u32[]{:S(2)}) %collective-permute-start) | collective-permute-done | bytes 524320 | tf_op jit(solution)/shard_map/while/body/eval_jaxpr/ppermute | solution.py:13
  90.4 1.3 collective-permute-start
  91.7 11.4 %collective-permute-done = bf16[128,2048]{0,1:T(8,128)(2,1)S(1)} collective-permute-done((bf16[128,2048]{0,1:T(8,128)(2,1)S(1)}, bf16[128,2048]{0,1:T(8,128)(2,1)S(1)}, u32[]{:S(2)}, u32[]{:S(2)}) %collective-permute-start) | collective-permute-done | bytes 524320 | tf_op jit(solution)/shard_map/while/body/eval_jaxpr/ppermute | solution.py:13
  103.1 1.3 collective-permute-start
  104.4 10.5 %collective-permute-done = bf16[128,2048]{0,1:T(8,128)(2,1)S(1)} collective-permute-done((bf16[128,2048]{0,1:T(8,128)(2,1)S(1)}, bf16[128,2048]{0,1:T(8,128)(2,1)S(1)}, u32[]{:S(2)}, u32[]{:S(2)}) %collective-permute-start) | collective-permute-done | bytes 524320 | tf_op jit(solution)/shard_map/while/body/eval_jaxpr/ppermute | solution.py:13
  114.9 1.3 collective-permute-start
  116.2 9.9 %collective-permute-done = bf16[128,2048]{0,1:T(8,128)(2,1)S(1)} collective-permute-done((bf16[128,2048]{0,1:T(8,128)(2,1)S(1)}, bf16[128,2048]{0,1:T(8,128)(2,1)S(1)}, u32[]{:S(2)}, u32[]{:S(2)}) %collective-permute-start) | collective-permute-done | bytes 524320 | tf_op jit(solution)/shard_map/while/body/eval_jaxpr/ppermute | solution.py:13
  126.1 1.3 collective-permute-start
  127.4 10.4 %collective-permute-done = bf16[128,2048]{0,1:T(8,128)(2,1)S(1)} collective-permute-done((bf16[128,2048]{0,1:T(8,128)(2,1)S(1)}, bf16[128,2048]{0,1:T(8,128)(2,1)S(1)}, u32[]{:S(2)}, u32[]{:S(2)}) %collective-permute-start) | collective-permute-done | bytes 524320 | tf_op jit(solution)/shard_map/while/body/eval_jaxpr/ppermute | solution.py:13
  137.8 1.3 collective-permute-start
  139.1 11.8 %collective-permute-done = bf16[128,2048]{0,1:T(8,128)(2,1)S(1)} collective-permute-done((bf16[128,2048]{0,1:T(8,128)(2,1)S(1)}, bf16[128,2048]{0,1:T(8,128)(2,1)S(1)}, u32[]{:S(2)}, u32[]{:S(2)}) %collective-permute-start) | collective-permute-done | bytes 524320 | tf_op jit(solution)/shard_map/while/body/eval_jaxpr/ppermute | solution.py:13
  150.9 1.3 collective-permute-start
  152.2 13.6 %collective-permute-done = bf16[128,2048]{0,1:T(8,128)(2,1)S(1)} collective-permute-done((bf16[128,2048]{0,1:T(8,128)(2,1)S(1)}, bf16[128,2048]{0,1:T(8,128)(2,1)S(1)}, u32[]{:S(2)}, u32[]{:S(2)}) %collective-permute-start) | collective-permute-done | bytes 524320 | tf_op jit(solution)/shard_map/while/body/eval_jaxpr/ppermute | solution.py:13
  165.8 1.3 collective-permute-start
  167.1 15.0 %collective-permute-done = bf16[128,2048]{0,1:T(8,128)(2,1)S(1)} collective-permute-done((bf16[128,2048]{0,1:T(8,128)(2,1)S(1)}, bf16[128,2048]{0,1:T(8,128)(2,1)S(1)}, u32[]{:S(2)}, u32[]{:S(2)}) %collective-permute-start) | collective-permute-done | bytes 524320 | tf_op jit(solution)/shard_map/while/body/eval_jaxpr/ppermute | solution.py:13
  182.1 1.3 collective-permute-start
  183.4 16.1 %collective-permute-done = bf16[128,2048]{0,1:T(8,128)(2,1)S(1)} collective-permute-done((bf16[128,2048]{0,1:T(8,128)(2,1)S(1)}, bf16[128,2048]{0,1:T(8,128)(2,1)S(1)}, u32[]{:S(2)}, u32[]{:S(2)}) %collective-permute-start) | collective-permute-done | bytes 524320 | tf_op jit(solution)/shard_map/while/body/eval_jaxpr/ppermute | solution.py:13
  199.5 1.3 collective-permute-start
  200.8 17.4 %collective-permute-done = bf16[128,2048]{0,1:T(8,128)(2,1)S(1)} collective-permute-done((bf16[128,2048]{0,1:T(8,128)(2,1)S(1)}, bf16[128,2048]{0,1:T(8,128)(2,1)S(1)}, u32[]{:S(2)}, u32[]{:S(2)}) %collective-permute-start) | collective-permute-done | bytes 524320 | tf_op jit(solution)/shard_map/while/body/eval_jaxpr/ppermute | solution.py:13
  218.2 1.3 collective-permute-start
  219.5 15.9 %collective-permute-done = bf16[128,2048]{0,1:T(8,128)(2,1)S(1)} collective-permute-done((bf16[128,2048]{0,1:T(8,128)(2,1)S(1)}, bf16[128,2048]{0,1:T(8,128)(2,1)S(1)}, u32[]{:S(2)}, u32[]{:S(2)}) %collective-permute-start) | collective-permute-done | bytes 524320 | tf_op jit(solution)/shard_map/while/body/eval_jaxpr/ppermute | solution.py:13
  235.4 1.3 collective-permute-start
  236.7 126.9 %collective-permute-done = bf16[128,2048]{0,1:T(8,128)(2,1)S(1)} collective-permute-done((bf16[128,2048]{0,1:T(8,128)(2,1)S(1)}, bf16[128,2048]{0,1:T(8,128)(2,1)S(1)}, u32[]{:S(2)}, u32[]{:S(2)}) %collective-permute-start) | collective-permute-done | bytes 524320 | tf_op jit(solution)/shard_map/while/body/eval_jaxpr/ppermute | solution.py:13
  363.6 11.2 %conditional.3 = ((bf16[128,2048]{0,1:T(8,128)(2,1)S(1)}, bf16[2,128,2048]{1,2,0:T(8,128)(2,1)}, f32[2,256,512]{1,2,0:T(8,128)}, f32[2,256,512]{1,2,0:T(8,128)})) conditional(s32[]{:T(128)} %convert_element_type.61, (bf16[128,2048]{0,1:T(8,128)(2,1)S(1)}, bf16[2,128,2048]{1,2,0:T(8,128)(2,1)}, f32[2,256,512]{1,2,0:T(8,128)}, ...), branch_computations={%region_1.1_spmd, %region_2.5_spmd} | conditional | flops 812841216 | bytes 30028450 | solution.py:146
  363.6 1.1 bitcast_select_fusion.2
  364.8 1.0 constant_dynamic-slice_fusion.4
  365.8 1.7 constant_dynamic-slice_fusion.1
  367.5 1.1 constant_dynamic-slice_fusion.2
  372.5 1.1 bitcast_dynamic-update-slice_fusion
  373.6 1.0 constant_dynamic-update-slice_fusion
  374.8 1.3 collective-permute-start
  376.1 11.1 %collective-permute-done = bf16[128,2048]{0,1:T(8,128)(2,1)S(1)} collective-permute-done((bf16[128,2048]{0,1:T(8,128)(2,1)S(1)}, bf16[128,2048]{0,1:T(8,128)(2,1)S(1)}, u32[]{:S(2)}, u32[]{:S(2)}) %collective-permute-start) | collective-permute-done | bytes 524320 | tf_op jit(solution)/shard_map/while/body/eval_jaxpr/ppermute | solution.py:13
  387.2 11.3 %conditional.3 = ((bf16[128,2048]{0,1:T(8,128)(2,1)S(1)}, bf16[2,128,2048]{1,2,0:T(8,128)(2,1)}, f32[2,256,512]{1,2,0:T(8,128)}, f32[2,256,512]{1,2,0:T(8,128)})) conditional(s32[]{:T(128)} %convert_element_type.61, (bf16[128,2048]{0,1:T(8,128)(2,1)S(1)}, bf16[2,128,2048]{1,2,0:T(8,128)(2,1)}, f32[2,256,512]{1,2,0:T(8,128)}, ...), branch_computations={%region_1.1_spmd, %region_2.5_spmd} | conditional | flops 812841216 | bytes 30028450 | solution.py:146
  387.2 1.1 bitcast_select_fusion.2
  389.4 1.7 constant_dynamic-slice_fusion.1
  391.1 1.1 constant_dynamic-slice_fusion.2
  396.1 1.2 bitcast_dynamic-update-slice_fusion
  397.3 1.0 constant_dynamic-update-slice_fusion
  398.5 1.6 copy.35
  400.9 15.1 %collective-permute-start.3 = (f32[2,128,512]{2,1,0:T(8,128)}, f32[2,128,512]{2,1,0:T(8,128)S(1)}, u32[]{:S(2)}, u32[]{:S(2)}) collective-permute-start(f32[2,128,512]{2,1,0:T(8,128)} %slice.17), channel_id=1, source_target_pairs={{1,0},{2,1},{3,2},{4,3},{5,4},{6,5},{7,6},{8,7},{9,8},{10,9},{11,1... | collective-permute-start | bytes 1572872 | tf_op jit(solution)/shard_map/ppermute | solution.py:13
  416.1 1.6 copy.37
  418.4 1.9 collective-permute-start.4
  420.4 2.3 copy.34
  422.6 1.9 collective-permute-done.3
  425.3 5.0 %collective-permute-done.4 = f32[2,128,512]{2,1,0:T(8,128)S(1)} collective-permute-done((f32[2,128,512]{2,1,0:T(8,128)}, f32[2,128,512]{2,1,0:T(8,128)S(1)}, u32[]{:S(2)}, u32[]{:S(2)}) %collective-permute-start.4) | collective-permute-done | bytes 524320 | tf_op jit(solution)/shard_map/ppermute | solution.py:13
  (63 shorter events, 15.2 us)
Async XLA Ops:
  0.6 12.8 %copy-start.1 = (bf16[2,128,2048]{2,1,0:T(8,128)(2,1)S(1)}, bf16[2,128,2048]{2,1,0:T(8,128)(2,1)}, u32[]{:S(2)}) copy-start(bf16[2,128,2048]{2,1,0:T(8,128)(2,1)} %param.12) | copy-start | bytes 3145732
  1.9 12.9 %collective-permute-start.2 = (bf16[2,128,512]{1,2,0:T(8,128)(2,1)S(1)}, bf16[2,128,512]{1,2,0:T(8,128)(2,1)S(1)}, u32[]{:S(2)}, u32[]{:S(2)}) collective-permute-start(bf16[2,128,512]{1,2,0:T(8,128)(2,1)S(1)} %bitcast.98), channel_id=1, source_target_pairs={{0,1},{1,2},{2,3},{3,4},{4,5},{5,6},{6,7},{7,8},{8,9},{9,10},{10,1... | collective-permute-start | bytes 786440 | tf_op jit(solution)/shard_map/ppermute | solution.py:13
  8.3 7.3 %collective-permute-start.1 = (bf16[2,128,512]{1,2,0:T(8,128)(2,1)S(1)}, bf16[2,128,512]{1,2,0:T(8,128)(2,1)S(1)}, u32[]{:S(2)}, u32[]{:S(2)}) collective-permute-start(bf16[2,128,512]{1,2,0:T(8,128)(2,1)S(1)} %bitcast.96), channel_id=1, source_target_pairs={{0,1},{1,2},{2,3},{3,4},{4,5},{5,6},{6,7},{7,8},{8,9},{9,10},{10,1... | collective-permute-start | bytes 786440 | tf_op jit(solution)/shard_map/ppermute | solution.py:13
  11.1 3.6 copy-start.3
  19.7 14.9 %collective-permute-start = (bf16[128,2048]{0,1:T(8,128)(2,1)S(1)}, bf16[128,2048]{0,1:T(8,128)(2,1)S(1)}, u32[]{:S(2)}, u32[]{:S(2)}) collective-permute-start(bf16[128,2048]{0,1:T(8,128)(2,1)S(1)} %get-tuple-element.661), channel_id=1, source_target_pairs={{32,0},{64,32},{96,64},{128,96},{160,128},{192,160},{224,192},{256... | collective-permute-start | bytes 1572872 | tf_op jit(solution)/shard_map/while/body/eval_jaxpr/ppermute | solution.py:13
  34.6 14.0 %collective-permute-start = (bf16[128,2048]{0,1:T(8,128)(2,1)S(1)}, bf16[128,2048]{0,1:T(8,128)(2,1)S(1)}, u32[]{:S(2)}, u32[]{:S(2)}) collective-permute-start(bf16[128,2048]{0,1:T(8,128)(2,1)S(1)} %get-tuple-element.661), channel_id=1, source_target_pairs={{32,0},{64,32},{96,64},{128,96},{160,128},{192,160},{224,192},{256... | collective-permute-start | bytes 1572872 | tf_op jit(solution)/shard_map/while/body/eval_jaxpr/ppermute | solution.py:13
  48.6 13.2 %collective-permute-start = (bf16[128,2048]{0,1:T(8,128)(2,1)S(1)}, bf16[128,2048]{0,1:T(8,128)(2,1)S(1)}, u32[]{:S(2)}, u32[]{:S(2)}) collective-permute-start(bf16[128,2048]{0,1:T(8,128)(2,1)S(1)} %get-tuple-element.661), channel_id=1, source_target_pairs={{32,0},{64,32},{96,64},{128,96},{160,128},{192,160},{224,192},{256... | collective-permute-start | bytes 1572872 | tf_op jit(solution)/shard_map/while/body/eval_jaxpr/ppermute | solution.py:13
  61.8 15.1 %collective-permute-start = (bf16[128,2048]{0,1:T(8,128)(2,1)S(1)}, bf16[128,2048]{0,1:T(8,128)(2,1)S(1)}, u32[]{:S(2)}, u32[]{:S(2)}) collective-permute-start(bf16[128,2048]{0,1:T(8,128)(2,1)S(1)} %get-tuple-element.661), channel_id=1, source_target_pairs={{32,0},{64,32},{96,64},{128,96},{160,128},{192,160},{224,192},{256... | collective-permute-start | bytes 1572872 | tf_op jit(solution)/shard_map/while/body/eval_jaxpr/ppermute | solution.py:13
  76.8 13.6 %collective-permute-start = (bf16[128,2048]{0,1:T(8,128)(2,1)S(1)}, bf16[128,2048]{0,1:T(8,128)(2,1)S(1)}, u32[]{:S(2)}, u32[]{:S(2)}) collective-permute-start(bf16[128,2048]{0,1:T(8,128)(2,1)S(1)} %get-tuple-element.661), channel_id=1, source_target_pairs={{32,0},{64,32},{96,64},{128,96},{160,128},{192,160},{224,192},{256... | collective-permute-start | bytes 1572872 | tf_op jit(solution)/shard_map/while/body/eval_jaxpr/ppermute | solution.py:13
  90.4 12.7 %collective-permute-start = (bf16[128,2048]{0,1:T(8,128)(2,1)S(1)}, bf16[128,2048]{0,1:T(8,128)(2,1)S(1)}, u32[]{:S(2)}, u32[]{:S(2)}) collective-permute-start(bf16[128,2048]{0,1:T(8,128)(2,1)S(1)} %get-tuple-element.661), channel_id=1, source_target_pairs={{32,0},{64,32},{96,64},{128,96},{160,128},{192,160},{224,192},{256... | collective-permute-start | bytes 1572872 | tf_op jit(solution)/shard_map/while/body/eval_jaxpr/ppermute | solution.py:13
  103.1 11.8 %collective-permute-start = (bf16[128,2048]{0,1:T(8,128)(2,1)S(1)}, bf16[128,2048]{0,1:T(8,128)(2,1)S(1)}, u32[]{:S(2)}, u32[]{:S(2)}) collective-permute-start(bf16[128,2048]{0,1:T(8,128)(2,1)S(1)} %get-tuple-element.661), channel_id=1, source_target_pairs={{32,0},{64,32},{96,64},{128,96},{160,128},{192,160},{224,192},{256... | collective-permute-start | bytes 1572872 | tf_op jit(solution)/shard_map/while/body/eval_jaxpr/ppermute | solution.py:13
  114.9 11.2 %collective-permute-start = (bf16[128,2048]{0,1:T(8,128)(2,1)S(1)}, bf16[128,2048]{0,1:T(8,128)(2,1)S(1)}, u32[]{:S(2)}, u32[]{:S(2)}) collective-permute-start(bf16[128,2048]{0,1:T(8,128)(2,1)S(1)} %get-tuple-element.661), channel_id=1, source_target_pairs={{32,0},{64,32},{96,64},{128,96},{160,128},{192,160},{224,192},{256... | collective-permute-start | bytes 1572872 | tf_op jit(solution)/shard_map/while/body/eval_jaxpr/ppermute | solution.py:13
  126.1 11.7 %collective-permute-start = (bf16[128,2048]{0,1:T(8,128)(2,1)S(1)}, bf16[128,2048]{0,1:T(8,128)(2,1)S(1)}, u32[]{:S(2)}, u32[]{:S(2)}) collective-permute-start(bf16[128,2048]{0,1:T(8,128)(2,1)S(1)} %get-tuple-element.661), channel_id=1, source_target_pairs={{32,0},{64,32},{96,64},{128,96},{160,128},{192,160},{224,192},{256... | collective-permute-start | bytes 1572872 | tf_op jit(solution)/shard_map/while/body/eval_jaxpr/ppermute | solution.py:13
  137.8 13.1 %collective-permute-start = (bf16[128,2048]{0,1:T(8,128)(2,1)S(1)}, bf16[128,2048]{0,1:T(8,128)(2,1)S(1)}, u32[]{:S(2)}, u32[]{:S(2)}) collective-permute-start(bf16[128,2048]{0,1:T(8,128)(2,1)S(1)} %get-tuple-element.661), channel_id=1, source_target_pairs={{32,0},{64,32},{96,64},{128,96},{160,128},{192,160},{224,192},{256... | collective-permute-start | bytes 1572872 | tf_op jit(solution)/shard_map/while/body/eval_jaxpr/ppermute | solution.py:13
  150.9 14.9 %collective-permute-start = (bf16[128,2048]{0,1:T(8,128)(2,1)S(1)}, bf16[128,2048]{0,1:T(8,128)(2,1)S(1)}, u32[]{:S(2)}, u32[]{:S(2)}) collective-permute-start(bf16[128,2048]{0,1:T(8,128)(2,1)S(1)} %get-tuple-element.661), channel_id=1, source_target_pairs={{32,0},{64,32},{96,64},{128,96},{160,128},{192,160},{224,192},{256... | collective-permute-start | bytes 1572872 | tf_op jit(solution)/shard_map/while/body/eval_jaxpr/ppermute | solution.py:13
  165.8 16.3 %collective-permute-start = (bf16[128,2048]{0,1:T(8,128)(2,1)S(1)}, bf16[128,2048]{0,1:T(8,128)(2,1)S(1)}, u32[]{:S(2)}, u32[]{:S(2)}) collective-permute-start(bf16[128,2048]{0,1:T(8,128)(2,1)S(1)} %get-tuple-element.661), channel_id=1, source_target_pairs={{32,0},{64,32},{96,64},{128,96},{160,128},{192,160},{224,192},{256... | collective-permute-start | bytes 1572872 | tf_op jit(solution)/shard_map/while/body/eval_jaxpr/ppermute | solution.py:13
  182.1 17.4 %collective-permute-start = (bf16[128,2048]{0,1:T(8,128)(2,1)S(1)}, bf16[128,2048]{0,1:T(8,128)(2,1)S(1)}, u32[]{:S(2)}, u32[]{:S(2)}) collective-permute-start(bf16[128,2048]{0,1:T(8,128)(2,1)S(1)} %get-tuple-element.661), channel_id=1, source_target_pairs={{32,0},{64,32},{96,64},{128,96},{160,128},{192,160},{224,192},{256... | collective-permute-start | bytes 1572872 | tf_op jit(solution)/shard_map/while/body/eval_jaxpr/ppermute | solution.py:13
  199.5 18.7 %collective-permute-start = (bf16[128,2048]{0,1:T(8,128)(2,1)S(1)}, bf16[128,2048]{0,1:T(8,128)(2,1)S(1)}, u32[]{:S(2)}, u32[]{:S(2)}) collective-permute-start(bf16[128,2048]{0,1:T(8,128)(2,1)S(1)} %get-tuple-element.661), channel_id=1, source_target_pairs={{32,0},{64,32},{96,64},{128,96},{160,128},{192,160},{224,192},{256... | collective-permute-start | bytes 1572872 | tf_op jit(solution)/shard_map/while/body/eval_jaxpr/ppermute | solution.py:13
  218.2 17.2 %collective-permute-start = (bf16[128,2048]{0,1:T(8,128)(2,1)S(1)}, bf16[128,2048]{0,1:T(8,128)(2,1)S(1)}, u32[]{:S(2)}, u32[]{:S(2)}) collective-permute-start(bf16[128,2048]{0,1:T(8,128)(2,1)S(1)} %get-tuple-element.661), channel_id=1, source_target_pairs={{32,0},{64,32},{96,64},{128,96},{160,128},{192,160},{224,192},{256... | collective-permute-start | bytes 1572872 | tf_op jit(solution)/shard_map/while/body/eval_jaxpr/ppermute | solution.py:13
  235.4 128.1 %collective-permute-start = (bf16[128,2048]{0,1:T(8,128)(2,1)S(1)}, bf16[128,2048]{0,1:T(8,128)(2,1)S(1)}, u32[]{:S(2)}, u32[]{:S(2)}) collective-permute-start(bf16[128,2048]{0,1:T(8,128)(2,1)S(1)} %get-tuple-element.661), channel_id=1, source_target_pairs={{32,0},{64,32},{96,64},{128,96},{160,128},{192,160},{224,192},{256... | collective-permute-start | bytes 1572872 | tf_op jit(solution)/shard_map/while/body/eval_jaxpr/ppermute | solution.py:13
  369.4 1.0 copy-start
  373.6 1.2 copy-start.2
  374.8 12.4 %collective-permute-start = (bf16[128,2048]{0,1:T(8,128)(2,1)S(1)}, bf16[128,2048]{0,1:T(8,128)(2,1)S(1)}, u32[]{:S(2)}, u32[]{:S(2)}) collective-permute-start(bf16[128,2048]{0,1:T(8,128)(2,1)S(1)} %get-tuple-element.661), channel_id=1, source_target_pairs={{32,0},{64,32},{96,64},{128,96},{160,128},{192,160},{224,192},{256... | collective-permute-start | bytes 1572872 | tf_op jit(solution)/shard_map/while/body/eval_jaxpr/ppermute | solution.py:13
  393.0 1.0 copy-start
  397.3 1.2 copy-start.2
  400.9 23.6 %collective-permute-start.3 = (f32[2,128,512]{2,1,0:T(8,128)}, f32[2,128,512]{2,1,0:T(8,128)S(1)}, u32[]{:S(2)}, u32[]{:S(2)}) collective-permute-start(f32[2,128,512]{2,1,0:T(8,128)} %slice.17), channel_id=1, source_target_pairs={{1,0},{2,1},{3,2},{4,3},{5,4},{6,5},{7,6},{8,7},{9,8},{10,9},{11,1... | collective-permute-start | bytes 1572872 | tf_op jit(solution)/shard_map/ppermute | solution.py:13
  418.4 11.9 %collective-permute-start.4 = (f32[2,128,512]{2,1,0:T(8,128)}, f32[2,128,512]{2,1,0:T(8,128)S(1)}, u32[]{:S(2)}, u32[]{:S(2)}) collective-permute-start(f32[2,128,512]{2,1,0:T(8,128)} %slice.19), channel_id=1, source_target_pairs={{1,0},{2,1},{3,2},{4,3},{5,4},{6,5},{7,6},{8,7},{9,8},{10,9},{11,1... | collective-permute-start | bytes 1572872 | tf_op jit(solution)/shard_map/ppermute | solution.py:13
where the time goes:
time: 432 us; the launch traced here: 431 us
  waiting for transfers between devices  341 us (79%)
  starting transfers between devices  46.1 us (11%)
  local copies, waits for them, and re-layouts  28.2 us (7%)
  other arithmetic  8.63 us (2%)
  matrix products  5.88 us (1%)
    ppermute x21, waiting for transfers between devices, from_behind(): return lax.ppermute(block, axis, route)  341 us
    ppermute x21, starting transfers between devices, from_behind(): return lax.ppermute(block, axis, route)  46.1 us
  transfers between devices with their start and end apart: 21, of which 19 were waited for; matrix products, arithmetic and copies ran while one was open for 3% of the time, Pallas kernels for 0%

commit v1 on v0

v1 whole, which is shorter than its diff:
```python
import jax
import jax.numpy as jnp
from jax import lax
from jax.sharding import PartitionSpec as P

DH = 128
WINDOW = 128


def from_behind(block, axis, distance):
    devices = range(lax.axis_size(axis))
    route = [(i - distance, i) for i in devices if i - distance in devices]
    return lax.ppermute(block, axis, route)


def softmax_rows(scores, allowed):
    masked = jnp.where(allowed, scores, -jnp.inf)
    row_max = jnp.max(masked, axis=-1, keepdims=True)
    weights = jnp.exp(masked - row_max)
    return weights / jnp.sum(weights, axis=-1, keepdims=True)


def tile_backward(query, key_rows, value_rows, grad_out, allowed):
    row_count = query.shape[0]
    key_count = key_rows.shape[0]
    kv_heads = key_rows.shape[1] // DH
    group_size = query.shape[1] // (kv_heads * DH)
    score_scale = DH ** (-0.5)
    query_heads = query.reshape(row_count, kv_heads, group_size, DH)
    grad_heads = grad_out.reshape(row_count, kv_heads, group_size, DH)
    key_heads = key_rows.reshape(key_count, kv_heads, DH)
    value_heads = value_rows.reshape(key_count, kv_heads, DH)
    scores = (
        jnp.einsum("qhgd,khd->hgqk", query_heads, key_heads, preferred_element_type=jnp.float32)
        * score_scale
    )
    probability = softmax_rows(scores, allowed)
    prob_low = probability.astype(jnp.bfloat16)
    output = jnp.einsum("hgqk,khd->qhgd", prob_low, value_heads, preferred_element_type=jnp.float32)
    grad_prob = jnp.einsum(
        "qhgd,khd->hgqk", grad_heads, value_heads, preferred_element_type=jnp.float32
    )
    grad_dot = jnp.transpose(jnp.sum(grad_heads.astype(jnp.float32) * output, axis=-1), (1, 2, 0))[
        ..., None
    ]
    grad_score = (probability * (grad_prob - grad_dot)).astype(jnp.bfloat16)
    key_grad = (
        jnp.einsum("hgqk,qhgd->khd", grad_score, query_heads, preferred_element_type=jnp.float32)
        * score_scale
    )
    value_grad = jnp.einsum(
        "hgqk,qhgd->khd", prob_low, grad_heads, preferred_element_type=jnp.float32
    )
    return key_grad.reshape(key_count, -1), value_grad.reshape(key_count, -1)


def chain_backward(query_t, key_t, value_t, grad_top, allowed):
    layer_count, row_count, width = query_t.shape
    heads = width // DH
    score_scale = DH ** (-0.5)
    query_heads = query_t.reshape(layer_count, row_count, heads, DH)
    scores = (
        jnp.einsum("lqhd,lkd->lhqk", query_heads, key_t, preferred_element_type=jnp.float32)
        * score_scale
    )
    probability = softmax_rows(scores, allowed[None, None])
    prob_low = probability.astype(jnp.bfloat16)
    output = jnp.einsum("lhqk,lkd->lhqd", prob_low, value_t, preferred_element_type=jnp.float32)
    grad_start = jnp.transpose(grad_top.reshape(row_count, heads, DH), (1, 0, 2))

    def step(index, carry):
        grad, grads = carry
        layer = layer_count - 1 - index
        value_rows = lax.dynamic_index_in_dim(value_t, layer, 0, keepdims=False)
        key_rows = lax.dynamic_index_in_dim(key_t, layer, 0, keepdims=False)
        prob = lax.dynamic_index_in_dim(probability, layer, 0, keepdims=False)
        out = lax.dynamic_index_in_dim(output, layer, 0, keepdims=False)
        grad_prob = jnp.einsum("hqd,kd->hqk", grad, value_rows, preferred_element_type=jnp.float32)
        grad_dot = jnp.sum(grad.astype(jnp.float32) * out, axis=-1, keepdims=True)
        grad_score = (prob * (grad_prob - grad_dot)).astype(jnp.bfloat16)
        query_grad = (
            jnp.einsum("hqk,kd->hqd", grad_score, key_rows, preferred_element_type=jnp.float32)
            * score_scale
        )
        grad_next = (grad.astype(jnp.float32) + query_grad).astype(jnp.bfloat16)
        grads = lax.dynamic_update_index_in_dim(grads, grad_next, layer, 0)
        return grad_next, grads

    grads = jnp.zeros((layer_count, heads, row_count, DH), jnp.bfloat16)
    _, grads = lax.fori_loop(0, layer_count, step, (grad_start, grads))
    return jnp.transpose(grads, (0, 2, 1, 3)).reshape(layer_count, row_count, width)


def per_device(queries, keys, values, out_grad, segments):
    micro_count = queries.shape[1]
    row_count = queries.shape[2]
    query_width = queries.shape[3]
    key_width = keys.shape[3]
    section_count = lax.axis_size("pipe")
    section_index = lax.axis_index("pipe")
    seq_index = lax.axis_index("seq")
    kv_heads = key_width // DH
    q_heads = query_width // DH
    group_size = q_heads // kv_heads
    head_blocks = section_count // micro_count
    block_heads = q_heads // head_blocks
    block_width = block_heads * DH
    blocks_per_kv = group_size // block_heads
    own_query = queries[0]
    own_key = keys[0]
    own_value = values[0]
    seg_padded = jnp.concatenate(
        [jnp.full((micro_count, row_count), -1, jnp.int32), segments], axis=1
    )
    query_pos = seq_index * row_count + jnp.arange(row_count, dtype=jnp.int32)
    key_pos = seq_index * row_count - row_count + jnp.arange(2 * row_count, dtype=jnp.int32)
    seg_query = lax.dynamic_slice_in_dim(
        seg_padded, seq_index * row_count + row_count, row_count, axis=1
    )
    seg_key = lax.dynamic_slice_in_dim(seg_padded, seq_index * row_count, 2 * row_count, axis=1)
    near = (
        (key_pos[None, :] <= query_pos[:, None])
        & (query_pos[:, None] - key_pos[None, :] < WINDOW)
        & (key_pos[None, :] >= 0)
    )
    masks = near[None] & (seg_query[:, :, None] == seg_key[:, None, :])
    halo_key, halo_value = from_behind((own_key, own_value), "seq", 1)
    key_rows = jnp.concatenate([halo_key, own_key], axis=1)
    value_rows = jnp.concatenate([halo_value, own_value], axis=1)

    my_block = section_index // micro_count
    my_micro = section_index % micro_count
    my_kv = my_block // blocks_per_kv
    query_send = jnp.transpose(
        own_query.reshape(micro_count, row_count, head_blocks, block_width), (2, 0, 1, 3)
    ).reshape(section_count, row_count, block_width)
    kv_send = []
    for rows in (key_rows, value_rows):
        split = jnp.transpose(rows.reshape(micro_count, 2 * row_count, kv_heads, DH), (2, 0, 1, 3))
        split = jnp.broadcast_to(
            split[:, None], (kv_heads, blocks_per_kv, micro_count, 2 * row_count, DH)
        )
        kv_send.append(split.reshape(section_count, 2 * row_count, DH))
    query_t = lax.all_to_all(query_send, "pipe", 0, 0)
    key_t = lax.all_to_all(kv_send[0], "pipe", 0, 0)
    value_t = lax.all_to_all(kv_send[1], "pipe", 0, 0)
    grad_top = lax.dynamic_slice(
        out_grad, (my_micro, 0, my_block * block_width), (1, row_count, block_width)
    )[0]
    allowed = lax.dynamic_index_in_dim(masks, my_micro, 0, keepdims=False)
    grads = chain_backward(query_t, key_t, value_t, grad_top, allowed)
    grads_above = jnp.concatenate([grads[1:], grad_top[None]], axis=0)
    back_send = jnp.stack([grads_above, grads], axis=1)
    back = lax.all_to_all(back_send, "pipe", 0, 0)
    back = jnp.transpose(
        back.reshape(head_blocks, micro_count, 2, row_count, block_width), (2, 1, 3, 0, 4)
    ).reshape(2, micro_count, row_count, query_width)
    grad_in = back[0]
    query_all = back[1]

    key_parts = []
    value_parts = []
    for micro in range(micro_count):
        key_grad, value_grad = tile_backward(
            own_query[micro], key_rows[micro], value_rows[micro], grad_in[micro], masks[micro]
        )
        key_parts.append(key_grad)
        value_parts.append(value_grad)
    key_all = jnp.stack(key_parts)
    value_all = jnp.stack(value_parts)
    back_key, back_value = from_behind(
        (key_all[:, :row_count], value_all[:, :row_count]), "seq", -1
    )
    key_grads = (key_all[:, row_count:] + back_key).astype(jnp.bfloat16)
    value_grads = (value_all[:, row_count:] + back_value).astype(jnp.bfloat16)
    return (query_all[None], key_grads[None], value_grads[None])


def solution(mesh):
    placed = (
        P("pipe", None, "seq", None),
        P("pipe", None, "seq", None),
        P("pipe", None, "seq", None),
        P(None, "seq", None),
        P(),
    )
    return jax.shard_map(
        per_device,
        mesh=mesh,
        in_specs=placed,
        out_specs=(
            P("pipe", None, "seq", None),
            P("pipe", None, "seq", None),
            P("pipe", None, "seq", None),
        ),
        check_vma=False,
    )
```

time: 432 us -> 207 us (0.48)
  waiting for transfers between devices: 341 us -> 35.5 us
  matrix products: 5.88 us -> 44.4 us
  other arithmetic: 8.63 us -> 37.2 us
  local copies, waits for them, and re-layouts: 28.2 us -> 46.8 us
  starting transfers between devices: 46.1 us -> 38.5 us
    ppermute x21 -> x4, waiting for transfers between devices: 341 us -> 2.5 us  [from_behind(): return lax.ppermute(block, axis, route)]
    all_to_all x0 -> x4, waiting for transfers between devices: none -> 33 us  [the longest x1 14.4 us: per_device(): back = lax.all_to_all(back_send, 'pipe', 0, 0)]
    ppermute x21 -> x4, starting transfers between devices: 46.1 us -> 17.1 us  [from_behind(): return lax.ppermute(block, axis, route)]
    dot_general x4 -> x18, matrix products: 1.65 us -> 28.8 us  [the longest x16 22.3 us: step(): jnp.einsum('hqk,kd->hqd', grad_score, key_rows, preferred_element_type=jn...]
    all_to_all x0 -> x4, starting transfers between devices: none -> 21.4 us  [the longest x1 6.89 us: per_device(): query_t = lax.all_to_all(query_send, 'pipe', 0, 0)]
    reduce_sum x0 -> x16, other arithmetic: none -> 16.3 us  [step(): grad_dot = jnp.sum(grad.astype(jnp.float32) * out, axis=-1, keepdims=True)]
    slice x2 -> x7, local copies, waits for them, and re-layouts: 1.65 us -> 10.2 us  [the longest x3 5.88 us: per_device(): grad_in[micro]]
    dynamic_slice x10 -> x1, local copies, waits for them, and re-layouts: 7.49 us -> 0.01 us  [per_device(): lax.dynamic_slice(out_grad, (my_micro, 0, my_block * block_width), (1, ro...]
  transfers between devices with their start and end apart: 21 -> 8, of which waited for: 19 -> 5; matrix products, arithmetic and copies ran while one was open for 3% -> 25% of each run, Pallas kernels for 0% -> 0%
where the time goes in v1:
time: 207 us; the launch traced here: 204 us
  local copies, waits for them, and re-layouts  46.8 us (23%)
  matrix products  44.4 us (21%)
  starting transfers between devices  38.5 us (19%)
  other arithmetic  37.2 us (18%)
  waiting for transfers between devices  35.5 us (17%)
    dot_general x16, matrix products, step(): jnp.einsum('hqk,kd->hqd', grad_score, key_rows, preferred_element_type=jn...  22.3 us
    ppermute x4, starting transfers between devices, from_behind(): return lax.ppermute(block, axis, route)  17.1 us
    reduce_sum x16, other arithmetic, step(): grad_dot = jnp.sum(grad.astype(jnp.float32) * out, axis=-1, keepdims=True)  16.3 us
    all_to_all x1, waiting for transfers between devices, per_device(): back = lax.all_to_all(back_send, 'pipe', 0, 0)  14.4 us
    all_to_all x1, waiting for transfers between devices, per_device(): value_t = lax.all_to_all(kv_send[1], 'pipe', 0, 0)  9.8 us
    unnamed x53, local copies, waits for them, and re-layouts  8.44 us
    all_to_all x1, waiting for transfers between devices, per_device(): key_t = lax.all_to_all(kv_send[0], 'pipe', 0, 0)  7.22 us
    all_to_all x1, starting transfers between devices, per_device(): query_t = lax.all_to_all(query_send, 'pipe', 0, 0)  6.89 us
  transfers between devices with their start and end apart: 8, of which 5 were waited for; matrix products, arithmetic and copies ran while one was open for 25% of the time, Pallas kernels for 0%

profile of v1, /device:TPU:97, one launch (start us, length us, event | category | flops | bytes accessed | tf_op | source)
XLA Modules:
  0.0 204.3 jit_solution(1424687874584479922)
XLA Ops:
  0.6 1.7 copy.134
  2.4 1.3 copy.135
  3.7 6.9 %all-to-all-start.1 = ((bf16[16,128,256]{2,1,0:T(8,128)(2,1)}), bf16[16,128,256]{2,1,0:T(8,128)(2,1)S(1)}, u32[]{:S(2)}, u32[]{:S(2)}) async-start(bf16[16,128,256]{2,1,0:T(8,128)(2,1)} %bitcast.248), calls=%async_computation.1 | async-start | bytes 2097152 | tf_op jit(solution)/shard_map/all_to_all | solution.py:144
  11.7 5.6 %collective-permute-start = (bf16[2,128,512]{1,2,0:T(8,128)(2,1)S(1)}, bf16[2,128,512]{1,2,0:T(8,128)(2,1)}, u32[]{:S(2)}, u32[]{:S(2)}) collective-permute-start(bf16[2,128,512]{1,2,0:T(8,128)(2,1)S(1)} %bitcast.254), channel_id=1, source_target_pairs={{0,1},{1,2},{2,3},{3,4},{4,5},{5,6},{6,7},{7,8},{8,9},{9,10},{10,1... | collective-permute-start | bytes 786440 | tf_op jit(solution)/shard_map/ppermute | solution.py:13
  17.3 1.8 copy.138
  19.1 1.9 collective-permute-start.1
  21.1 1.8 maximum_bitcast_fusion.1
  22.9 2.1 %copy.133 = bf16[4,2,256,128]{3,2,1,0:T(8,128)(2,1)} copy(bf16[4,2,256,128]{2,3,0,1:T(8,128)(2,1)} %maximum_bitcast_fusion.1) | data formatting | bytes 1048576 | tf_op jit(solution)/shard_map/transpose | solution.py:139
  25.0 1.6 all-to-all-done.1
  26.6 2.6 %broadcast_in_dim.82 = bf16[4,2,2,256,128]{4,3,2,1,0:T(8,128)(2,1)} broadcast(bf16[4,2,256,128]{3,2,1,0:T(8,128)(2,1)} %copy.133), dimensions={0,2,3,4} | broadcast | bytes 1572864 | tf_op jit(solution)/shard_map/broadcast_in_dim | solution.py:140
  29.2 5.4 %all-to-all-start = ((bf16[16,256,128]{2,1,0:T(8,128)(2,1)}), bf16[16,256,128]{2,1,0:T(8,128)(2,1)S(1)}, u32[]{:S(2)}, u32[]{:S(2)}) async-start(bf16[16,256,128]{2,1,0:T(8,128)(2,1)} %bitcast.249), calls=%async_computation | async-start | bytes 2097152 | tf_op jit(solution)/shard_map/all_to_all | solution.py:145
  35.7 1.5 slice_bitcast_fusion.1
  37.2 1.9 maximum_bitcast_fusion.2
  39.1 2.0 %copy.140 = bf16[4,2,256,128]{3,2,1,0:T(8,128)(2,1)} copy(bf16[4,2,256,128]{2,3,0,1:T(8,128)(2,1)} %maximum_bitcast_fusion.2) | data formatting | bytes 1048576 | tf_op jit(solution)/shard_map/transpose | solution.py:139
  41.2 2.3 %copy.136 = bf16[16,128,256]{1,2,0:T(8,128)(2,1)} copy(bf16[16,128,256]{2,1,0:T(8,128)(2,1)} %copy-done.12) | data formatting | bytes 2097152 | tf_op jit(solution)/shard_map/all_to_all | solution.py:144
  43.5 7.2 %all-to-all-done = bf16[16,256,128]{2,1,0:T(8,128)(2,1)S(1)} async-done(((bf16[16,256,128]{2,1,0:T(8,128)(2,1)}), bf16[16,256,128]{2,1,0:T(8,128)(2,1)S(1)}, u32[]{:S(2)}, u32[]{:S(2)}) %all-to-all-start) | async-done | bytes 1048608 | tf_op jit(solution)/shard_map/all_to_all | solution.py:145
  50.7 2.6 %broadcast_in_dim.84 = bf16[4,2,2,256,128]{4,3,2,1,0:T(8,128)(2,1)} broadcast(bf16[4,2,256,128]{3,2,1,0:T(8,128)(2,1)} %copy.140), dimensions={0,2,3,4} | broadcast | bytes 1572864 | tf_op jit(solution)/shard_map/broadcast_in_dim | solution.py:140
  53.3 4.6 %all-to-all-start.2 = ((bf16[16,256,128]{2,1,0:T(8,128)(2,1)}), bf16[16,256,128]{2,1,0:T(8,128)(2,1)S(1)}, u32[]{:S(2)}, u32[]{:S(2)}) async-start(bf16[16,256,128]{2,1,0:T(8,128)(2,1)} %bitcast.250), calls=%async_computation.2 | async-start | bytes 2097152 | tf_op jit(solution)/shard_map/all_to_all | solution.py:146
  57.9 2.2 %fusion.45 = f32[16,256,128,2]{2,1,3,0:T(8,128)S(1)} fusion(bf16[16,128,2,128]{1,3,2,0:T(8,128)(2,1)} %bitcast.252, bf16[16,256,128]{2,1,0:T(8,128)(2,1)} %copy-done.3), kind=kOutput, calls=%fused_computation.62 | convolution fusion | flops 268435456 | bytes 6291456 | tf_op jit(solution)/shard_map/lqhd,lkd->lhqk/dot_general | solution.py:63
  61.2 2.3 %broadcast_divide_fusion = f32[16,2,128,256]{2,3,1,0:T(8,128)} fusion(f32[16,2,128,256]{2,3,1,0:T(8,128)S(1)} %get-tuple-element.250, f32[16,2,128]{2,1,0:T(2,128)S(1)} %get-tuple-element.249), kind=kLoop, calls=%fused_computation.38 | loop fusion | flops 1048576 | bytes 8404992 | tf_op jit(solution)/shard_map/div | solution.py:20
  63.5 9.8 %all-to-all-done.2 = bf16[16,256,128]{2,1,0:T(8,128)(2,1)S(1)} async-done(((bf16[16,256,128]{2,1,0:T(8,128)(2,1)}), bf16[16,256,128]{2,1,0:T(8,128)(2,1)S(1)}, u32[]{:S(2)}, u32[]{:S(2)}) %all-to-all-start.2) | async-done | bytes 1048608 | tf_op jit(solution)/shard_map/all_to_all | solution.py:146
  74.3 4.3 %fusion.27 = f32[16,2,128,128]{3,2,1,0:T(8,128)} fusion(f32[16,2,128,256]{2,3,1,0:T(8,128)} %broadcast_divide_fusion, bf16[16,256,128]{2,1,0:T(8,128)(2,1)S(1)} %all-to-all-done.2), kind=kOutput, calls=%fused_computation.36 | convolution fusion | flops 269484032 | bytes 7340032 | tf_op jit(solution)/shard_map/lhqk,lkd->lhqd/dot_general | solution.py:68
  78.8 41.8 %while.17 = (s32[]{:T(128)}, bf16[2,128,128]{2,1,0:T(8,128)(2,1)S(1)}, bf16[16,2,128,128]{2,3,1,0:T(8,128)(2,1)S(1)}, f32[16,2,128,256]{2,3,1,0:T(8,128)}, bf16[...) while((s32[]{:T(128)}, ...), condition=%wide.region_4.5_spmd, body=%wide.region_2.4_spmd.sunk | while | flops 33980164 | bytes 1183403 | solution.py:90
  79.9 1.4 fusion.115
  82.5 1.4 fusion.115
  85.1 1.4 fusion.115
  87.7 1.4 fusion.115
  90.3 1.4 fusion.115
  93.0 1.4 fusion.115
  95.6 1.4 fusion.115
  98.2 1.4 fusion.115
  100.8 1.4 fusion.115
  103.4 1.4 fusion.115
  106.0 1.4 fusion.115
  108.6 1.4 fusion.115
  111.2 1.4 fusion.115
  113.8 1.4 fusion.115
  116.5 1.4 fusion.115
  119.1 1.4 fusion.115
  121.9 1.5 copy.144
  123.3 4.6 %all-to-all-start.3 = ((bf16[16,2,128,256]{2,3,1,0:T(8,128)(2,1)}), bf16[16,2,128,256]{2,3,1,0:T(8,128)(2,1)}, u32[]{:S(2)}, u32[]{:S(2)}) async-start(bf16[16,2,128,256]{2,3,1,0:T(8,128)(2,1)} %copy.144), calls=%async_computation.3 | async-start | bytes 4194304 | tf_op jit(solution)/shard_map/all_to_all | solution.py:154
  128.9 2.0 fusion.63
  132.0 2.2 %fusion.82 = (f32[4,4,128]{2,1,0:T(4,128)S(1)}, f32[4,4,128,256]{2,3,1,0:T(8,128)}) fusion(pred[128,256]{0,1:T(8,128)(4,1)S(1)} %copy-done.22, bf16[256,4,128,1]{0,2,3,1:T(8,128)(2,1)S(1)} %bitcast.274, bf16[128,4,4,128]{0,3,2,1:T(8,128)(2,1)S(1)} %bitcast.272), kind=kOutput, calls=%fused_computation.120 | convolution fusion | flops 136315136 | bytes 2924544 | tf_op jit(solution)/shard_map/sub | solution.py:19
  134.2 2.1 %fusion.83 = (f32[4,4,128]{2,1,0:T(4,128)S(1)}, f32[4,4,128,256]{2,3,1,0:T(8,128)}) fusion(pred[128,256]{0,1:T(8,128)(4,1)S(1)} %copy-done.21, bf16[256,4,128,1]{0,2,3,1:T(8,128)(2,1)S(1)} %bitcast.273, bf16[128,4,4,128]{0,3,2,1:T(8,128)(2,1)S(1)} %bitcast.269), kind=kOutput, calls=%fused_computation.121 | convolution fusion | flops 136315136 | bytes 2924544 | tf_op jit(solution)/shard_map/sub | solution.py:19
  136.3 2.0 fusion.56
  138.8 14.4 %all-to-all-done.3 = bf16[16,2,128,256]{2,3,1,0:T(8,128)(2,1)} async-done(((bf16[16,2,128,256]{2,3,1,0:T(8,128)(2,1)}), bf16[16,2,128,256]{2,3,1,0:T(8,128)(2,1)}, u32[]{:S(2)}, u32[]{:S(2)}) %all-to-all-start.3) | async-done | bytes 2097184 | tf_op jit(solution)/shard_map/all_to_all | solution.py:154
  153.2 3.9 %copy.145 = bf16[16,2,128,256]{3,2,1,0:T(8,128)(2,1)} copy(bf16[16,2,128,256]{2,3,1,0:T(8,128)(2,1)} %all-to-all-done.3) | data formatting | bytes 4194304 | tf_op jit(solution)/shard_map/all_to_all | solution.py:154
  157.1 2.3 %fusion.79 = (bf16[1,1,128,8,256]{4,2,0,1,3:T(8,128)(2,1)}, bf16[1,1,128,8,256]{4,2,0,1,3:T(8,128)(2,1)}) fusion(bf16[2,2,128,8,256]{4,2,0,1,3:T(8,128)(2,1)} %bitcast.239), kind=kLoop, calls=%fused_computation.117 | loop fusion | bytes 2097152 | tf_op jit(solution)/shard_map/slice | solution.py:165
  159.4 2.1 %copy.158 = bf16[1,1,128,8,256]{2,4,3,1,0:T(8,128)(2,1)} copy(bf16[1,1,128,8,256]{4,2,0,1,3:T(8,128)(2,1)} %get-tuple-element.239) | data formatting | bytes 1048576 | tf_op jit(solution)/shard_map/slice | solution.py:165
  161.5 2.4 %fusion.85 = f32[4,128,256,1]{2,1,3,0:T(8,128)} fusion(bf16[128,4,4,128]{0,3,2,1:T(8,128)(2,1)} %bitcast.245, bf16[4,4,128,256]{2,3,1,0:T(8,128)(2,1)S(1)} %fusion.56), kind=kOutput, calls=%fused_computation.123 | convolution fusion | flops 134217728 | bytes 2097152 | tf_op jit(solution)/shard_map/hgqk,qhgd->khd/dot_general | solution.py:51
  164.2 2.6 %fusion.43 = f32[4,256,128]{1,2,0:T(8,128)S(1)} fusion(bf16[128,4,4,128]{0,3,2,1:T(8,128)(2,1)} %bitcast.271, bf16[256,4,128,1]{0,2,3,1:T(8,128)(2,1)S(1)} %bitcast.265, bf16[128,4,4,128]{0,3,2,1:T(8,128)(2,1)} %bitcast.246, f32[4,4,128]{2,1,0:T(4,128)S(1)} %bitcast.275, f32[4,4,128,256]{2,3,1,0:T(8,128)} %get-tuple-element.252, ...), kind=kOutput, calls=%fused_computation.55 | convolution fusion | flops 270663680 | bytes 3948544 | tf_op jit(solution)/shard_map/hgqk,qhgd->khd/dot_general | solution.py:48
  167.1 1.5 copy.150
  168.9 3.3 %fusion.42 = f32[4,256,128]{1,2,0:T(8,128)} fusion(bf16[128,4,4,128]{0,3,2,1:T(8,128)(2,1)} %bitcast.270, bf16[256,4,128,1]{0,2,3,1:T(8,128)(2,1)S(1)} %bitcast.263, bf16[128,4,4,128]{0,3,2,1:T(8,128)(2,1)S(1)} %bitcast.243, f32[4,4,128]{2,1,0:T(4,128)S(1)} %bitcast.276, f32[4,4,128,256]{2,3,1,0:T(8,128)} %get-tuple-element.254, ...), kind=kOutput, calls=%fused_computation.54 | convolution fusion | flops 270663680 | bytes 3948544 | tf_op jit(solution)/shard_map/hgqk,qhgd->khd/dot_general | solution.py:48
  174.4 7.7 %collective-permute-start.2 = (f32[2,128,512]{2,1,0:T(8,128)}, f32[2,128,512]{2,1,0:T(8,128)}, u32[]{:S(2)}, u32[]{:S(2)}) collective-permute-start(f32[2,128,512]{2,1,0:T(8,128)} %pad_maximum_fusion.2), channel_id=1, source_target_pairs={{1,0},{2,1},{3,2},{4,3},{5,4},{6,5},{7,6},{8,7},{9,8},{10,9},{11,1... | collective-permute-start | bytes 1572872 | tf_op jit(solution)/shard_map/ppermute | solution.py:13
  182.1 2.3 %fusion.84 = f32[4,128,256,1]{2,1,3,0:T(8,128)} fusion(bf16[128,4,4,128]{0,3,2,1:T(8,128)(2,1)} %bitcast.244, bf16[4,4,128,256]{2,3,1,0:T(8,128)(2,1)S(1)} %fusion.55), kind=kOutput, calls=%fused_computation.122 | convolution fusion | flops 134217728 | bytes 2097152 | tf_op jit(solution)/shard_map/hgqk,qhgd->khd/dot_general | solution.py:51
  184.4 2.2 %copy.168 = f32[1,256,512]{2,1,0:T(8,128)} copy(f32[1,256,512]{1,2,0:T(8,128)} %bitcast.260) | data formatting | bytes 1048576 | tf_op jit(solution)/shard_map/stack;reshape | solution.py:170
  186.6 2.0 copy.167
  188.6 1.9 pad_maximum_fusion.1
  190.5 1.9 collective-permute-start.3
  193.5 2.4 %copy.146 = bf16[1,2,128,8,256]{2,4,3,1,0:T(8,128)(2,1)} copy(bf16[1,2,128,8,256]{4,2,0,1,3:T(8,128)(2,1)} %slice.81) | data formatting | bytes 2097152 | tf_op jit(solution)/shard_map/slice | solution.py:159
  195.8 2.4 %copy.169 = bf16[1,2,128,2048]{3,2,1,0:T(8,128)(2,1)} copy(bf16[1,2,128,2048]{2,3,1,0:T(8,128)(2,1)} %bitcast.251) | data formatting | bytes 2097152
  198.2 1.8 fusion.65
  200.0 2.5 %collective-permute-done.3 = f32[2,128,512]{2,1,0:T(8,128)} collective-permute-done((f32[2,128,512]{2,1,0:T(8,128)}, f32[2,128,512]{2,1,0:T(8,128)}, u32[]{:S(2)}, u32[]{:S(2)}) %collective-permute-start.3) | collective-permute-done | bytes 524320 | tf_op jit(solution)/shard_map/ppermute | solution.py:13
  202.5 1.8 fusion.66
  (140 shorter events, 31.0 us)
Async XLA Ops:
  0.6 34.8 %copy-start = (bf16[2,128,2048]{2,1,0:T(8,128)(2,1)S(1)}, bf16[2,128,2048]{2,1,0:T(8,128)(2,1)}, u32[]{:S(2)}) copy-start(bf16[2,128,2048]{2,1,0:T(8,128)(2,1)} %param.10) | copy-start | bytes 3145732
  3.7 17.4 %copy-start.20 = (s32[2,4096]{1,0:T(2,128)S(1)}, s32[2,4096]{1,0:T(2,128)}, u32[]{:S(2)}) copy-start(s32[2,4096]{1,0:T(2,128)} %param.11) | copy-start | bytes 98308
  3.7 22.9 %all-to-all-start.1 = ((bf16[16,128,256]{2,1,0:T(8,128)(2,1)}), bf16[16,128,256]{2,1,0:T(8,128)(2,1)S(1)}, u32[]{:S(2)}, u32[]{:S(2)}) async-start(bf16[16,128,256]{2,1,0:T(8,128)(2,1)} %bitcast.248), calls=%async_computation.1 | async-start | bytes 2097152 | tf_op jit(solution)/shard_map/all_to_all | solution.py:144
  11.7 9.4 %collective-permute-start = (bf16[2,128,512]{1,2,0:T(8,128)(2,1)S(1)}, bf16[2,128,512]{1,2,0:T(8,128)(2,1)}, u32[]{:S(2)}, u32[]{:S(2)}) collective-permute-start(bf16[2,128,512]{1,2,0:T(8,128)(2,1)S(1)} %bitcast.254), channel_id=1, source_target_pairs={{0,1},{1,2},{2,3},{3,4},{4,5},{5,6},{6,7},{7,8},{8,9},{9,10},{10,1... | collective-permute-start | bytes 786440 | tf_op jit(solution)/shard_map/ppermute | solution.py:13
  19.1 18.1 %collective-permute-start.1 = (bf16[2,128,512]{1,2,0:T(8,128)(2,1)}, bf16[2,128,512]{1,2,0:T(8,128)(2,1)}, u32[]{:S(2)}, u32[]{:S(2)}) collective-permute-start(bf16[2,128,512]{1,2,0:T(8,128)(2,1)} %bitcast.257), channel_id=1, source_target_pairs={{0,1},{1,2},{2,3},{3,4},{4,5},{5,6},{6,7},{7,8},{8,9},{9,10},{10,1... | collective-permute-start | bytes 786440 | tf_op jit(solution)/shard_map/ppermute | solution.py:13
  26.6 2.6 %copy-start.12 = (bf16[16,128,256]{2,1,0:T(8,128)(2,1)}, bf16[16,128,256]{2,1,0:T(8,128)(2,1)S(1)}, u32[]{:S(2)}) copy-start(bf16[16,128,256]{2,1,0:T(8,128)(2,1)S(1)} %all-to-all-done.1) | copy-start | bytes 3145732
  29.2 21.5 %all-to-all-start = ((bf16[16,256,128]{2,1,0:T(8,128)(2,1)}), bf16[16,256,128]{2,1,0:T(8,128)(2,1)S(1)}, u32[]{:S(2)}, u32[]{:S(2)}) async-start(bf16[16,256,128]{2,1,0:T(8,128)(2,1)} %bitcast.249), calls=%async_computation | async-start | bytes 2097152 | tf_op jit(solution)/shard_map/all_to_all | solution.py:145
  35.6 7.9 %copy-start.17 = (bf16[1,128,256]{1,2,0:T(8,128)(2,1)}, bf16[1,128,256]{1,2,0:T(8,128)(2,1)S(1)}, u32[]{:S(2)}) copy-start(bf16[1,128,256]{1,2,0:T(8,128)(2,1)S(1)} %copy.207) | copy-start | bytes 196612
  50.7 2.6 %copy-start.3 = (bf16[16,256,128]{2,1,0:T(8,128)(2,1)}, bf16[16,256,128]{2,1,0:T(8,128)(2,1)S(1)}, u32[]{:S(2)}) copy-start(bf16[16,256,128]{2,1,0:T(8,128)(2,1)S(1)} %all-to-all-done) | copy-start | bytes 3145732
  53.3 20.0 %all-to-all-start.2 = ((bf16[16,256,128]{2,1,0:T(8,128)(2,1)}), bf16[16,256,128]{2,1,0:T(8,128)(2,1)S(1)}, u32[]{:S(2)}, u32[]{:S(2)}) async-start(bf16[16,256,128]{2,1,0:T(8,128)(2,1)} %bitcast.250), calls=%async_computation.2 | async-start | bytes 2097152 | tf_op jit(solution)/shard_map/all_to_all | solution.py:146
  57.8 2.3 %copy-start.23 = (pred[128,256]{0,1:T(8,128)(4,1)S(1)}, pred[128,256]{0,1:T(8,128)(4,1)}, u32[]{:S(2)}) copy-start(pred[128,256]{0,1:T(8,128)(4,1)} %get-tuple-element.248) | copy-start | bytes 98308
  73.3 1.0 copy-start.2
  123.3 29.8 %all-to-all-start.3 = ((bf16[16,2,128,256]{2,3,1,0:T(8,128)(2,1)}), bf16[16,2,128,256]{2,3,1,0:T(8,128)(2,1)}, u32[]{:S(2)}, u32[]{:S(2)}) async-start(bf16[16,2,128,256]{2,3,1,0:T(8,128)(2,1)} %copy.144), calls=%async_computation.3 | async-start | bytes 4194304 | tf_op jit(solution)/shard_map/all_to_all | solution.py:154
  128.0 1.0 copy-start.13
  128.0 4.0 %copy-start.22 = (pred[128,256]{0,1:T(8,128)(4,1)S(1)}, pred[128,256]{0,1:T(8,128)(4,1)}, u32[]{:S(2)}) copy-start(pred[128,256]{0,1:T(8,128)(4,1)} %get-tuple-element.247) | copy-start | bytes 98308
  128.9 5.3 %copy-start.18 = (bf16[1,1,128,2048]{2,3,1,0:T(8,128)(2,1)}, bf16[1,1,128,2048]{2,3,1,0:T(8,128)(2,1)S(1)}, u32[]{:S(2)}) copy-start(bf16[1,1,128,2048]{2,3,1,0:T(8,128)(2,1)S(1)} %get-tuple-element.240) | copy-start | bytes 1572868
  128.9 3.1 %copy-start.19 = (bf16[1,1,128,2048]{2,3,1,0:T(8,128)(2,1)S(1)}, bf16[1,1,128,2048]{2,3,1,0:T(8,128)(2,1)}, u32[]{:S(2)}) copy-start(bf16[1,1,128,2048]{2,3,1,0:T(8,128)(2,1)} %get-tuple-element.241) | copy-start | bytes 1572868
  132.0 2.2 %copy-start.21 = (pred[128,256]{0,1:T(8,128)(4,1)S(1)}, pred[128,256]{0,1:T(8,128)(4,1)}, u32[]{:S(2)}) copy-start(pred[128,256]{0,1:T(8,128)(4,1)} %get-tuple-element.246) | copy-start | bytes 98308
  136.3 2.2 %copy-start.14 = (f32[4,4,128,256]{2,3,1,0:T(8,128)S(1)}, f32[4,4,128,256]{2,3,1,0:T(8,128)}, u32[]{:S(2)}) copy-start(f32[4,4,128,256]{2,3,1,0:T(8,128)} %get-tuple-element.254) | copy-start | bytes 6291460
  159.4 4.5 %copy-start.16 = (bf16[1,256,512]{1,2,0:T(8,128)(2,1)S(1)}, bf16[1,256,512]{1,2,0:T(8,128)(2,1)}, u32[]{:S(2)}) copy-start(bf16[1,256,512]{1,2,0:T(8,128)(2,1)} %get-tuple-element.245) | copy-start | bytes 786436
  161.5 2.4 %copy-start.11 = (bf16[1,1,128,8,256]{2,4,3,1,0:T(8,128)(2,1)S(1)}, bf16[1,1,128,8,256]{2,4,3,1,0:T(8,128)(2,1)}, u32[]{:S(2)}) copy-start(bf16[1,1,128,8,256]{2,4,3,1,0:T(8,128)(2,1)} %copy.158) | copy-start | bytes 1572868
  166.8 1.7 copy-start.15
  167.1 6.4 %copy-start.4 = (f32[1,256,512]{2,1,0:T(8,128)}, f32[1,256,512]{2,1,0:T(8,128)S(1)}, u32[]{:S(2)}) copy-start(f32[1,256,512]{2,1,0:T(8,128)S(1)} %copy.164) | copy-start | bytes 1572868
  168.6 3.6 %copy-start.10 = (bf16[1,1,128,8,256]{2,4,3,1,0:T(8,128)(2,1)}, bf16[1,1,128,8,256]{2,4,3,1,0:T(8,128)(2,1)S(1)}, u32[]{:S(2)}) copy-start(bf16[1,1,128,8,256]{2,4,3,1,0:T(8,128)(2,1)S(1)} %copy.150) | copy-start | bytes 1572868
  173.5 8.6 %copy-start.6 = (f32[1,256,512]{2,1,0:T(8,128)}, f32[1,256,512]{2,1,0:T(8,128)S(1)}, u32[]{:S(2)}) copy-start(f32[1,256,512]{2,1,0:T(8,128)S(1)} %copy.163) | copy-start | bytes 1572868
  174.4 23.8 %collective-permute-start.2 = (f32[2,128,512]{2,1,0:T(8,128)}, f32[2,128,512]{2,1,0:T(8,128)}, u32[]{:S(2)}, u32[]{:S(2)}) collective-permute-start(f32[2,128,512]{2,1,0:T(8,128)} %pad_maximum_fusion.2), channel_id=1, source_target_pairs={{1,0},{2,1},{3,2},{4,3},{5,4},{6,5},{7,6},{8,7},{9,8},{10,9},{11,1... | collective-permute-start | bytes 1572872 | tf_op jit(solution)/shard_map/ppermute | solution.py:13
  184.4 8.0 %copy-start.1 = (bf16[16,2,128,256]{3,2,1,0:T(8,128)(2,1)S(1)}, bf16[16,2,128,256]{3,2,1,0:T(8,128)(2,1)}, u32[]{:S(2)}) copy-start(bf16[16,2,128,256]{3,2,1,0:T(8,128)(2,1)} %copy.145) | copy-start | bytes 6291460
  190.5 12.0 %collective-permute-start.3 = (f32[2,128,512]{2,1,0:T(8,128)}, f32[2,128,512]{2,1,0:T(8,128)}, u32[]{:S(2)}, u32[]{:S(2)}) collective-permute-start(f32[2,128,512]{2,1,0:T(8,128)} %pad_maximum_fusion.1), channel_id=1, source_target_pairs={{1,0},{2,1},{3,2},{4,3},{5,4},{6,5},{7,6},{8,7},{9,8},{10,9},{11,1... | collective-permute-start | bytes 1572872 | tf_op jit(solution)/shard_map/ppermute | solution.py:13
  193.5 4.7 %copy-start.5 = (f32[1,256,512]{2,1,0:T(8,128)S(1)}, f32[1,256,512]{2,1,0:T(8,128)}, u32[]{:S(2)}) copy-start(f32[1,256,512]{2,1,0:T(8,128)} %copy-done.4) | copy-start | bytes 1572868
  193.5 4.7 %copy-start.7 = (f32[1,256,512]{2,1,0:T(8,128)S(1)}, f32[1,256,512]{2,1,0:T(8,128)}, u32[]{:S(2)}) copy-start(f32[1,256,512]{2,1,0:T(8,128)} %copy-done.6) | copy-start | bytes 1572868
  195.8 6.7 %copy-start.8 = (f32[1,256,512]{2,1,0:T(8,128)S(1)}, f32[1,256,512]{2,1,0:T(8,128)}, u32[]{:S(2)}) copy-start(f32[1,256,512]{2,1,0:T(8,128)} %copy.168) | copy-start | bytes 1572868
  195.8 6.7 %copy-start.9 = (f32[1,256,512]{2,1,0:T(8,128)S(1)}, f32[1,256,512]{2,1,0:T(8,128)}, u32[]{:S(2)}) copy-start(f32[1,256,512]{2,1,0:T(8,128)} %copy.167) | copy-start | bytes 1572868

commit v2 on v1

v2 whole, which is shorter than its diff:
```python
import jax
import jax.numpy as jnp
from jax import lax
from jax.experimental import pallas as pl
from jax.experimental.pallas import tpu as pltpu
from jax.sharding import PartitionSpec as P

DH = 128
WINDOW = 128
SCALE = DH ** (-0.5)
NT = (((1,), (1,)), ((), ()))
TN = (((0,), (0,)), ((), ()))


def from_behind(block, axis, distance):
    devices = range(lax.axis_size(axis))
    route = [(i - distance, i) for i in devices if i - distance in devices]
    return lax.ppermute(block, axis, route)


def head_core(q, k, v, g, allowed):
    scores = lax.dot_general(q, k, NT, preferred_element_type=jnp.float32) * SCALE
    masked = jnp.where(allowed, scores, -jnp.inf)
    row_max = jnp.max(masked, axis=-1, keepdims=True)
    weights = jnp.exp(masked - row_max)
    prob = weights / jnp.sum(weights, axis=-1, keepdims=True)
    prob_low = prob.astype(jnp.bfloat16)
    out = jnp.dot(prob_low, v, preferred_element_type=jnp.float32)
    grad_prob = lax.dot_general(g, v, NT, preferred_element_type=jnp.float32)
    grad_dot = jnp.sum(g.astype(jnp.float32) * out, axis=-1, keepdims=True)
    grad_score = (prob * (grad_prob - grad_dot)).astype(jnp.bfloat16)
    return prob_low, grad_score


def chain_kernel(q_ref, k_ref, v_ref, g0_ref, m_ref, o_ref):
    layers = q_ref.shape[0]
    heads = q_ref.shape[2] // DH
    allowed = m_ref[...] != 0

    def step(i, g):
        layer = layers - 1 - i
        k = k_ref[layer]
        v = v_ref[layer]
        outs = []
        for h in range(heads):
            cols = slice(h * DH, (h + 1) * DH)
            q = q_ref[layer, :, cols]
            gh = g[:, cols]
            _, grad_score = head_core(q, k, v, gh, allowed)
            dq = jnp.dot(grad_score, k, preferred_element_type=jnp.float32) * SCALE
            outs.append((gh.astype(jnp.float32) + dq).astype(jnp.bfloat16))
        g_new = jnp.concatenate(outs, axis=-1) if heads > 1 else outs[0]
        o_ref[layer] = g_new
        return g_new

    lax.fori_loop(0, layers, step, g0_ref[...])


def chain_call(query_t, key_t, value_t, grad_top, allowed_i32, interpret=False):
    return pl.pallas_call(
        chain_kernel,
        out_shape=jax.ShapeDtypeStruct(query_t.shape, jnp.bfloat16),
        interpret=interpret,
    )(query_t, key_t, value_t, grad_top, allowed_i32)


def layer_kernel(q_ref, k_ref, v_ref, g_ref, m_ref, dk_ref, dv_ref, gl_ref):
    heads = q_ref.shape[2] // DH
    allowed = m_ref[0] != 0
    k = k_ref[0]
    v = v_ref[0]
    dk = None
    dv = None
    for h in range(heads):
        cols = slice(h * DH, (h + 1) * DH)
        q = q_ref[0, :, cols]
        g = g_ref[0, :, cols]
        prob_low, grad_score = head_core(q, k, v, g, allowed)
        dq = jnp.dot(grad_score, k, preferred_element_type=jnp.float32) * SCALE
        gl_ref[0, :, cols] = (g.astype(jnp.float32) + dq).astype(jnp.bfloat16)
        dk_h = lax.dot_general(grad_score, q, TN, preferred_element_type=jnp.float32)
        dv_h = lax.dot_general(prob_low, g, TN, preferred_element_type=jnp.float32)
        dk = dk_h if dk is None else dk + dk_h
        dv = dv_h if dv is None else dv + dv_h
    dk_ref[0] = dk * SCALE
    dv_ref[0] = dv


def layer_call(query, key_rows, value_rows, grad_in, allowed_i32, interpret=False):
    micro, rows, width = query.shape
    keys2 = key_rows.shape[1]
    kv_heads = key_rows.shape[2] // DH
    group = width // (kv_heads * DH)
    gw = group * DH
    return pl.pallas_call(
        layer_kernel,
        grid=(micro, kv_heads),
        in_specs=[
            pl.BlockSpec((1, rows, gw), lambda m, g: (m, 0, g)),
            pl.BlockSpec((1, keys2, DH), lambda m, g: (m, 0, g)),
            pl.BlockSpec((1, keys2, DH), lambda m, g: (m, 0, g)),
            pl.BlockSpec((1, rows, gw), lambda m, g: (m, 0, g)),
            pl.BlockSpec((1, rows, keys2), lambda m, g: (m, 0, 0)),
        ],
        out_specs=[
            pl.BlockSpec((1, keys2, DH), lambda m, g: (m, 0, g)),
            pl.BlockSpec((1, keys2, DH), lambda m, g: (m, 0, g)),
            pl.BlockSpec((1, rows, gw), lambda m, g: (m, 0, g)),
        ],
        out_shape=[
            jax.ShapeDtypeStruct(key_rows.shape, jnp.float32),
            jax.ShapeDtypeStruct(key_rows.shape, jnp.float32),
            jax.ShapeDtypeStruct(query.shape, jnp.bfloat16),
        ],
        interpret=interpret,
    )(query, key_rows, value_rows, grad_in, allowed_i32)


def per_device(queries, keys, values, out_grad, segments):
    micro_count = queries.shape[1]
    row_count = queries.shape[2]
    query_width = queries.shape[3]
    key_width = keys.shape[3]
    section_count = lax.axis_size("pipe")
    section_index = lax.axis_index("pipe")
    seq_index = lax.axis_index("seq")
    kv_heads = key_width // DH
    q_heads = query_width // DH
    group_size = q_heads // kv_heads
    head_blocks = section_count // micro_count
    block_heads = q_heads // head_blocks
    block_width = block_heads * DH
    blocks_per_kv = group_size // block_heads
    own_query = queries[0]
    own_key = keys[0]
    own_value = values[0]
    seg_padded = jnp.concatenate(
        [jnp.full((micro_count, row_count), -1, jnp.int32), segments], axis=1
    )
    query_pos = seq_index * row_count + jnp.arange(row_count, dtype=jnp.int32)
    key_pos = seq_index * row_count - row_count + jnp.arange(2 * row_count, dtype=jnp.int32)
    seg_query = lax.dynamic_slice_in_dim(
        seg_padded, seq_index * row_count + row_count, row_count, axis=1
    )
    seg_key = lax.dynamic_slice_in_dim(seg_padded, seq_index * row_count, 2 * row_count, axis=1)
    near = (
        (key_pos[None, :] <= query_pos[:, None])
        & (query_pos[:, None] - key_pos[None, :] < WINDOW)
        & (key_pos[None, :] >= 0)
    )
    masks = (near[None] & (seg_query[:, :, None] == seg_key[:, None, :])).astype(jnp.int32)
    halo_key, halo_value = from_behind((own_key, own_value), "seq", 1)
    key_rows = jnp.concatenate([halo_key, own_key], axis=1)
    value_rows = jnp.concatenate([halo_value, own_value], axis=1)

    my_block = section_index // micro_count
    my_micro = section_index % micro_count
    query_send = jnp.transpose(
        own_query.reshape(micro_count, row_count, head_blocks, block_width), (2, 0, 1, 3)
    ).reshape(section_count, row_count, block_width)
    kv_send = []
    for rows in (own_key, own_value):
        split = jnp.transpose(rows.reshape(micro_count, row_count, kv_heads, DH), (2, 0, 1, 3))
        split = jnp.broadcast_to(
            split[:, None], (kv_heads, blocks_per_kv, micro_count, row_count, DH)
        )
        kv_send.append(split.reshape(section_count, row_count, DH))
    sent = lax.all_to_all(jnp.concatenate([query_send] + kv_send, axis=-1), "pipe", 0, 0)
    query_t = sent[..., :block_width]
    key_own_t = sent[..., block_width:block_width + DH]
    value_own_t = sent[..., block_width + DH:]
    key_halo_t, value_halo_t = from_behind((key_own_t, value_own_t), "seq", 1)
    key_t = jnp.concatenate([key_halo_t, key_own_t], axis=1)
    value_t = jnp.concatenate([value_halo_t, value_own_t], axis=1)
    grad_top = lax.dynamic_slice(
        out_grad, (my_micro, 0, my_block * block_width), (1, row_count, block_width)
    )[0]
    allowed = lax.dynamic_index_in_dim(masks, my_micro, 0, keepdims=False)
    grads = chain_call(query_t, key_t, value_t, grad_top, allowed)
    grads_above = jnp.concatenate([grads[1:], grad_top[None]], axis=0)
    back = lax.all_to_all(grads_above, "pipe", 0, 0)
    grad_in = jnp.transpose(
        back.reshape(head_blocks, micro_count, row_count, block_width), (1, 2, 0, 3)
    ).reshape(micro_count, row_count, query_width)

    key_all, value_all, query_all = layer_call(own_query, key_rows, value_rows, grad_in, masks)
    back_key, back_value = from_behind(
        (key_all[:, :row_count], value_all[:, :row_count]), "seq", -1
    )
    key_grads = (key_all[:, row_count:] + back_key).astype(jnp.bfloat16)
    value_grads = (value_all[:, row_count:] + back_value).astype(jnp.bfloat16)
    return (query_all[None], key_grads[None], value_grads[None])


def solution(mesh):
    placed = (
        P("pipe", None, "seq", None),
        P("pipe", None, "seq", None),
        P("pipe", None, "seq", None),
        P(None, "seq", None),
        P(),
    )
    return jax.shard_map(
        per_device,
        mesh=mesh,
        in_specs=placed,
        out_specs=(
            P("pipe", None, "seq", None),
            P("pipe", None, "seq", None),
            P("pipe", None, "seq", None),
        ),
        check_vma=False,
    )
```

time: 207 us -> 151 us (0.73); the launches traced: 204 us -> 151 us
  matrix products: 44.4 us -> 0 us
  Pallas kernels: 0 us -> 41.2 us
  local copies, waits for them, and re-layouts: 46.8 us -> 11 us
  other arithmetic: 37.2 us -> 8.22 us
  waiting for transfers between devices: 35.5 us -> 58.5 us
  starting transfers between devices: 38.5 us -> 30.7 us
    pallas_call x0 -> x2, Pallas kernels: none -> 41.2 us  [the longest x1 21.6 us: layer_call(): pl.pallas_call(layer_kernel, grid=(micro, kv_heads), in_specs=[pl.BlockSp...]
    dot_general x24 -> x0, matrix products: 40.1 us -> none  [the longest x16 22.3 us: step(): jnp.einsum('hqk,kd->hqd', grad_score, key_rows, preferred_element_type=jn...]
    ppermute x4 -> x6, waiting for transfers between devices: 2.5 us -> 21.1 us  [from_behind(): return lax.ppermute(block, axis, route)]
    reduce_sum x16 -> x0, other arithmetic: 16.3 us -> none  [step(): grad_dot = jnp.sum(grad.astype(jnp.float32) * out, axis=-1, keepdims=True)]
    all_to_all x4 -> x2, starting transfers between devices: 21.4 us -> 10.4 us  [the longest x1 6.75 us: per_device(): lax.all_to_all(jnp.concatenate([query_send] + kv_send, axis=-1), 'pipe',...]
    another operation x5 -> x3, local copies, waits for them, and re-layouts: 7.14 us -> 0.35 us  [the longest x1 0.22 us: per_device(): own_query.reshape(micro_count, row_count, head_blocks, block_width)]
    slice x6 -> x4, local copies, waits for them, and re-layouts: 10.1 us -> 3.64 us  [the longest x1 1.23 us: per_device(): value_all[:, :row_count]]
    all_to_all x2 -> x0, local copies, waits for them, and re-layouts: 6.21 us -> none  [the longest x1 3.93 us: per_device(): back = lax.all_to_all(back_send, 'pipe', 0, 0)]
  transfers between devices with their start and end apart: 8 -> 8, of which waited for: 5 -> 8; matrix products, arithmetic and copies ran while one was open for 25% -> 5% of each run, Pallas kernels for 0% -> 0%
where the time goes in v2:
time: 151 us
  waiting for transfers between devices  58.5 us (39%)
  Pallas kernels  41.2 us (27%)
  starting transfers between devices  30.7 us (20%)
  local copies, waits for them, and re-layouts  11 us (7%)
  other arithmetic  8.22 us (5%)
    all_to_all x1, waiting for transfers between devices, per_device(): lax.all_to_all(jnp.concatenate([query_send] + kv_send, axis=-1), 'pipe',...  30.1 us
    pallas_call x1, Pallas kernels, layer_call(): pl.pallas_call(layer_kernel, grid=(micro, kv_heads), in_specs=[pl.BlockSp...  21.6 us
    ppermute x6, waiting for transfers between devices, from_behind(): return lax.ppermute(block, axis, route)  21.1 us
    ppermute x6, starting transfers between devices, from_behind(): return lax.ppermute(block, axis, route)  20.3 us
    pallas_call x1, Pallas kernels, chain_call(): pl.pallas_call(chain_kernel, out_shape=jax.ShapeDtypeStruct(query_t.shape...  19.6 us
    all_to_all x1, waiting for transfers between devices, per_device(): back = lax.all_to_all(grads_above, 'pipe', 0, 0)  7.32 us
    all_to_all x1, starting transfers between devices, per_device(): lax.all_to_all(jnp.concatenate([query_send] + kv_send, axis=-1), 'pipe',...  6.75 us
    all_to_all x1, starting transfers between devices, per_device(): back = lax.all_to_all(grads_above, 'pipe', 0, 0)  3.66 us
  transfers between devices with their start and end apart: 8, of which 8 were waited for; matrix products, arithmetic and copies ran while one was open for 5% of the time, Pallas kernels for 0%

profile of v2, /device:TPU:97, one launch (start us, length us, event | category | flops | bytes accessed | tf_op | source)
XLA Modules:
  0.0 150.6 jit_solution(16455202035131305453)
XLA Ops:
  0.6 0.0 copy-start
  0.6 0.0 copy-start.4
  0.7 1.6 %copy.12 = bf16[32,8,8,256]{3,2,1,0:T(8,128)(2,1)S(1)} copy(bf16[32,8,8,256]{3,1,2,0:T(8,128)(2,1)} %bitcast.34) | data formatting | bytes 2097152
  2.3 0.0 copy-start.6
  2.3 0.2 copy.8
  2.5 0.0 copy-done.4
  2.5 0.1 reshape_squeeze.10
  2.7 0.6 copy-done.6
  3.2 0.1 reshape_squeeze.11
  3.4 0.1 broadcast_in_dim.10
  3.5 0.1 broadcast_in_dim.11
  3.6 1.6 %pad_maximum_fusion = bf16[16,128,512]{2,1,0:T(8,128)(2,1)} fusion(bf16[16,128,128]{2,1,0:T(8,128)(2,1)S(1)} %bitcast.41, bf16[16,128,128]{2,1,0:T(8,128)(2,1)S(1)} %bitcast.40, bf16[16,128,256]{2,1,0:T(8,128)(2,1)S(1)} %bitcast.39), kind=kLoop, calls=%fused_computation | loop fusion | flops 6291456 | bytes 4194304 | tf_op jit(solution)/shard_map/concatenate | solution.py:168
  5.1 6.8 %all-to-all-start = ((bf16[16,128,512]{2,1,0:T(8,128)(2,1)}), bf16[16,128,512]{2,1,0:T(8,128)(2,1)S(1)}, u32[]{:S(2)}, u32[]{:S(2)}) async-start(bf16[16,128,512]{2,1,0:T(8,128)(2,1)} %pad_maximum_fusion), calls=%async_computation | async-start | bytes 4194304 | tf_op jit(solution)/shard_map/all_to_all | solution.py:168
  11.9 0.0 copy-start.8
  12.0 0.0 copy-done
  12.0 0.6 fusion.5.g0_ref
  12.7 0.1 fusion.3
  12.8 30.1 %all-to-all-done = bf16[16,128,512]{2,1,0:T(8,128)(2,1)S(1)} async-done(((bf16[16,128,512]{2,1,0:T(8,128)(2,1)}), bf16[16,128,512]{2,1,0:T(8,128)(2,1)S(1)}, u32[]{:S(2)}, u32[]{:S(2)}) %all-to-all-start) | async-done | bytes 2097184 | tf_op jit(solution)/shard_map/all_to_all | solution.py:168
  42.9 0.3 fusion.4
  43.2 6.4 %collective-permute-start.3 = (bf16[16,128,128]{2,1,0:T(8,128)(2,1)S(1)}, bf16[16,128,128]{2,1,0:T(8,128)(2,1)S(1)}, u32[]{:S(2)}, u32[]{:S(2)}) collective-permute-start(bf16[16,128,128]{2,1,0:T(8,128)(2,1)S(1)} %get-tuple-element.9), channel_id=1, source_target_pairs={{0,1},{1,2},{2,3},{3,4},{4,5},{5,6},{6,7},{7,8},{8,9},{9,10},{10,1... | collective-permute-start | bytes 1572872 | tf_op jit(solution)/shard_map/ppermute | solution.py:18
  49.6 0.0 copy-done.8
  49.6 1.9 %collective-permute-start.2 = (bf16[16,128,128]{2,1,0:T(8,128)(2,1)S(1)}, bf16[16,128,128]{2,1,0:T(8,128)(2,1)S(1)}, u32[]{:S(2)}, u32[]{:S(2)}) collective-permute-start(bf16[16,128,128]{2,1,0:T(8,128)(2,1)S(1)} %get-tuple-element.10), channel_id=1, source_target_pairs={{0,1},{1,2},{2,3},{3,4},{4,5},{5,6},{6,7},{7,8},{8,9},{9,10},{10,1... | collective-permute-start | bytes 1572872 | tf_op jit(solution)/shard_map/ppermute | solution.py:18
  51.6 0.1 and_convert_fusion.m_ref
  51.7 0.0 copy-start.1
  51.7 0.7 dynamic-slice_bitcast_fusion.m_ref
  52.4 1.1 slice.32.q_ref
  53.5 2.2 %collective-permute-done.3 = bf16[16,128,128]{2,1,0:T(8,128)(2,1)S(1)} collective-permute-done((bf16[16,128,128]{2,1,0:T(8,128)(2,1)S(1)}, bf16[16,128,128]{2,1,0:T(8,128)(2,1)S(1)}, u32[]{:S(2)}, u32[]{:S(2)}) %collective-permute-start.3) | collective-permute-done | bytes 524320 | tf_op jit(solution)/shard_map/ppermute | solution.py:18
  55.7 1.1 pad_maximum_fusion.2.v_ref
  56.7 0.0 copy-done.1
  56.7 4.6 %collective-permute-done.2 = bf16[16,128,128]{2,1,0:T(8,128)(2,1)S(1)} collective-permute-done((bf16[16,128,128]{2,1,0:T(8,128)(2,1)S(1)}, bf16[16,128,128]{2,1,0:T(8,128)(2,1)S(1)}, u32[]{:S(2)}, u32[]{:S(2)}) %collective-permute-start.2) | collective-permute-done | bytes 524320 | tf_op jit(solution)/shard_map/ppermute | solution.py:18
  61.3 1.1 pad_maximum_fusion.1.k_ref
  62.4 19.6 %shard_map.76 = bf16[16,128,256]{2,1,0:T(8,128)(2,1)} custom-call(bf16[16,128,256]{2,1,0:T(8,128)(2,1)} %slice.32.q_ref, bf16[16,256,128]{2,1,0:T(8,128)(2,1)} %pad_maximum_fusion.1.k_ref, bf16[16,256,128]{2,1,0:T(8,128)(2,1)} %pad_maximum_fusion.2.v_ref, bf16[128,256]{1,0:T(8,128)(2,1)} %fusion.5.g0_ref, s32[128,256]{1,0:T(8,128)} %dynamic-slice_bitcast_fusion.m_ref), custom_call_target="tpu_custom_call" | custom-call | tf_op jit(solution)/shard_map/pallas_call | solution.py:60
  82.0 0.0 slice-start
  82.0 1.2 slice-done
  83.2 0.0 copy-start.5
  83.2 0.0 copy-start.7
  83.2 1.1 pad_maximum_fusion.3
  84.2 3.7 %all-to-all-start.1 = ((bf16[16,128,256]{2,1,0:T(8,128)(2,1)}), bf16[16,128,256]{2,1,0:T(8,128)(2,1)S(1)}, u32[]{:S(2)}, u32[]{:S(2)}) async-start(bf16[16,128,256]{2,1,0:T(8,128)(2,1)} %pad_maximum_fusion.3), calls=%async_computation.1 | async-start | bytes 2097152 | tf_op jit(solution)/shard_map/all_to_all | solution.py:181
  87.9 0.0 copy-done.5
  87.9 5.6 %collective-permute-start = (bf16[2,128,512]{2,1,0:T(8,128)(2,1)S(1)}, bf16[2,128,512]{2,1,0:T(8,128)(2,1)S(1)}, u32[]{:S(2)}, u32[]{:S(2)}) collective-permute-start(bf16[2,128,512]{2,1,0:T(8,128)(2,1)S(1)} %bitcast.44), channel_id=1, source_target_pairs={{0,1},{1,2},{2,3},{3,4},{4,5},{5,6},{6,7},{7,8},{8,9},{9,10},{10,1... | collective-permute-start | bytes 786440 | tf_op jit(solution)/shard_map/ppermute | solution.py:18
  93.5 0.0 copy-done.7
  93.5 1.9 %collective-permute-start.1 = (bf16[2,128,512]{2,1,0:T(8,128)(2,1)S(1)}, bf16[2,128,512]{2,1,0:T(8,128)(2,1)S(1)}, u32[]{:S(2)}, u32[]{:S(2)}) collective-permute-start(bf16[2,128,512]{2,1,0:T(8,128)(2,1)S(1)} %bitcast.46), channel_id=1, source_target_pairs={{0,1},{1,2},{2,3},{3,4},{4,5},{5,6},{6,7},{7,8},{8,9},{9,10},{10,1... | collective-permute-start | bytes 786440 | tf_op jit(solution)/shard_map/ppermute | solution.py:18
  95.4 1.4 collective-permute-done
  96.8 0.8 pad_maximum_fusion.4.k_ref
  97.6 2.0 %collective-permute-done.1 = bf16[2,128,512]{2,1,0:T(8,128)(2,1)S(1)} collective-permute-done((bf16[2,128,512]{2,1,0:T(8,128)(2,1)S(1)}, bf16[2,128,512]{2,1,0:T(8,128)(2,1)S(1)}, u32[]{:S(2)}, u32[]{:S(2)}) %collective-permute-start.1) | collective-permute-done | bytes 262176 | tf_op jit(solution)/shard_map/ppermute | solution.py:18
  99.6 0.8 pad_maximum_fusion.5.v_ref
  100.4 7.3 %all-to-all-done.1 = bf16[16,128,256]{2,1,0:T(8,128)(2,1)S(1)} async-done(((bf16[16,128,256]{2,1,0:T(8,128)(2,1)}), bf16[16,128,256]{2,1,0:T(8,128)(2,1)S(1)}, u32[]{:S(2)}, u32[]{:S(2)}) %all-to-all-start.1) | async-done | bytes 1048608 | tf_op jit(solution)/shard_map/all_to_all | solution.py:181
  107.8 0.6 copy.14
  108.3 1.3 reshape.112.g_ref
  109.7 21.6 %shard_map.77 = (f32[2,256,512]{2,1,0:T(8,128)}, f32[2,256,512]{2,1,0:T(8,128)}, bf16[2,128,2048]{2,1,0:T(8,128)(2,1)}) custom-call(bf16[2,128,2048]{2,1,0:T(8,128)(2,1)} %bitcast.35, bf16[2,256,512]{2,1,0:T(8,128)(2,1)} %pad_maximum_fusion.4.k_ref, bf16[2,256,512]{2,1,0:T(8,128)(2,1)} %pad_maximum_fusion.5.v_ref, bf16[2,128,2048]{2,1,0:T(8,128)(2,1)} %reshape.112.g_ref, ...), custom_call_target="tpu_custom_call" | custom-call | tf_op jit(solution)/shard_map/pallas_call | solution.py:95
  131.3 0.0 copy-start.3
  131.3 0.0 copy-start.2
  131.3 1.2 slice.31
  132.5 2.5 %collective-permute-start.5 = (f32[2,128,512]{2,1,0:T(8,128)S(1)}, f32[2,128,512]{2,1,0:T(8,128)S(1)}, u32[]{:S(2)}, u32[]{:S(2)}) collective-permute-start(f32[2,128,512]{2,1,0:T(8,128)S(1)} %slice.31), channel_id=1, source_target_pairs={{1,0},{2,1},{3,2},{4,3},{5,4},{6,5},{7,6},{8,7},{9,8},{10,9},{11,1... | collective-permute-start | bytes 1572872 | tf_op jit(solution)/shard_map/ppermute | solution.py:18
  135.0 1.1 slice.29
  136.1 1.9 %collective-permute-start.4 = (f32[2,128,512]{2,1,0:T(8,128)S(1)}, f32[2,128,512]{2,1,0:T(8,128)S(1)}, u32[]{:S(2)}, u32[]{:S(2)}) collective-permute-start(f32[2,128,512]{2,1,0:T(8,128)S(1)} %slice.29), channel_id=1, source_target_pairs={{1,0},{2,1},{3,2},{4,3},{5,4},{6,5},{7,6},{8,7},{9,8},{10,9},{11,1... | collective-permute-start | bytes 1572872 | tf_op jit(solution)/shard_map/ppermute | solution.py:18
  138.0 6.2 %collective-permute-done.5 = f32[2,128,512]{2,1,0:T(8,128)S(1)} collective-permute-done((f32[2,128,512]{2,1,0:T(8,128)S(1)}, f32[2,128,512]{2,1,0:T(8,128)S(1)}, u32[]{:S(2)}, u32[]{:S(2)}) %collective-permute-start.5) | collective-permute-done | bytes 524320 | tf_op jit(solution)/shard_map/ppermute | solution.py:18
  144.2 0.0 copy-done.3
  144.2 0.8 fusion.1
  145.0 4.8 %collective-permute-done.4 = f32[2,128,512]{2,1,0:T(8,128)S(1)} collective-permute-done((f32[2,128,512]{2,1,0:T(8,128)S(1)}, f32[2,128,512]{2,1,0:T(8,128)S(1)}, u32[]{:S(2)}, u32[]{:S(2)}) %collective-permute-start.4) | collective-permute-done | bytes 524320 | tf_op jit(solution)/shard_map/ppermute | solution.py:18
  149.8 0.0 copy-done.2
  149.8 0.8 fusion
  (8 shorter events, 0.1 us)
Async XLA Ops:
  0.6 11.4 %copy-start = (bf16[2,128,2048]{2,1,0:T(8,128)(2,1)S(1)}, bf16[2,128,2048]{2,1,0:T(8,128)(2,1)}, u32[]{:S(2)}) copy-start(bf16[2,128,2048]{2,1,0:T(8,128)(2,1)} %param.8) | copy-start | bytes 3145732
  0.6 1.9 %copy-start.4 = (bf16[1,2,128,512]{3,2,1,0:T(8,128)(2,1)S(1)}, bf16[1,2,128,512]{3,2,1,0:T(8,128)(2,1)}, u32[]{:S(2)}) copy-start(bf16[1,2,128,512]{3,2,1,0:T(8,128)(2,1)} %param.6) | copy-start | bytes 786436
  2.3 1.0 copy-start.6
  5.1 37.7 %all-to-all-start = ((bf16[16,128,512]{2,1,0:T(8,128)(2,1)}), bf16[16,128,512]{2,1,0:T(8,128)(2,1)S(1)}, u32[]{:S(2)}, u32[]{:S(2)}) async-start(bf16[16,128,512]{2,1,0:T(8,128)(2,1)} %pad_maximum_fusion), calls=%async_computation | async-start | bytes 4194304 | tf_op jit(solution)/shard_map/all_to_all | solution.py:168
  11.9 37.7 %copy-start.8 = (s32[2,4096]{1,0:T(2,128)S(1)}, s32[2,4096]{1,0:T(2,128)}, u32[]{:S(2)}) copy-start(s32[2,4096]{1,0:T(2,128)} %param.9) | copy-start | bytes 98308
  43.2 12.5 %collective-permute-start.3 = (bf16[16,128,128]{2,1,0:T(8,128)(2,1)S(1)}, bf16[16,128,128]{2,1,0:T(8,128)(2,1)S(1)}, u32[]{:S(2)}, u32[]{:S(2)}) collective-permute-start(bf16[16,128,128]{2,1,0:T(8,128)(2,1)S(1)} %get-tuple-element.9), channel_id=1, source_target_pairs={{0,1},{1,2},{2,3},{3,4},{4,5},{5,6},{6,7},{7,8},{8,9},{9,10},{10,1... | collective-permute-start | bytes 1572872 | tf_op jit(solution)/shard_map/ppermute | solution.py:18
  49.6 11.7 %collective-permute-start.2 = (bf16[16,128,128]{2,1,0:T(8,128)(2,1)S(1)}, bf16[16,128,128]{2,1,0:T(8,128)(2,1)S(1)}, u32[]{:S(2)}, u32[]{:S(2)}) collective-permute-start(bf16[16,128,128]{2,1,0:T(8,128)(2,1)S(1)} %get-tuple-element.10), channel_id=1, source_target_pairs={{0,1},{1,2},{2,3},{3,4},{4,5},{5,6},{6,7},{7,8},{8,9},{9,10},{10,1... | collective-permute-start | bytes 1572872 | tf_op jit(solution)/shard_map/ppermute | solution.py:18
  51.7 5.1 %copy-start.1 = (s32[2,128,256]{2,1,0:T(8,128)}, s32[2,128,256]{2,1,0:T(8,128)S(1)}, u32[]{:S(2)}) copy-start(s32[2,128,256]{2,1,0:T(8,128)S(1)} %and_convert_fusion.m_ref) | copy-start | bytes 786436
  82.0 1.2 slice-start
  83.2 4.7 %copy-start.5 = (bf16[1,2,128,512]{3,2,1,0:T(8,128)(2,1)S(1)}, bf16[1,2,128,512]{3,2,1,0:T(8,128)(2,1)}, u32[]{:S(2)}) copy-start(bf16[1,2,128,512]{3,2,1,0:T(8,128)(2,1)} %param.6) | copy-start | bytes 786436
  83.2 10.3 %copy-start.7 = (bf16[1,2,128,512]{3,2,1,0:T(8,128)(2,1)S(1)}, bf16[1,2,128,512]{3,2,1,0:T(8,128)(2,1)}, u32[]{:S(2)}) copy-start(bf16[1,2,128,512]{3,2,1,0:T(8,128)(2,1)} %param.7) | copy-start | bytes 786436
  84.2 23.5 %all-to-all-start.1 = ((bf16[16,128,256]{2,1,0:T(8,128)(2,1)}), bf16[16,128,256]{2,1,0:T(8,128)(2,1)S(1)}, u32[]{:S(2)}, u32[]{:S(2)}) async-start(bf16[16,128,256]{2,1,0:T(8,128)(2,1)} %pad_maximum_fusion.3), calls=%async_computation.1 | async-start | bytes 2097152 | tf_op jit(solution)/shard_map/all_to_all | solution.py:181
  87.9 8.9 %collective-permute-start = (bf16[2,128,512]{2,1,0:T(8,128)(2,1)S(1)}, bf16[2,128,512]{2,1,0:T(8,128)(2,1)S(1)}, u32[]{:S(2)}, u32[]{:S(2)}) collective-permute-start(bf16[2,128,512]{2,1,0:T(8,128)(2,1)S(1)} %bitcast.44), channel_id=1, source_target_pairs={{0,1},{1,2},{2,3},{3,4},{4,5},{5,6},{6,7},{7,8},{8,9},{9,10},{10,1... | collective-permute-start | bytes 786440 | tf_op jit(solution)/shard_map/ppermute | solution.py:18
  93.5 6.1 %collective-permute-start.1 = (bf16[2,128,512]{2,1,0:T(8,128)(2,1)S(1)}, bf16[2,128,512]{2,1,0:T(8,128)(2,1)S(1)}, u32[]{:S(2)}, u32[]{:S(2)}) collective-permute-start(bf16[2,128,512]{2,1,0:T(8,128)(2,1)S(1)} %bitcast.46), channel_id=1, source_target_pairs={{0,1},{1,2},{2,3},{3,4},{4,5},{5,6},{6,7},{7,8},{8,9},{9,10},{10,1... | collective-permute-start | bytes 786440 | tf_op jit(solution)/shard_map/ppermute | solution.py:18
  131.3 13.0 %copy-start.3 = (f32[2,256,512]{2,1,0:T(8,128)S(1)}, f32[2,256,512]{2,1,0:T(8,128)}, u32[]{:S(2)}) copy-start(f32[2,256,512]{2,1,0:T(8,128)} %get-tuple-element.8) | copy-start | bytes 3145732
  131.3 18.6 %copy-start.2 = (f32[2,256,512]{2,1,0:T(8,128)S(1)}, f32[2,256,512]{2,1,0:T(8,128)}, u32[]{:S(2)}) copy-start(f32[2,256,512]{2,1,0:T(8,128)} %get-tuple-element.7) | copy-start | bytes 3145732
  132.5 11.7 %collective-permute-start.5 = (f32[2,128,512]{2,1,0:T(8,128)S(1)}, f32[2,128,512]{2,1,0:T(8,128)S(1)}, u32[]{:S(2)}, u32[]{:S(2)}) collective-permute-start(f32[2,128,512]{2,1,0:T(8,128)S(1)} %slice.31), channel_id=1, source_target_pairs={{1,0},{2,1},{3,2},{4,3},{5,4},{6,5},{7,6},{8,7},{9,8},{10,9},{11,1... | collective-permute-start | bytes 1572872 | tf_op jit(solution)/shard_map/ppermute | solution.py:18
  136.1 13.7 %collective-permute-start.4 = (f32[2,128,512]{2,1,0:T(8,128)S(1)}, f32[2,128,512]{2,1,0:T(8,128)S(1)}, u32[]{:S(2)}, u32[]{:S(2)}) collective-permute-start(f32[2,128,512]{2,1,0:T(8,128)S(1)} %slice.29), channel_id=1, source_target_pairs={{1,0},{2,1},{3,2},{4,3},{5,4},{6,5},{7,6},{8,7},{9,8},{10,9},{11,1... | collective-permute-start | bytes 1572872 | tf_op jit(solution)/shard_map/ppermute | solution.py:18

commit v3 on v2

--- a/solution.py
+++ b/solution.py
@@ -32,19 +32,24 @@
     return prob_low, grad_score
 
 
-def chain_kernel(q_ref, k_ref, v_ref, g0_ref, m_ref, o_ref):
-    layers = q_ref.shape[0]
-    heads = q_ref.shape[2] // DH
+def chain_kernel(x_ref, halo_ref, g0_ref, m_ref, o_ref):
+    layers = x_ref.shape[0]
+    width = o_ref.shape[2]
+    heads = width // DH
     allowed = m_ref[...] != 0
 
     def step(i, g):
         layer = layers - 1 - i
-        k = k_ref[layer]
-        v = v_ref[layer]
+        k = jnp.concatenate(
+            [halo_ref[layer, :, :DH], x_ref[layer, :, width:width + DH]], axis=0
+        )
+        v = jnp.concatenate(
+            [halo_ref[layer, :, DH:], x_ref[layer, :, width + DH:]], axis=0
+        )
         outs = []
         for h in range(heads):
             cols = slice(h * DH, (h + 1) * DH)
-            q = q_ref[layer, :, cols]
+            q = x_ref[layer, :, cols]
             gh = g[:, cols]
             _, grad_score = head_core(q, k, v, gh, allowed)
             dq = jnp.dot(grad_score, k, preferred_element_type=jnp.float32) * SCALE
@@ -53,22 +58,25 @@
         o_ref[layer] = g_new
         return g_new
 
-    lax.fori_loop(0, layers, step, g0_ref[...])
-
-
-def chain_call(query_t, key_t, value_t, grad_top, allowed_i32, interpret=False):
+    lax.fori_loop(0, layers, step, g0_ref[...], unroll=True)
+
+
+def chain_call(sent, halo, grad_top, allowed_i32, interpret=False):
+    layers, rows, _ = sent.shape
     return pl.pallas_call(
         chain_kernel,
-        out_shape=jax.ShapeDtypeStruct(query_t.shape, jnp.bfloat16),
+        out_shape=jax.ShapeDtypeStruct((layers, rows, grad_top.shape[1]), jnp.bfloat16),
         interpret=interpret,
-    )(query_t, key_t, value_t, grad_top, allowed_i32)
-
-
-def layer_kernel(q_ref, k_ref, v_ref, g_ref, m_ref, dk_ref, dv_ref, gl_ref):
+    )(sent, halo, grad_top, allowed_i32)
+
+
+def layer_kernel(q_ref, kh_ref, ko_ref, vh_ref, vo_ref, g_ref, m_ref,
+                 dkh_ref, dko_ref, dvh_ref, dvo_ref, gl_ref):
     heads = q_ref.shape[2] // DH
+    rows = kh_ref.shape[1]
     allowed = m_ref[0] != 0
-    k = k_ref[0]
-    v = v_ref[0]
+    k = jnp.concatenate([kh_ref[0], ko_ref[0]], axis=0)
+    v = jnp.concatenate([vh_ref[0], vo_ref[0]], axis=0)
     dk = None
     dv = None
     for h in range(heads):
@@ -82,38 +90,32 @@
         dv_h = lax.dot_general(prob_low, g, TN, preferred_element_type=jnp.float32)
         dk = dk_h if dk is None else dk + dk_h
         dv = dv_h if dv is None else dv + dv_h
-    dk_ref[0] = dk * SCALE
-    dv_ref[0] = dv
-
-
-def layer_call(query, key_rows, value_rows, grad_in, allowed_i32, interpret=False):
+    dk = dk * SCALE
+    dkh_ref[0] = dk[:rows]
+    dko_ref[0] = dk[rows:]
+    dvh_ref[0] = dv[:rows]
+    dvo_ref[0] = dv[rows:]
+
+
+def layer_call(query, key_halo, key_own, value_halo, value_own, grad_in, allowed_i32,
+               interpret=False):
     micro, rows, width = query.shape
-    keys2 = key_rows.shape[1]
-    kv_heads = key_rows.shape[2] // DH
+    kv_heads = key_own.shape[2] // DH
     group = width // (kv_heads * DH)
     gw = group * DH
+    kv_spec = pl.BlockSpec((1, rows, DH), lambda m, g: (m, 0, g))
+    q_spec = pl.BlockSpec((1, rows, gw), lambda m, g: (m, 0, g))
+    kv_shape = jax.ShapeDtypeStruct(key_own.shape, jnp.float32)
     return pl.pallas_call(
         layer_kernel,
         grid=(micro, kv_heads),
-        in_specs=[
-            pl.BlockSpec((1, rows, gw), lambda m, g: (m, 0, g)),
-            pl.BlockSpec((1, keys2, DH), lambda m, g: (m, 0, g)),
-            pl.BlockSpec((1, keys2, DH), lambda m, g: (m, 0, g)),
-            pl.BlockSpec((1, rows, gw), lambda m, g: (m, 0, g)),
-            pl.BlockSpec((1, rows, keys2), lambda m, g: (m, 0, 0)),
-        ],
-        out_specs=[
-            pl.BlockSpec((1, keys2, DH), lambda m, g: (m, 0, g)),
-            pl.BlockSpec((1, keys2, DH), lambda m, g: (m, 0, g)),
-            pl.BlockSpec((1, rows, gw), lambda m, g: (m, 0, g)),
-        ],
-        out_shape=[
-            jax.ShapeDtypeStruct(key_rows.shape, jnp.float32),
-            jax.ShapeDtypeStruct(key_rows.shape, jnp.float32),
-            jax.ShapeDtypeStruct(query.shape, jnp.bfloat16),
-        ],
+        in_specs=[q_spec, kv_spec, kv_spec, kv_spec, kv_spec, q_spec,
+                  pl.BlockSpec((1, rows, 2 * rows), lambda m, g: (m, 0, 0))],
+        out_specs=[kv_spec, kv_spec, kv_spec, kv_spec, q_spec],
+        out_shape=[kv_shape, kv_shape, kv_shape, kv_shape,
+                   jax.ShapeDtypeStruct(query.shape, jnp.bfloat16)],
         interpret=interpret,
-    )(query, key_rows, value_rows, grad_in, allowed_i32)
+    )(query, key_halo, key_own, value_halo, value_own, grad_in, allowed_i32)
 
 
 def per_device(queries, keys, values, out_grad, segments):
@@ -150,8 +152,6 @@
     )
     masks = (near[None] & (seg_query[:, :, None] == seg_key[:, None, :])).astype(jnp.int32)
     halo_key, halo_value = from_behind((own_key, own_value), "seq", 1)
-    key_rows = jnp.concatenate([halo_key, own_key], axis=1)
-    value_rows = jnp.concatenate([halo_value, own_value], axis=1)
 
     my_block = section_index // micro_count
     my_micro = section_index % micro_count
@@ -166,29 +166,25 @@
         )
         kv_send.append(split.reshape(section_count, row_count, DH))
     sent = lax.all_to_all(jnp.concatenate([query_send] + kv_send, axis=-1), "pipe", 0, 0)
-    query_t = sent[..., :block_width]
-    key_own_t = sent[..., block_width:block_width + DH]
-    value_own_t = sent[..., block_width + DH:]
-    key_halo_t, value_halo_t = from_behind((key_own_t, value_own_t), "seq", 1)
-    key_t = jnp.concatenate([key_halo_t, key_own_t], axis=1)
-    value_t = jnp.concatenate([value_halo_t, value_own_t], axis=1)
+    sent, halo_key, halo_value = lax.optimization_barrier((sent, halo_key, halo_value))
+    halo_t = from_behind(sent[..., block_width:], "seq", 1)
     grad_top = lax.dynamic_slice(
         out_grad, (my_micro, 0, my_block * block_width), (1, row_count, block_width)
     )[0]
     allowed = lax.dynamic_index_in_dim(masks, my_micro, 0, keepdims=False)
-    grads = chain_call(query_t, key_t, value_t, grad_top, allowed)
+    grads = chain_call(sent, halo_t, grad_top, allowed)
     grads_above = jnp.concatenate([grads[1:], grad_top[None]], axis=0)
     back = lax.all_to_all(grads_above, "pipe", 0, 0)
     grad_in = jnp.transpose(
         back.reshape(head_blocks, micro_count, row_count, block_width), (1, 2, 0, 3)
     ).reshape(micro_count, row_count, query_width)
 
-    key_all, value_all, query_all = layer_call(own_query, key_rows, value_rows, grad_in, masks)
-    back_key, back_value = from_behind(
-        (key_all[:, :row_count], value_all[:, :row_count]), "seq", -1
-    )
-    key_grads = (key_all[:, row_count:] + back_key).astype(jnp.bfloat16)
-    value_grads = (value_all[:, row_count:] + back_value).astype(jnp.bfloat16)
+    key_back, key_own_grad, value_back, value_own_grad, query_all = layer_call(
+        own_query, halo_key, own_key, halo_value, own_value, grad_in, masks
+    )
+    back_key, back_value = from_behind((key_back, value_back), "seq", -1)
+    key_grads = (key_own_grad + back_key).astype(jnp.bfloat16)
+    value_grads = (value_own_grad + back_value).astype(jnp.bfloat16)
     return (query_all[None], key_grads[None], value_grads[None])
 
 

time: 151 us -> 139 us (0.921)
  blocking collectives: 0 us -> 20 us
  waiting for transfers between devices: 58.5 us -> 44.4 us
  Pallas kernels: 41.2 us -> 33.3 us
  starting transfers between devices: 30.7 us -> 25.7 us
  other arithmetic: 8.22 us -> 5.51 us
  local copies, waits for them, and re-layouts: 11 us -> 8.87 us
    all_to_all x0 -> x1, blocking collectives: none -> 20 us  [per_device(): back = lax.all_to_all(grads_above, 'pipe', 0, 0)]
    all_to_all x1, waiting for transfers between devices: 30.1 us -> 19.1 us  [per_device(): lax.all_to_all(jnp.concatenate([query_send] + kv_send, axis=-1), 'pipe',...]
    pallas_call x2, Pallas kernels: 41.2 us -> 33.3 us  [the longest x1 21.7 us: layer_call(): pl.pallas_call(layer_kernel, grid=(micro, kv_heads), in_specs=[q_spec, kv...]
    all_to_all x1 -> x0, waiting for transfers between devices: 7.32 us -> none  [per_device(): back = lax.all_to_all(grads_above, 'pipe', 0, 0)]
    ppermute x6 -> x5, waiting for transfers between devices: 21.1 us -> 25.3 us  [from_behind(): return lax.ppermute(block, axis, route)]
    concatenate x4 -> x0, other arithmetic: 3.81 us -> none  [the longest x1 1.09 us: per_device(): key_t = jnp.concatenate([key_halo_t, key_own_t], axis=1)]
    all_to_all x1 -> x0, starting transfers between devices: 3.66 us -> none  [per_device(): back = lax.all_to_all(grads_above, 'pipe', 0, 0)]
    slice x4 -> x1, local copies, waits for them, and re-layouts: 3.64 us -> 1.12 us  [per_device(): halo_t = from_behind(sent[..., block_width:], 'seq', 1)]
  transfers between devices with their start and end apart: 8 -> 6, of which waited for: 8 -> 6; matrix products, arithmetic and copies ran while one was open for 5% -> 2% of each run, Pallas kernels for 0% -> 0%
where the time goes in v3:
time: 139 us
  waiting for transfers between devices  44.4 us (32%)
  Pallas kernels  33.3 us (24%)
  starting transfers between devices  25.7 us (18%)
  blocking collectives  20 us (14%)
  local copies, waits for them, and re-layouts  8.87 us (6%)
  other arithmetic  5.51 us (4%)
    ppermute x5, waiting for transfers between devices, from_behind(): return lax.ppermute(block, axis, route)  25.3 us
    pallas_call x1, Pallas kernels, layer_call(): pl.pallas_call(layer_kernel, grid=(micro, kv_heads), in_specs=[q_spec, kv...  21.7 us
    all_to_all x1, blocking collectives, per_device(): back = lax.all_to_all(grads_above, 'pipe', 0, 0)  20 us
    all_to_all x1, waiting for transfers between devices, per_device(): lax.all_to_all(jnp.concatenate([query_send] + kv_send, axis=-1), 'pipe',...  19.1 us
    ppermute x5, starting transfers between devices, from_behind(): return lax.ppermute(block, axis, route)  18.9 us
    pallas_call x1, Pallas kernels, chain_call(): pl.pallas_call(chain_kernel, out_shape=jax.ShapeDtypeStruct((layers, rows...  11.6 us
    all_to_all x1, starting transfers between devices, per_device(): lax.all_to_all(jnp.concatenate([query_send] + kv_send, axis=-1), 'pipe',...  6.75 us
    broadcast_in_dim x2, other arithmetic, per_device(): return (query_all[None], key_grads[None], value_grads[None])  3.63 us
  transfers between devices with their start and end apart: 6, of which 6 were waited for; matrix products, arithmetic and copies ran while one was open for 2% of the time, Pallas kernels for 0%

profile of v3, /device:TPU:97, one launch (start us, length us, event | category | flops | bytes accessed | tf_op | source)
XLA Modules:
  0.0 138.7 jit_solution(3152775478783278182)
XLA Ops:
  0.6 0.0 copy-start
  0.6 0.0 copy-start.3
  0.7 1.6 %copy.12 = bf16[32,8,8,256]{3,2,1,0:T(8,128)(2,1)S(1)} copy(bf16[32,8,8,256]{3,1,2,0:T(8,128)(2,1)} %bitcast.34) | data formatting | bytes 2097152
  2.3 0.2 copy.8
  2.5 0.0 copy-done.3
  2.5 0.1 reshape_squeeze.10
  2.6 1.0 reshape_squeeze.11
  3.7 0.1 broadcast_in_dim.10
  3.8 0.1 broadcast_in_dim.11
  3.9 1.6 %pad_maximum_fusion = bf16[16,128,512]{2,1,0:T(8,128)(2,1)} fusion(bf16[16,128,128]{2,1,0:T(8,128)(2,1)S(1)} %bitcast.41, bf16[16,128,128]{2,1,0:T(8,128)(2,1)S(1)} %bitcast.40, bf16[16,128,256]{2,1,0:T(8,128)(2,1)S(1)} %bitcast.39), kind=kLoop, calls=%fused_computation | loop fusion | flops 6291456 | bytes 4194304 | tf_op jit(solution)/shard_map/concatenate | solution.py:168
  5.5 6.8 %all-to-all-start = ((bf16[16,128,512]{2,1,0:T(8,128)(2,1)}), bf16[16,128,512]{2,1,0:T(8,128)(2,1)S(1)}, u32[]{:S(2)}, u32[]{:S(2)}) async-start(bf16[16,128,512]{2,1,0:T(8,128)(2,1)} %pad_maximum_fusion), calls=%async_computation | async-start | bytes 4194304 | tf_op jit(solution)/shard_map/all_to_all | solution.py:168
  12.3 0.0 copy-start.4
  12.3 5.6 %collective-permute-start = (bf16[2,128,512]{2,1,0:T(8,128)(2,1)S(1)}, bf16[2,128,512]{2,1,0:T(8,128)(2,1)}, u32[]{:S(2)}, u32[]{:S(2)}) collective-permute-start(bf16[2,128,512]{2,1,0:T(8,128)(2,1)S(1)} %bitcast.45), channel_id=1, source_target_pairs={{0,1},{1,2},{2,3},{3,4},{4,5},{5,6},{6,7},{7,8},{8,9},{9,10},{10,1... | collective-permute-start | bytes 786440 | tf_op jit(solution)/shard_map/ppermute | solution.py:18
  17.9 1.9 %collective-permute-start.1 = (bf16[2,128,512]{2,1,0:T(8,128)(2,1)}, bf16[2,128,512]{2,1,0:T(8,128)(2,1)}, u32[]{:S(2)}, u32[]{:S(2)}) collective-permute-start(bf16[2,128,512]{2,1,0:T(8,128)(2,1)} %bitcast.46), channel_id=1, source_target_pairs={{0,1},{1,2},{2,3},{3,4},{4,5},{5,6},{6,7},{7,8},{8,9},{9,10},{10,1... | collective-permute-start | bytes 786440 | tf_op jit(solution)/shard_map/ppermute | solution.py:18
  19.8 1.3 collective-permute-done.kh_ref
  21.2 2.9 %collective-permute-done.1.vh_ref = bf16[2,128,512]{2,1,0:T(8,128)(2,1)} collective-permute-done((bf16[2,128,512]{2,1,0:T(8,128)(2,1)}, bf16[2,128,512]{2,1,0:T(8,128)(2,1)}, u32[]{:S(2)}, u32[]{:S(2)}) %collective-permute-start.1) | collective-permute-done | bytes 262176 | tf_op jit(solution)/shard_map/ppermute | solution.py:18
  24.1 19.1 %all-to-all-done.x_ref = bf16[16,128,512]{2,1,0:T(8,128)(2,1)S(1)} async-done(((bf16[16,128,512]{2,1,0:T(8,128)(2,1)}), bf16[16,128,512]{2,1,0:T(8,128)(2,1)S(1)}, u32[]{:S(2)}, u32[]{:S(2)}) %all-to-all-start) | async-done | bytes 2097184 | tf_op jit(solution)/shard_map/all_to_all | solution.py:168
  43.2 0.0 copy-start.1
  43.2 1.1 slice.6
  44.3 6.4 %collective-permute-start.2 = (bf16[16,128,256]{2,1,0:T(8,128)(2,1)}, bf16[16,128,256]{2,1,0:T(8,128)(2,1)}, u32[]{:S(2)}, u32[]{:S(2)}) collective-permute-start(bf16[16,128,256]{2,1,0:T(8,128)(2,1)} %slice.6), channel_id=1, source_target_pairs={{0,1},{1,2},{2,3},{3,4},{4,5},{5,6},{6,7},{7,8},{8,9},{9,10},{10,1... | collective-permute-start | bytes 3145736 | tf_op jit(solution)/shard_map/ppermute | solution.py:18
  50.8 0.0 copy-done.4
  50.8 0.0 copy-done
  50.8 0.6 fusion.4.g0_ref
  51.5 0.1 fusion.3
  51.6 0.1 and_convert_fusion.m_ref
  51.7 0.0 copy-start.2
  51.7 0.7 dynamic-slice_bitcast_fusion.m_ref
  52.5 10.3 %collective-permute-done.2.halo_ref = bf16[16,128,256]{2,1,0:T(8,128)(2,1)} collective-permute-done((bf16[16,128,256]{2,1,0:T(8,128)(2,1)}, bf16[16,128,256]{2,1,0:T(8,128)(2,1)}, u32[]{:S(2)}, u32[]{:S(2)}) %collective-permute-start.2) | collective-permute-done | bytes 1048608 | tf_op jit(solution)/shard_map/ppermute | solution.py:18
  62.8 0.0 copy-done.1
  62.8 11.6 %shard_map.76 = bf16[16,128,256]{2,1,0:T(8,128)(2,1)} custom-call(bf16[16,128,512]{2,1,0:T(8,128)(2,1)} %copy-done.1, bf16[16,128,256]{2,1,0:T(8,128)(2,1)} %collective-permute-done.2.halo_ref, bf16[128,256]{1,0:T(8,128)(2,1)} %fusion.4.g0_ref, s32[128,256]{1,0:T(8,128)} %dynamic-slice_bitcast_fusion.m_ref), custom_call_target="tpu_custom_call" | custom-call | tf_op jit(solution)/shard_map/pallas_call | solution.py:66
  74.4 0.0 copy-done.2
  74.4 0.0 slice-start
  74.4 1.2 slice-done
  75.6 0.1 pad_maximum_fusion.1
  75.7 20.0 %all_to_all.10 = bf16[16,128,256]{2,1,0:T(8,128)(2,1)S(1)} all-to-all(bf16[16,128,256]{2,1,0:T(8,128)(2,1)S(1)} %pad_maximum_fusion.1), channel_id=1, replica_groups=mesh['pipe'=16,'seq'=32] {'pipe'}, dimensions={0} | all-to-all | bytes 2097152 | tf_op jit(solution)/shard_map/all_to_all | solution.py:177
  95.7 0.6 copy.14
  96.3 1.3 reshape.112.g_ref
  97.6 21.7 %shard_map.77 = (f32[2,128,512]{2,1,0:T(8,128)}, f32[2,128,512]{2,1,0:T(8,128)}, f32[2,128,512]{2,1,0:T(8,128)}, f32[2,128,512]{2,1,0:T(8,128)}, bf16[2,128,2048]{2,1,0:T(8,128)(2,1)}) custom-call(bf16[2,128,2048]{2,1,0:T(8,128)(2,1)} %bitcast.35, bf16[2,128,512]{2,1,0:T(8,128)(2,1)} %collective-permute-done.kh_ref, bf16[2,128,512]{2,1,0:T(8,128)(2,1)} %bitcast.44, ...), custom_call_target="tpu_custom_call" | custom-call | tf_op jit(solution)/shard_map/pallas_call | solution.py:109
  119.3 3.1 %collective-permute-start.4 = (f32[2,128,512]{2,1,0:T(8,128)}, f32[2,128,512]{2,1,0:T(8,128)S(1)}, u32[]{:S(2)}, u32[]{:S(2)}) collective-permute-start(f32[2,128,512]{2,1,0:T(8,128)} %get-tuple-element.18), channel_id=1, source_target_pairs={{1,0},{2,1},{3,2},{4,3},{5,4},{6,5},{7,6},{8,7},{9,8},{10,9},{11,1... | collective-permute-start | bytes 1572872 | tf_op jit(solution)/shard_map/ppermute | solution.py:18
  122.4 1.9 %collective-permute-start.3 = (f32[2,128,512]{2,1,0:T(8,128)}, f32[2,128,512]{2,1,0:T(8,128)S(1)}, u32[]{:S(2)}, u32[]{:S(2)}) collective-permute-start(f32[2,128,512]{2,1,0:T(8,128)} %get-tuple-element.16), channel_id=1, source_target_pairs={{1,0},{2,1},{3,2},{4,3},{5,4},{6,5},{7,6},{8,7},{9,8},{10,9},{11,1... | collective-permute-start | bytes 1572872 | tf_op jit(solution)/shard_map/ppermute | solution.py:18
  124.3 7.0 %collective-permute-done.4 = f32[2,128,512]{2,1,0:T(8,128)S(1)} collective-permute-done((f32[2,128,512]{2,1,0:T(8,128)}, f32[2,128,512]{2,1,0:T(8,128)S(1)}, u32[]{:S(2)}, u32[]{:S(2)}) %collective-permute-start.4) | collective-permute-done | bytes 524320 | tf_op jit(solution)/shard_map/ppermute | solution.py:18
  131.3 1.8 %fusion.1 = bf16[1,2,128,512]{3,2,1,0:T(8,128)(2,1)} fusion(f32[2,128,512]{2,1,0:T(8,128)} %get-tuple-element.17, f32[2,128,512]{2,1,0:T(8,128)S(1)} %collective-permute-done.4), kind=kLoop, calls=%fused_computation.6 | loop fusion | flops 262144 | bytes 1310720 | tf_op jit(solution)/shard_map/broadcast_in_dim | solution.py:188
  133.1 3.8 %collective-permute-done.3 = f32[2,128,512]{2,1,0:T(8,128)S(1)} collective-permute-done((f32[2,128,512]{2,1,0:T(8,128)}, f32[2,128,512]{2,1,0:T(8,128)S(1)}, u32[]{:S(2)}, u32[]{:S(2)}) %collective-permute-start.3) | collective-permute-done | bytes 524320 | tf_op jit(solution)/shard_map/ppermute | solution.py:18
  136.9 1.8 %fusion = bf16[1,2,128,512]{3,2,1,0:T(8,128)(2,1)} fusion(f32[2,128,512]{2,1,0:T(8,128)} %get-tuple-element.15, f32[2,128,512]{2,1,0:T(8,128)S(1)} %collective-permute-done.3), kind=kLoop, calls=%fused_computation.5 | loop fusion | flops 262144 | bytes 1310720 | tf_op jit(solution)/shard_map/broadcast_in_dim | solution.py:188
  (8 shorter events, 0.1 us)
Async XLA Ops:
  0.6 50.2 %copy-start = (bf16[2,128,2048]{2,1,0:T(8,128)(2,1)S(1)}, bf16[2,128,2048]{2,1,0:T(8,128)(2,1)}, u32[]{:S(2)}) copy-start(bf16[2,128,2048]{2,1,0:T(8,128)(2,1)} %param.8) | copy-start | bytes 3145732
  0.6 1.9 %copy-start.3 = (bf16[1,2,128,512]{3,2,1,0:T(8,128)(2,1)S(1)}, bf16[1,2,128,512]{3,2,1,0:T(8,128)(2,1)}, u32[]{:S(2)}) copy-start(bf16[1,2,128,512]{3,2,1,0:T(8,128)(2,1)} %param.6) | copy-start | bytes 786436
  5.5 37.7 %all-to-all-start = ((bf16[16,128,512]{2,1,0:T(8,128)(2,1)}), bf16[16,128,512]{2,1,0:T(8,128)(2,1)S(1)}, u32[]{:S(2)}, u32[]{:S(2)}) async-start(bf16[16,128,512]{2,1,0:T(8,128)(2,1)} %pad_maximum_fusion), calls=%async_computation | async-start | bytes 4194304 | tf_op jit(solution)/shard_map/all_to_all | solution.py:168
  12.3 38.5 %copy-start.4 = (s32[2,4096]{1,0:T(2,128)S(1)}, s32[2,4096]{1,0:T(2,128)}, u32[]{:S(2)}) copy-start(s32[2,4096]{1,0:T(2,128)} %param.9) | copy-start | bytes 98308
  12.3 8.9 %collective-permute-start = (bf16[2,128,512]{2,1,0:T(8,128)(2,1)S(1)}, bf16[2,128,512]{2,1,0:T(8,128)(2,1)}, u32[]{:S(2)}, u32[]{:S(2)}) collective-permute-start(bf16[2,128,512]{2,1,0:T(8,128)(2,1)S(1)} %bitcast.45), channel_id=1, source_target_pairs={{0,1},{1,2},{2,3},{3,4},{4,5},{5,6},{6,7},{7,8},{8,9},{9,10},{10,1... | collective-permute-start | bytes 786440 | tf_op jit(solution)/shard_map/ppermute | solution.py:18
  17.9 6.2 %collective-permute-start.1 = (bf16[2,128,512]{2,1,0:T(8,128)(2,1)}, bf16[2,128,512]{2,1,0:T(8,128)(2,1)}, u32[]{:S(2)}, u32[]{:S(2)}) collective-permute-start(bf16[2,128,512]{2,1,0:T(8,128)(2,1)} %bitcast.46), channel_id=1, source_target_pairs={{0,1},{1,2},{2,3},{3,4},{4,5},{5,6},{6,7},{7,8},{8,9},{9,10},{10,1... | collective-permute-start | bytes 786440 | tf_op jit(solution)/shard_map/ppermute | solution.py:18
  43.2 19.6 %copy-start.1 = (bf16[16,128,512]{2,1,0:T(8,128)(2,1)}, bf16[16,128,512]{2,1,0:T(8,128)(2,1)S(1)}, u32[]{:S(2)}) copy-start(bf16[16,128,512]{2,1,0:T(8,128)(2,1)S(1)} %all-to-all-done.x_ref) | copy-start | bytes 6291460
  44.3 18.4 %collective-permute-start.2 = (bf16[16,128,256]{2,1,0:T(8,128)(2,1)}, bf16[16,128,256]{2,1,0:T(8,128)(2,1)}, u32[]{:S(2)}, u32[]{:S(2)}) collective-permute-start(bf16[16,128,256]{2,1,0:T(8,128)(2,1)} %slice.6), channel_id=1, source_target_pairs={{0,1},{1,2},{2,3},{3,4},{4,5},{5,6},{6,7},{7,8},{8,9},{9,10},{10,1... | collective-permute-start | bytes 3145736 | tf_op jit(solution)/shard_map/ppermute | solution.py:18
  51.7 22.7 %copy-start.2 = (s32[2,128,256]{2,1,0:T(8,128)}, s32[2,128,256]{2,1,0:T(8,128)S(1)}, u32[]{:S(2)}) copy-start(s32[2,128,256]{2,1,0:T(8,128)S(1)} %and_convert_fusion.m_ref) | copy-start | bytes 786436
  74.4 1.2 slice-start
  119.3 12.0 %collective-permute-start.4 = (f32[2,128,512]{2,1,0:T(8,128)}, f32[2,128,512]{2,1,0:T(8,128)S(1)}, u32[]{:S(2)}, u32[]{:S(2)}) collective-permute-start(f32[2,128,512]{2,1,0:T(8,128)} %get-tuple-element.18), channel_id=1, source_target_pairs={{1,0},{2,1},{3,2},{4,3},{5,4},{6,5},{7,6},{8,7},{9,8},{10,9},{11,1... | collective-permute-start | bytes 1572872 | tf_op jit(solution)/shard_map/ppermute | solution.py:18
  122.4 14.5 %collective-permute-start.3 = (f32[2,128,512]{2,1,0:T(8,128)}, f32[2,128,512]{2,1,0:T(8,128)S(1)}, u32[]{:S(2)}, u32[]{:S(2)}) collective-permute-start(f32[2,128,512]{2,1,0:T(8,128)} %get-tuple-element.16), channel_id=1, source_target_pairs={{1,0},{2,1},{3,2},{4,3},{5,4},{6,5},{7,6},{8,7},{9,8},{10,9},{11,1... | collective-permute-start | bytes 1572872 | tf_op jit(solution)/shard_map/ppermute | solution.py:18

commit v4 on v3

--- a/solution.py
+++ b/solution.py
@@ -1,9 +1,11 @@
+import functools
+
 import jax
 import jax.numpy as jnp
 from jax import lax
 from jax.experimental import pallas as pl
-from jax.experimental.pallas import tpu as pltpu
 from jax.sharding import PartitionSpec as P
+
 
 DH = 128
 WINDOW = 128
@@ -32,19 +34,20 @@
     return prob_low, grad_score
 
 
-def chain_kernel(x_ref, halo_ref, g0_ref, m_ref, o_ref):
-    layers = x_ref.shape[0]
+def chain_kernel(x_ref, halo_ref, g0_ref, m_ref, o_ref, g_out_ref, *, first):
+    layers = halo_ref.shape[0]
     width = o_ref.shape[2]
     heads = width // DH
     allowed = m_ref[...] != 0
 
     def step(i, g):
-        layer = layers - 1 - i
+        local = layers - 1 - i
+        layer = first + local
         k = jnp.concatenate(
-            [halo_ref[layer, :, :DH], x_ref[layer, :, width:width + DH]], axis=0
+            [halo_ref[local, :, :DH], x_ref[layer, :, width:width + DH]], axis=0
         )
         v = jnp.concatenate(
-            [halo_ref[layer, :, DH:], x_ref[layer, :, width + DH:]], axis=0
+            [halo_ref[local, :, DH:], x_ref[layer, :, width + DH:]], axis=0
         )
         outs = []
         for h in range(heads):
@@ -55,17 +58,21 @@
             dq = jnp.dot(grad_score, k, preferred_element_type=jnp.float32) * SCALE
             outs.append((gh.astype(jnp.float32) + dq).astype(jnp.bfloat16))
         g_new = jnp.concatenate(outs, axis=-1) if heads > 1 else outs[0]
-        o_ref[layer] = g_new
+        o_ref[local] = g_new
         return g_new
 
-    lax.fori_loop(0, layers, step, g0_ref[...], unroll=True)
-
-
-def chain_call(sent, halo, grad_top, allowed_i32, interpret=False):
-    layers, rows, _ = sent.shape
+    g_out_ref[...] = lax.fori_loop(0, layers, step, g0_ref[...], unroll=True)
+
+
+def chain_call(sent, halo, grad_top, allowed_i32, first, interpret=False):
+    layers, rows, _ = halo.shape
+    width = grad_top.shape[1]
     return pl.pallas_call(
-        chain_kernel,
-        out_shape=jax.ShapeDtypeStruct((layers, rows, grad_top.shape[1]), jnp.bfloat16),
+        functools.partial(chain_kernel, first=first),
+        out_shape=(
+            jax.ShapeDtypeStruct((layers, rows, width), jnp.bfloat16),
+            jax.ShapeDtypeStruct((rows, width), jnp.bfloat16),
+        ),
         interpret=interpret,
     )(sent, halo, grad_top, allowed_i32)
 
@@ -97,28 +104,30 @@
     dvo_ref[0] = dv[rows:]
 
 
-def layer_call(query, key_halo, key_own, value_halo, value_own, grad_in, allowed_i32,
+def layer_call(query, key_halo, key_own, value_halo, value_own, grad_in, allowed_i32, micro,
                interpret=False):
-    micro, rows, width = query.shape
+    _, rows, width = query.shape
     kv_heads = key_own.shape[2] // DH
     group = width // (kv_heads * DH)
     gw = group * DH
-    kv_spec = pl.BlockSpec((1, rows, DH), lambda m, g: (m, 0, g))
-    q_spec = pl.BlockSpec((1, rows, gw), lambda m, g: (m, 0, g))
-    kv_shape = jax.ShapeDtypeStruct(key_own.shape, jnp.float32)
+    kv_spec = pl.BlockSpec((1, rows, DH), lambda m, g: (micro, 0, g))
+    q_spec = pl.BlockSpec((1, rows, gw), lambda m, g: (micro, 0, g))
+    kv_out = pl.BlockSpec((1, rows, DH), lambda m, g: (0, 0, g))
+    q_out = pl.BlockSpec((1, rows, gw), lambda m, g: (0, 0, g))
+    kv_shape = jax.ShapeDtypeStruct((1, rows, key_own.shape[2]), jnp.float32)
     return pl.pallas_call(
         layer_kernel,
-        grid=(micro, kv_heads),
+        grid=(1, kv_heads),
         in_specs=[q_spec, kv_spec, kv_spec, kv_spec, kv_spec, q_spec,
-                  pl.BlockSpec((1, rows, 2 * rows), lambda m, g: (m, 0, 0))],
-        out_specs=[kv_spec, kv_spec, kv_spec, kv_spec, q_spec],
+                  pl.BlockSpec((1, rows, 2 * rows), lambda m, g: (micro, 0, 0))],
+        out_specs=[kv_out, kv_out, kv_out, kv_out, q_out],
         out_shape=[kv_shape, kv_shape, kv_shape, kv_shape,
-                   jax.ShapeDtypeStruct(query.shape, jnp.bfloat16)],
+                   jax.ShapeDtypeStruct((1, rows, width), jnp.bfloat16)],
         interpret=interpret,
     )(query, key_halo, key_own, value_halo, value_own, grad_in, allowed_i32)
 
 
-def per_device(queries, keys, values, out_grad, segments):
+def device_body(queries, keys, values, out_grad, segments):
     micro_count = queries.shape[1]
     row_count = queries.shape[2]
     query_width = queries.shape[3]
@@ -167,24 +176,37 @@
         kv_send.append(split.reshape(section_count, row_count, DH))
     sent = lax.all_to_all(jnp.concatenate([query_send] + kv_send, axis=-1), "pipe", 0, 0)
     sent, halo_key, halo_value = lax.optimization_barrier((sent, halo_key, halo_value))
-    halo_t = from_behind(sent[..., block_width:], "seq", 1)
+    split_at = section_count // 2
+    halo_hi = from_behind(sent[split_at:, :, block_width:], "seq", 1)
+    halo_lo = from_behind(sent[:split_at, :, block_width:], "seq", 1)
     grad_top = lax.dynamic_slice(
         out_grad, (my_micro, 0, my_block * block_width), (1, row_count, block_width)
     )[0]
     allowed = lax.dynamic_index_in_dim(masks, my_micro, 0, keepdims=False)
-    grads = chain_call(sent, halo_t, grad_top, allowed)
-    grads_above = jnp.concatenate([grads[1:], grad_top[None]], axis=0)
+    grads_hi, grad_mid = chain_call(sent, halo_hi, grad_top, allowed, split_at)
+    grads_lo, _ = chain_call(sent, halo_lo, grad_mid, allowed, 0)
+    grads_above = jnp.concatenate([grads_lo[1:], grads_hi, grad_top[None]], axis=0)
     back = lax.all_to_all(grads_above, "pipe", 0, 0)
     grad_in = jnp.transpose(
         back.reshape(head_blocks, micro_count, row_count, block_width), (1, 2, 0, 3)
     ).reshape(micro_count, row_count, query_width)
 
-    key_back, key_own_grad, value_back, value_own_grad, query_all = layer_call(
-        own_query, halo_key, own_key, halo_value, own_value, grad_in, masks
-    )
-    back_key, back_value = from_behind((key_back, value_back), "seq", -1)
-    key_grads = (key_own_grad + back_key).astype(jnp.bfloat16)
-    value_grads = (value_own_grad + back_value).astype(jnp.bfloat16)
+    query_parts = []
+    key_parts = []
+    value_parts = []
+    for micro in range(micro_count):
+        key_back, key_own_grad, value_back, value_own_grad, query_part = layer_call(
+            own_query, halo_key, own_key, halo_value, own_value, grad_in, masks, micro
+        )
+        back_key, back_value = from_behind(
+            (key_back.astype(jnp.bfloat16), value_back.astype(jnp.bfloat16)), "seq", -1
+        )
+        key_parts.append(key_own_grad + back_key.astype(jnp.float32))
+        value_parts.append(value_own_grad + back_value.astype(jnp.float32))
+        query_parts.append(query_part)
+    query_all = jnp.concatenate(query_parts, axis=0)
+    key_grads = jnp.concatenate(key_parts, axis=0).astype(jnp.bfloat16)
+    value_grads = jnp.concatenate(value_parts, axis=0).astype(jnp.bfloat16)
     return (query_all[None], key_grads[None], value_grads[None])
 
 
@@ -197,7 +219,7 @@
         P(),
     )
     return jax.shard_map(
-        per_device,
+        device_body,
         mesh=mesh,
         in_specs=placed,
         out_specs=(

time: 139 us -> 136 us (0.978)
  waiting for transfers between devices: 44.4 us -> 28.4 us
  starting transfers between devices: 25.7 us -> 31.8 us
  Pallas kernels: 33.3 us -> 38.2 us
  other arithmetic: 5.51 us -> 7.67 us
    ppermute x5 -> x8, waiting for transfers between devices: 25.3 us -> 9.22 us  [from_behind(): return lax.ppermute(block, axis, route)]
    ppermute x5 -> x8, starting transfers between devices: 18.9 us -> 24.9 us  [from_behind(): return lax.ppermute(block, axis, route)]
    pallas_call x2 -> x4, Pallas kernels: 33.3 us -> 38.2 us  [the longest x2 23.7 us: layer_call(): pl.pallas_call(layer_kernel, grid=(1, kv_heads), in_specs=[q_spec, kv_spe...]
    convert_element_type x1 -> x5, other arithmetic: 0.1 us -> 2.12 us  [the longest x2 1.03 us: device_body(): key_back.astype(jnp.bfloat16)]
    concatenate x2 -> x8, other arithmetic: 1.66 us -> 3.28 us  [the longest x1 1.58 us: device_body(): jnp.concatenate([query_send] + kv_send, axis=-1)]
    broadcast_in_dim x2 -> x1, other arithmetic: 3.63 us -> 2.15 us  [device_body(): return (query_all[None], key_grads[None], value_grads[None])]
  transfers between devices with their start and end apart: 6 -> 9, of which waited for: 6 -> 6; matrix products, arithmetic and copies ran while one was open for 2% -> 5% of each run, Pallas kernels for 0% -> 5%
where the time goes in v4:
time: 136 us; the launch traced here: 135 us
  Pallas kernels  38.2 us (28%)
  starting transfers between devices  31.8 us (23%)
  waiting for transfers between devices  28.4 us (21%)
  blocking collectives  19.9 us (15%)
  local copies, waits for them, and re-layouts  8.37 us (6%)
  other arithmetic  7.67 us (6%)
    ppermute x8, starting transfers between devices, from_behind(): return lax.ppermute(block, axis, route)  24.9 us
    pallas_call x2, Pallas kernels, layer_call(): pl.pallas_call(layer_kernel, grid=(1, kv_heads), in_specs=[q_spec, kv_spe...  23.7 us
    all_to_all x1, blocking collectives, device_body(): back = lax.all_to_all(grads_above, 'pipe', 0, 0)  19.9 us
    all_to_all x1, waiting for transfers between devices, device_body(): lax.all_to_all(jnp.concatenate([query_send] + kv_send, axis=-1), 'pipe',...  19.1 us
    pallas_call x2, Pallas kernels, chain_call(): pl.pallas_call(functools.partial(chain_kernel, first=first), out_shape=(j...  14.5 us
    ppermute x8, waiting for transfers between devices, from_behind(): return lax.ppermute(block, axis, route)  9.22 us
    all_to_all x1, starting transfers between devices, device_body(): lax.all_to_all(jnp.concatenate([query_send] + kv_send, axis=-1), 'pipe',...  6.89 us
  transfers between devices with their start and end apart: 9, of which 6 were waited for; matrix products, arithmetic and copies ran while one was open for 5% of the time, Pallas kernels for 5%

profile of v4, /device:TPU:97, one launch (start us, length us, event | category | flops | bytes accessed | tf_op | source)
XLA Modules:
  0.0 135.3 jit_solution(14046797254727815491)
XLA Ops:
  0.6 0.0 copy-start
  0.6 0.0 copy-start.2
  0.7 1.2 reshape_squeeze.11
  1.9 1.0 reshape_squeeze.10
  2.9 0.0 copy-done.2
  2.9 0.3 copy.12
  3.3 0.2 copy.8
  3.5 0.1 broadcast_in_dim.7
  3.6 0.1 broadcast_in_dim.6
  3.7 1.6 %pad_maximum_fusion = bf16[16,128,512]{2,1,0:T(8,128)(2,1)} fusion(bf16[16,128,128]{2,1,0:T(8,128)(2,1)S(1)} %bitcast.52, bf16[16,128,128]{2,1,0:T(8,128)(2,1)S(1)} %bitcast.53, bf16[16,128,256]{2,1,0:T(8,128)(2,1)S(1)} %bitcast.45), kind=kLoop, calls=%fused_computation | loop fusion | flops 6291456 | bytes 4194304 | tf_op jit(solution)/shard_map/concatenate | solution.py:177
  5.3 6.9 %all-to-all-start = ((bf16[16,128,512]{2,1,0:T(8,128)(2,1)}), bf16[16,128,512]{2,1,0:T(8,128)(2,1)S(1)}, u32[]{:S(2)}, u32[]{:S(2)}) async-start(bf16[16,128,512]{2,1,0:T(8,128)(2,1)} %pad_maximum_fusion), calls=%async_computation | async-start | bytes 4194304 | tf_op jit(solution)/shard_map/all_to_all | solution.py:177
  12.2 0.0 copy-done.4
  12.2 5.6 %collective-permute-start = (bf16[2,128,512]{2,1,0:T(8,128)(2,1)S(1)}, bf16[2,128,512]{2,1,0:T(8,128)(2,1)}, u32[]{:S(2)}, u32[]{:S(2)}) collective-permute-start(bf16[2,128,512]{2,1,0:T(8,128)(2,1)S(1)} %bitcast.48), channel_id=1, source_target_pairs={{0,1},{1,2},{2,3},{3,4},{4,5},{5,6},{6,7},{7,8},{8,9},{9,10},{10,1... | collective-permute-start | bytes 786440 | tf_op jit(solution)/shard_map/ppermute | solution.py:20
  17.8 1.9 %collective-permute-start.1 = (bf16[2,128,512]{2,1,0:T(8,128)(2,1)}, bf16[2,128,512]{2,1,0:T(8,128)(2,1)}, u32[]{:S(2)}, u32[]{:S(2)}) collective-permute-start(bf16[2,128,512]{2,1,0:T(8,128)(2,1)} %bitcast.49), channel_id=1, source_target_pairs={{0,1},{1,2},{2,3},{3,4},{4,5},{5,6},{6,7},{7,8},{8,9},{9,10},{10,1... | collective-permute-start | bytes 786440 | tf_op jit(solution)/shard_map/ppermute | solution.py:20
  19.7 0.0 copy-done.13
  19.8 0.0 copy-done
  19.9 0.7 fusion.7.g0_ref
  20.5 0.5 collective-permute-done.kh_ref
  21.1 2.9 %collective-permute-done.1.vh_ref = bf16[2,128,512]{2,1,0:T(8,128)(2,1)} collective-permute-done((bf16[2,128,512]{2,1,0:T(8,128)(2,1)}, bf16[2,128,512]{2,1,0:T(8,128)(2,1)}, u32[]{:S(2)}, u32[]{:S(2)}) %collective-permute-start.1) | collective-permute-done | bytes 262176 | tf_op jit(solution)/shard_map/ppermute | solution.py:20
  24.0 19.1 %all-to-all-done.x_ref = bf16[16,128,512]{2,1,0:T(8,128)(2,1)S(1)} async-done(((bf16[16,128,512]{2,1,0:T(8,128)(2,1)}), bf16[16,128,512]{2,1,0:T(8,128)(2,1)S(1)}, u32[]{:S(2)}, u32[]{:S(2)}) %all-to-all-start) | async-done | bytes 2097184 | tf_op jit(solution)/shard_map/all_to_all | solution.py:177
  43.1 1.0 fusion.6
  44.1 6.4 %collective-permute-start.3 = (bf16[8,128,256]{2,1,0:T(8,128)(2,1)S(1)}, bf16[8,128,256]{2,1,0:T(8,128)(2,1)}, u32[]{:S(2)}, u32[]{:S(2)}) collective-permute-start(bf16[8,128,256]{2,1,0:T(8,128)(2,1)S(1)} %get-tuple-element.36), channel_id=1, source_target_pairs={{0,1},{1,2},{2,3},{3,4},{4,5},{5,6},{6,7},{7,8},{8,9},{9,10},{10,1... | collective-permute-start | bytes 1572872 | tf_op jit(solution)/shard_map/ppermute | solution.py:20
  50.5 1.9 %collective-permute-start.2 = (bf16[8,128,256]{2,1,0:T(8,128)(2,1)}, bf16[8,128,256]{2,1,0:T(8,128)(2,1)}, u32[]{:S(2)}, u32[]{:S(2)}) collective-permute-start(bf16[8,128,256]{2,1,0:T(8,128)(2,1)} %get-tuple-element.35), channel_id=1, source_target_pairs={{0,1},{1,2},{2,3},{3,4},{4,5},{5,6},{6,7},{7,8},{8,9},{9,10},{10,1... | collective-permute-start | bytes 1572872 | tf_op jit(solution)/shard_map/ppermute | solution.py:20
  52.4 0.1 fusion.5
  52.5 0.1 and_convert_fusion.m_ref
  52.7 0.0 copy-start.3
  52.7 0.7 dynamic-slice_bitcast_fusion.m_ref
  53.4 3.2 %collective-permute-done.3.halo_ref = bf16[8,128,256]{2,1,0:T(8,128)(2,1)} collective-permute-done((bf16[8,128,256]{2,1,0:T(8,128)(2,1)S(1)}, bf16[8,128,256]{2,1,0:T(8,128)(2,1)}, u32[]{:S(2)}, u32[]{:S(2)}) %collective-permute-start.3) | collective-permute-done | bytes 524320 | tf_op jit(solution)/shard_map/ppermute | solution.py:20
  56.6 0.0 copy-done.1
  56.6 7.2 %shard_map.76 = (bf16[8,128,256]{2,1,0:T(8,128)(2,1)}, bf16[128,256]{1,0:T(8,128)(2,1)}) custom-call(bf16[16,128,512]{2,1,0:T(8,128)(2,1)} %copy-done.1, bf16[8,128,256]{2,1,0:T(8,128)(2,1)} %collective-permute-done.3.halo_ref, bf16[128,256]{1,0:T(8,128)(2,1)} %fusion.7.g0_ref, s32[128,256]{1,0:T(8,128)} %dynamic-slice_bitcast_fusion.m_ref), custom_call_target="tpu_custom_call" | custom-call | tf_op jit(solution)/shard_map/pallas_call | solution.py:70
  63.9 0.0 collective-permute-done.2.halo_ref
  63.9 7.3 %shard_map.77 = (bf16[8,128,256]{2,1,0:T(8,128)(2,1)}, bf16[128,256]{1,0:T(8,128)(2,1)}) custom-call(bf16[16,128,512]{2,1,0:T(8,128)(2,1)} %copy-done.1, bf16[8,128,256]{2,1,0:T(8,128)(2,1)} %collective-permute-done.2.halo_ref, bf16[128,256]{1,0:T(8,128)(2,1)} %get-tuple-element.22.g0_ref, s32[128,256]{1,0:T(8,128)} %dynamic-slice_bitcast_fusion.m_ref), custom_call_target="tpu_custom_call" | custom-call | tf_op jit(solution)/shard_map/pallas_call | solution.py:70
  71.1 0.0 copy-done.3
  71.1 1.0 slice.11
  72.2 0.0 copy-done.6
  72.2 0.1 pad_maximum_fusion.1
  72.3 19.9 %all_to_all.10 = bf16[16,128,256]{2,1,0:T(8,128)(2,1)S(1)} all-to-all(bf16[16,128,256]{2,1,0:T(8,128)(2,1)S(1)} %pad_maximum_fusion.1), channel_id=1, replica_groups=mesh['pipe'=16,'seq'=32] {'pipe'}, dimensions={0} | all-to-all | bytes 2097152 | tf_op jit(solution)/shard_map/all_to_all | solution.py:189
  92.2 0.6 copy.14
  92.8 1.3 reshape.174.g_ref
  94.1 11.7 %shard_map.79 = (f32[1,128,512]{2,1,0:T(8,128)}, f32[1,128,512]{2,1,0:T(8,128)}, f32[1,128,512]{2,1,0:T(8,128)}, f32[1,128,512]{2,1,0:T(8,128)}, bf16[1,128,2048]{2,1,0:T(8,128)(2,1)}) custom-call(bf16[2,128,2048]{2,1,0:T(8,128)(2,1)} %bitcast.39, bf16[2,128,512]{2,1,0:T(8,128)(2,1)} %collective-permute-done.kh_ref, bf16[2,128,512]{2,1,0:T(8,128)(2,1)} %bitcast.46, ...), custom_call_target="tpu_custom_call" | custom-call | tf_op jit(solution)/shard_map/pallas_call | solution.py:118
  105.8 0.0 copy-start.7
  105.8 0.0 copy-start.5
  105.8 11.9 %shard_map.78 = (f32[1,128,512]{2,1,0:T(8,128)}, f32[1,128,512]{2,1,0:T(8,128)}, f32[1,128,512]{2,1,0:T(8,128)}, f32[1,128,512]{2,1,0:T(8,128)}, bf16[1,128,2048]{2,1,0:T(8,128)(2,1)}) custom-call(bf16[2,128,2048]{2,1,0:T(8,128)(2,1)} %bitcast.40, bf16[2,128,512]{2,1,0:T(8,128)(2,1)} %collective-permute-done.kh_ref, bf16[2,128,512]{2,1,0:T(8,128)(2,1)} %bitcast.47, ...), custom_call_target="tpu_custom_call" | custom-call | tf_op jit(solution)/shard_map/pallas_call | solution.py:118
  117.8 0.0 copy-done.8
  117.8 0.0 copy-start.11
  117.8 3.3 %collective-permute-start.5 = (bf16[1,128,512]{2,1,0:T(8,128)(2,1)S(1)}, bf16[1,128,512]{2,1,0:T(8,128)(2,1)S(1)}, u32[]{:S(2)}, u32[]{:S(2)}) collective-permute-start(bf16[1,128,512]{2,1,0:T(8,128)(2,1)S(1)} %convert_element_type.46), channel_id=1, source_target_pairs={{1,0},{2,1},{3,2},{4,3},{5,4},{6,5},{7,6},{8,7},{9,8},{10,9},{11,1... | collective-permute-start | bytes 393224 | tf_op jit(solution)/shard_map/ppermute | solution.py:20
  121.1 0.0 copy-start.10
  121.2 1.0 convert_element_type.44
  122.2 1.9 %collective-permute-start.4 = (bf16[1,128,512]{2,1,0:T(8,128)(2,1)S(1)}, bf16[1,128,512]{2,1,0:T(8,128)(2,1)S(1)}, u32[]{:S(2)}, u32[]{:S(2)}) collective-permute-start(bf16[1,128,512]{2,1,0:T(8,128)(2,1)S(1)} %convert_element_type.44), channel_id=1, source_target_pairs={{1,0},{2,1},{3,2},{4,3},{5,4},{6,5},{7,6},{8,7},{9,8},{10,9},{11,1... | collective-permute-start | bytes 393224 | tf_op jit(solution)/shard_map/ppermute | solution.py:20
  124.1 0.0 copy-done.7
  124.1 1.9 %collective-permute-start.7 = (bf16[1,128,512]{2,1,0:T(8,128)(2,1)S(1)}, bf16[1,128,512]{2,1,0:T(8,128)(2,1)S(1)}, u32[]{:S(2)}, u32[]{:S(2)}) collective-permute-start(bf16[1,128,512]{2,1,0:T(8,128)(2,1)S(1)} %convert_element_type.50), channel_id=1, source_target_pairs={{1,0},{2,1},{3,2},{4,3},{5,4},{6,5},{7,6},{8,7},{9,8},{10,9},{11,1... | collective-permute-start | bytes 393224 | tf_op jit(solution)/shard_map/ppermute | solution.py:20
  126.1 1.0 convert_element_type.48
  127.0 1.9 %collective-permute-start.6 = (bf16[1,128,512]{2,1,0:T(8,128)(2,1)S(1)}, bf16[1,128,512]{2,1,0:T(8,128)(2,1)S(1)}, u32[]{:S(2)}, u32[]{:S(2)}) collective-permute-start(bf16[1,128,512]{2,1,0:T(8,128)(2,1)S(1)} %convert_element_type.48), channel_id=1, source_target_pairs={{1,0},{2,1},{3,2},{4,3},{5,4},{6,5},{7,6},{8,7},{9,8},{10,9},{11,1... | collective-permute-start | bytes 393224 | tf_op jit(solution)/shard_map/ppermute | solution.py:20
  129.0 0.0 copy-done.5
  129.0 0.0 copy-start.9
  129.0 2.2 %maximum_bitcast_fusion = bf16[1,2,128,2048]{3,2,1,0:T(8,128)(2,1)} fusion(bf16[1,128,2048]{2,1,0:T(8,128)(2,1)S(1)} %copy-done.5, bf16[1,128,2048]{2,1,0:T(8,128)(2,1)} %get-tuple-element.25), kind=kLoop, calls=%fused_computation.2 | loop fusion | flops 524288 | bytes 2097152 | tf_op jit(solution)/shard_map/broadcast_in_dim | solution.py:210
  131.1 0.0 collective-permute-done.5
  131.1 0.0 copy-done.12
  131.2 0.0 collective-permute-done.4
  131.2 0.0 copy-done.11
  131.2 0.4 collective-permute-done.7
  131.7 0.7 pad_maximum_fusion.2
  132.4 2.1 %collective-permute-done.6 = bf16[1,128,512]{2,1,0:T(8,128)(2,1)S(1)} collective-permute-done((bf16[1,128,512]{2,1,0:T(8,128)(2,1)S(1)}, bf16[1,128,512]{2,1,0:T(8,128)(2,1)S(1)}, u32[]{:S(2)}, u32[]{:S(2)}) %collective-permute-start.6) | collective-permute-done | bytes 131104 | tf_op jit(solution)/shard_map/ppermute | solution.py:20
  134.6 0.7 pad_maximum_fusion.3
  (22 shorter events, 0.3 us)
Async XLA Ops:
  0.6 19.2 %copy-start = (bf16[2,128,2048]{2,1,0:T(8,128)(2,1)S(1)}, bf16[2,128,2048]{2,1,0:T(8,128)(2,1)}, u32[]{:S(2)}) copy-start(bf16[2,128,2048]{2,1,0:T(8,128)(2,1)} %param.8) | copy-start | bytes 3145732
  0.6 2.3 %copy-start.2 = (bf16[1,2,128,2048]{3,2,1,0:T(8,128)(2,1)S(1)}, bf16[1,2,128,2048]{3,2,1,0:T(8,128)(2,1)}, u32[]{:S(2)}) copy-start(bf16[1,2,128,2048]{3,2,1,0:T(8,128)(2,1)} %param.5) | copy-start | bytes 3145732
  5.3 6.9 %copy-start.4 = (bf16[1,2,128,512]{3,2,1,0:T(8,128)(2,1)S(1)}, bf16[1,2,128,512]{3,2,1,0:T(8,128)(2,1)}, u32[]{:S(2)}) copy-start(bf16[1,2,128,512]{3,2,1,0:T(8,128)(2,1)} %param.6) | copy-start | bytes 786436
  5.3 14.5 %copy-start.13 = (s32[2,4096]{1,0:T(2,128)S(1)}, s32[2,4096]{1,0:T(2,128)}, u32[]{:S(2)}) copy-start(s32[2,4096]{1,0:T(2,128)} %param.9) | copy-start | bytes 98308
  5.3 37.9 %all-to-all-start = ((bf16[16,128,512]{2,1,0:T(8,128)(2,1)}), bf16[16,128,512]{2,1,0:T(8,128)(2,1)S(1)}, u32[]{:S(2)}, u32[]{:S(2)}) async-start(bf16[16,128,512]{2,1,0:T(8,128)(2,1)} %pad_maximum_fusion), calls=%async_computation | async-start | bytes 4194304 | tf_op jit(solution)/shard_map/all_to_all | solution.py:177
  12.2 8.9 %collective-permute-start = (bf16[2,128,512]{2,1,0:T(8,128)(2,1)S(1)}, bf16[2,128,512]{2,1,0:T(8,128)(2,1)}, u32[]{:S(2)}, u32[]{:S(2)}) collective-permute-start(bf16[2,128,512]{2,1,0:T(8,128)(2,1)S(1)} %bitcast.48), channel_id=1, source_target_pairs={{0,1},{1,2},{2,3},{3,4},{4,5},{5,6},{6,7},{7,8},{8,9},{9,10},{10,1... | collective-permute-start | bytes 786440 | tf_op jit(solution)/shard_map/ppermute | solution.py:20
  17.8 6.2 %collective-permute-start.1 = (bf16[2,128,512]{2,1,0:T(8,128)(2,1)}, bf16[2,128,512]{2,1,0:T(8,128)(2,1)}, u32[]{:S(2)}, u32[]{:S(2)}) collective-permute-start(bf16[2,128,512]{2,1,0:T(8,128)(2,1)} %bitcast.49), channel_id=1, source_target_pairs={{0,1},{1,2},{2,3},{3,4},{4,5},{5,6},{6,7},{7,8},{8,9},{9,10},{10,1... | collective-permute-start | bytes 786440 | tf_op jit(solution)/shard_map/ppermute | solution.py:20
  43.1 13.5 %copy-start.1 = (bf16[16,128,512]{2,1,0:T(8,128)(2,1)}, bf16[16,128,512]{2,1,0:T(8,128)(2,1)S(1)}, u32[]{:S(2)}) copy-start(bf16[16,128,512]{2,1,0:T(8,128)(2,1)S(1)} %all-to-all-done.x_ref) | copy-start | bytes 6291460
  44.1 12.5 %collective-permute-start.3 = (bf16[8,128,256]{2,1,0:T(8,128)(2,1)S(1)}, bf16[8,128,256]{2,1,0:T(8,128)(2,1)}, u32[]{:S(2)}, u32[]{:S(2)}) collective-permute-start(bf16[8,128,256]{2,1,0:T(8,128)(2,1)S(1)} %get-tuple-element.36), channel_id=1, source_target_pairs={{0,1},{1,2},{2,3},{3,4},{4,5},{5,6},{6,7},{7,8},{8,9},{9,10},{10,1... | collective-permute-start | bytes 1572872 | tf_op jit(solution)/shard_map/ppermute | solution.py:20
  50.5 13.3 %collective-permute-start.2 = (bf16[8,128,256]{2,1,0:T(8,128)(2,1)}, bf16[8,128,256]{2,1,0:T(8,128)(2,1)}, u32[]{:S(2)}, u32[]{:S(2)}) collective-permute-start(bf16[8,128,256]{2,1,0:T(8,128)(2,1)} %get-tuple-element.35), channel_id=1, source_target_pairs={{0,1},{1,2},{2,3},{3,4},{4,5},{5,6},{6,7},{7,8},{8,9},{9,10},{10,1... | collective-permute-start | bytes 1572872 | tf_op jit(solution)/shard_map/ppermute | solution.py:20
  52.7 18.5 %copy-start.3 = (s32[2,128,256]{2,1,0:T(8,128)}, s32[2,128,256]{2,1,0:T(8,128)S(1)}, u32[]{:S(2)}) copy-start(s32[2,128,256]{2,1,0:T(8,128)S(1)} %and_convert_fusion.m_ref) | copy-start | bytes 786436
  63.9 8.3 %copy-start.6 = (bf16[8,128,256]{2,1,0:T(8,128)(2,1)S(1)}, bf16[8,128,256]{2,1,0:T(8,128)(2,1)}, u32[]{:S(2)}) copy-start(bf16[8,128,256]{2,1,0:T(8,128)(2,1)} %get-tuple-element.24) | copy-start | bytes 1572868
  105.8 12.0 %copy-start.8 = (f32[1,128,512]{2,1,0:T(8,128)S(1)}, f32[1,128,512]{2,1,0:T(8,128)}, u32[]{:S(2)}) copy-start(f32[1,128,512]{2,1,0:T(8,128)} %get-tuple-element.30) | copy-start | bytes 786436
  105.8 18.3 %copy-start.7 = (f32[1,128,512]{2,1,0:T(8,128)S(1)}, f32[1,128,512]{2,1,0:T(8,128)}, u32[]{:S(2)}) copy-start(f32[1,128,512]{2,1,0:T(8,128)} %get-tuple-element.34) | copy-start | bytes 786436
  105.8 23.1 %copy-start.5 = (bf16[1,128,2048]{2,1,0:T(8,128)(2,1)S(1)}, bf16[1,128,2048]{2,1,0:T(8,128)(2,1)}, u32[]{:S(2)}) copy-start(bf16[1,128,2048]{2,1,0:T(8,128)(2,1)} %get-tuple-element.26) | copy-start | bytes 1572868
  117.8 13.4 %copy-start.12 = (f32[1,128,512]{2,1,0:T(8,128)S(1)}, f32[1,128,512]{2,1,0:T(8,128)}, u32[]{:S(2)}) copy-start(f32[1,128,512]{2,1,0:T(8,128)} %get-tuple-element.29) | copy-start | bytes 786436
  117.8 13.4 %copy-start.11 = (f32[1,128,512]{2,1,0:T(8,128)S(1)}, f32[1,128,512]{2,1,0:T(8,128)}, u32[]{:S(2)}) copy-start(f32[1,128,512]{2,1,0:T(8,128)} %get-tuple-element.27) | copy-start | bytes 786436
  117.8 13.3 %collective-permute-start.5 = (bf16[1,128,512]{2,1,0:T(8,128)(2,1)S(1)}, bf16[1,128,512]{2,1,0:T(8,128)(2,1)S(1)}, u32[]{:S(2)}, u32[]{:S(2)}) collective-permute-start(bf16[1,128,512]{2,1,0:T(8,128)(2,1)S(1)} %convert_element_type.46), channel_id=1, source_target_pairs={{1,0},{2,1},{3,2},{4,3},{5,4},{6,5},{7,6},{8,7},{9,8},{10,9},{11,1... | collective-permute-start | bytes 393224 | tf_op jit(solution)/shard_map/ppermute | solution.py:20
  121.1 10.5 %copy-start.10 = (f32[1,128,512]{2,1,0:T(8,128)S(1)}, f32[1,128,512]{2,1,0:T(8,128)}, u32[]{:S(2)}) copy-start(f32[1,128,512]{2,1,0:T(8,128)} %get-tuple-element.33) | copy-start | bytes 786436
  122.2 9.0 %collective-permute-start.4 = (bf16[1,128,512]{2,1,0:T(8,128)(2,1)S(1)}, bf16[1,128,512]{2,1,0:T(8,128)(2,1)S(1)}, u32[]{:S(2)}, u32[]{:S(2)}) collective-permute-start(bf16[1,128,512]{2,1,0:T(8,128)(2,1)S(1)} %convert_element_type.44), channel_id=1, source_target_pairs={{1,0},{2,1},{3,2},{4,3},{5,4},{6,5},{7,6},{8,7},{9,8},{10,9},{11,1... | collective-permute-start | bytes 393224 | tf_op jit(solution)/shard_map/ppermute | solution.py:20
  124.1 7.5 %collective-permute-start.7 = (bf16[1,128,512]{2,1,0:T(8,128)(2,1)S(1)}, bf16[1,128,512]{2,1,0:T(8,128)(2,1)S(1)}, u32[]{:S(2)}, u32[]{:S(2)}) collective-permute-start(bf16[1,128,512]{2,1,0:T(8,128)(2,1)S(1)} %convert_element_type.50), channel_id=1, source_target_pairs={{1,0},{2,1},{3,2},{4,3},{5,4},{6,5},{7,6},{8,7},{9,8},{10,9},{11,1... | collective-permute-start | bytes 393224 | tf_op jit(solution)/shard_map/ppermute | solution.py:20
  127.0 7.5 %collective-permute-start.6 = (bf16[1,128,512]{2,1,0:T(8,128)(2,1)S(1)}, bf16[1,128,512]{2,1,0:T(8,128)(2,1)S(1)}, u32[]{:S(2)}, u32[]{:S(2)}) collective-permute-start(bf16[1,128,512]{2,1,0:T(8,128)(2,1)S(1)} %convert_element_type.48), channel_id=1, source_target_pairs={{1,0},{2,1},{3,2},{4,3},{5,4},{6,5},{7,6},{8,7},{9,8},{10,9},{11,1... | collective-permute-start | bytes 393224 | tf_op jit(solution)/shard_map/ppermute | solution.py:20
  129.0 5.6 %copy-start.9 = (f32[1,128,512]{2,1,0:T(8,128)S(1)}, f32[1,128,512]{2,1,0:T(8,128)}, u32[]{:S(2)}) copy-start(f32[1,128,512]{2,1,0:T(8,128)} %get-tuple-element.31) | copy-start | bytes 786436

commit v5 on v4

--- a/solution.py
+++ b/solution.py
@@ -77,54 +77,65 @@
     )(sent, halo, grad_top, allowed_i32)
 
 
-def layer_kernel(q_ref, kh_ref, ko_ref, vh_ref, vo_ref, g_ref, m_ref,
-                 dkh_ref, dko_ref, dvh_ref, dvo_ref, gl_ref):
-    heads = q_ref.shape[2] // DH
-    rows = kh_ref.shape[1]
+def layer_kernel(q_ref, kvo_ref, kvh_ref, ga_ref, gb_ref, m_ref, gi_ref,
+                 dk_ref, dv_ref, back_ref, gl_ref):
+    del gi_ref
+    heads = q_ref.shape[3] // DH
+    rows = q_ref.shape[2]
     allowed = m_ref[0] != 0
-    k = jnp.concatenate([kh_ref[0], ko_ref[0]], axis=0)
-    v = jnp.concatenate([vh_ref[0], vo_ref[0]], axis=0)
+    k = jnp.concatenate([kvh_ref[0, 0, 0], kvo_ref[0, 0, 0]], axis=0)
+    v = jnp.concatenate([kvh_ref[1, 0, 0], kvo_ref[1, 0, 0]], axis=0)
+    grad = jnp.concatenate([ga_ref[0], gb_ref[0]], axis=-1)
     dk = None
     dv = None
     for h in range(heads):
         cols = slice(h * DH, (h + 1) * DH)
-        q = q_ref[0, :, cols]
-        g = g_ref[0, :, cols]
+        q = q_ref[0, 0, :, cols]
+        g = grad[:, cols]
         prob_low, grad_score = head_core(q, k, v, g, allowed)
         dq = jnp.dot(grad_score, k, preferred_element_type=jnp.float32) * SCALE
-        gl_ref[0, :, cols] = (g.astype(jnp.float32) + dq).astype(jnp.bfloat16)
+        gl_ref[0, 0, :, cols] = (g.astype(jnp.float32) + dq).astype(jnp.bfloat16)
         dk_h = lax.dot_general(grad_score, q, TN, preferred_element_type=jnp.float32)
         dv_h = lax.dot_general(prob_low, g, TN, preferred_element_type=jnp.float32)
         dk = dk_h if dk is None else dk + dk_h
         dv = dv_h if dv is None else dv + dv_h
     dk = dk * SCALE
-    dkh_ref[0] = dk[:rows]
-    dko_ref[0] = dk[rows:]
-    dvh_ref[0] = dv[:rows]
-    dvo_ref[0] = dv[rows:]
-
-
-def layer_call(query, key_halo, key_own, value_halo, value_own, grad_in, allowed_i32, micro,
-               interpret=False):
-    _, rows, width = query.shape
-    kv_heads = key_own.shape[2] // DH
+    back_ref[0, 0] = dk[:rows].astype(back_ref.dtype)
+    back_ref[1, 0] = dv[:rows].astype(back_ref.dtype)
+    dk_ref[0] = dk[rows:]
+    dv_ref[0] = dv[rows:]
+
+
+def layer_call(queries, kv_own, kv_halo, grad_t, allowed_i32, grad_prev, micro,
+               blocks_per_kv, interpret=False):
+    _, micro_count, rows, width = queries.shape
+    kv_heads = kv_own.shape[4] // DH
     group = width // (kv_heads * DH)
     gw = group * DH
-    kv_spec = pl.BlockSpec((1, rows, DH), lambda m, g: (micro, 0, g))
-    q_spec = pl.BlockSpec((1, rows, gw), lambda m, g: (micro, 0, g))
-    kv_out = pl.BlockSpec((1, rows, DH), lambda m, g: (0, 0, g))
-    q_out = pl.BlockSpec((1, rows, gw), lambda m, g: (0, 0, g))
-    kv_shape = jax.ShapeDtypeStruct((1, rows, key_own.shape[2]), jnp.float32)
+    bw = grad_t.shape[2]
+    kv_spec = pl.BlockSpec((2, 1, 1, rows, DH), lambda i, g: (0, 0, micro, 0, g))
+    q_spec = pl.BlockSpec((1, 1, rows, gw), lambda i, g: (0, micro, 0, g))
+    ga_spec = pl.BlockSpec(
+        (1, rows, bw), lambda i, g: ((g * blocks_per_kv) * micro_count + micro, 0, 0))
+    gb_spec = pl.BlockSpec(
+        (1, rows, bw), lambda i, g: ((g * blocks_per_kv + 1) * micro_count + micro, 0, 0))
+    own_out = pl.BlockSpec((1, rows, DH), lambda i, g: (0, 0, g))
+    own_shape = jax.ShapeDtypeStruct((1, rows, kv_heads * DH), jnp.float32)
     return pl.pallas_call(
         layer_kernel,
         grid=(1, kv_heads),
-        in_specs=[q_spec, kv_spec, kv_spec, kv_spec, kv_spec, q_spec,
-                  pl.BlockSpec((1, rows, 2 * rows), lambda m, g: (micro, 0, 0))],
-        out_specs=[kv_out, kv_out, kv_out, kv_out, q_out],
-        out_shape=[kv_shape, kv_shape, kv_shape, kv_shape,
-                   jax.ShapeDtypeStruct((1, rows, width), jnp.bfloat16)],
+        in_specs=[q_spec, kv_spec, kv_spec, ga_spec, gb_spec,
+                  pl.BlockSpec((1, rows, 2 * rows), lambda i, g: (micro, 0, 0)),
+                  pl.BlockSpec(memory_space=pl.ANY)],
+        out_specs=[own_out, own_out,
+                   pl.BlockSpec((2, 1, rows, DH), lambda i, g: (0, 0, 0, g)),
+                   q_spec],
+        out_shape=[own_shape, own_shape,
+                   jax.ShapeDtypeStruct((2, 1, rows, kv_heads * DH), jnp.bfloat16),
+                   jax.ShapeDtypeStruct(queries.shape, jnp.bfloat16)],
+        input_output_aliases={6: 3},
         interpret=interpret,
-    )(query, key_halo, key_own, value_halo, value_own, grad_in, allowed_i32)
+    )(queries, kv_own, kv_halo, grad_t, grad_t, allowed_i32, grad_prev)
 
 
 def device_body(queries, keys, values, out_grad, segments):
@@ -145,6 +156,7 @@
     own_query = queries[0]
     own_key = keys[0]
     own_value = values[0]
+    kv_own = jnp.stack([keys, values])
     seg_padded = jnp.concatenate(
         [jnp.full((micro_count, row_count), -1, jnp.int32), segments], axis=1
     )
@@ -160,7 +172,7 @@
         & (key_pos[None, :] >= 0)
     )
     masks = (near[None] & (seg_query[:, :, None] == seg_key[:, None, :])).astype(jnp.int32)
-    halo_key, halo_value = from_behind((own_key, own_value), "seq", 1)
+    kv_halo = from_behind(kv_own, "seq", 1)
 
     my_block = section_index // micro_count
     my_micro = section_index % micro_count
@@ -175,7 +187,7 @@
         )
         kv_send.append(split.reshape(section_count, row_count, DH))
     sent = lax.all_to_all(jnp.concatenate([query_send] + kv_send, axis=-1), "pipe", 0, 0)
-    sent, halo_key, halo_value = lax.optimization_barrier((sent, halo_key, halo_value))
+    sent, kv_halo = lax.optimization_barrier((sent, kv_halo))
     split_at = section_count // 2
     halo_hi = from_behind(sent[split_at:, :, block_width:], "seq", 1)
     halo_lo = from_behind(sent[:split_at, :, block_width:], "seq", 1)
@@ -186,25 +198,19 @@
     grads_hi, grad_mid = chain_call(sent, halo_hi, grad_top, allowed, split_at)
     grads_lo, _ = chain_call(sent, halo_lo, grad_mid, allowed, 0)
     grads_above = jnp.concatenate([grads_lo[1:], grads_hi, grad_top[None]], axis=0)
-    back = lax.all_to_all(grads_above, "pipe", 0, 0)
-    grad_in = jnp.transpose(
-        back.reshape(head_blocks, micro_count, row_count, block_width), (1, 2, 0, 3)
-    ).reshape(micro_count, row_count, query_width)
-
-    query_parts = []
+    grad_t = lax.all_to_all(grads_above, "pipe", 0, 0)
+
+    query_all = jnp.zeros(queries.shape, jnp.bfloat16)
     key_parts = []
     value_parts = []
     for micro in range(micro_count):
-        key_back, key_own_grad, value_back, value_own_grad, query_part = layer_call(
-            own_query, halo_key, own_key, halo_value, own_value, grad_in, masks, micro
-        )
-        back_key, back_value = from_behind(
-            (key_back.astype(jnp.bfloat16), value_back.astype(jnp.bfloat16)), "seq", -1
-        )
-        key_parts.append(key_own_grad + back_key.astype(jnp.float32))
-        value_parts.append(value_own_grad + back_value.astype(jnp.float32))
-        query_parts.append(query_part)
-    query_all = jnp.concatenate(query_parts, axis=0)
+        key_own_grad, value_own_grad, kv_back, query_all = layer_call(
+            queries, kv_own, kv_halo, grad_t, masks, query_all, micro, blocks_per_kv
+        )
+        kv_next = from_behind(kv_back, "seq", -1)
+        key_parts.append(key_own_grad + kv_next[0].astype(jnp.float32))
+        value_parts.append(value_own_grad + kv_next[1].astype(jnp.float32))
+    query_all = query_all[0]
     key_grads = jnp.concatenate(key_parts, axis=0).astype(jnp.bfloat16)
     value_grads = jnp.concatenate(value_parts, axis=0).astype(jnp.bfloat16)
     return (query_all[None], key_grads[None], value_grads[None])

time: 136 us -> 132 us (0.971)
  starting transfers between devices: 31.8 us -> 25.7 us
  waiting for transfers between devices: 28.4 us -> 33.1 us
  other arithmetic: 7.67 us -> 5.72 us
    ppermute x8 -> x5, waiting for transfers between devices: 9.22 us -> 15.9 us  [from_behind(): return lax.ppermute(block, axis, route)]
    ppermute x8 -> x5, starting transfers between devices: 24.9 us -> 18.8 us  [from_behind(): return lax.ppermute(block, axis, route)]
    broadcast_in_dim x1 -> x0, other arithmetic: 2.15 us -> none  [device_body(): return (query_all[None], key_grads[None], value_grads[None])]
    convert_element_type x4 -> x0, other arithmetic: 2.02 us -> none  [the longest x2 1.03 us: device_body(): key_back.astype(jnp.bfloat16)]
    all_to_all x1, waiting for transfers between devices: 19.1 us -> 17.2 us  [device_body(): lax.all_to_all(jnp.concatenate([query_send] + kv_send, axis=-1), 'pipe',...]
    reshape x2 -> x0, local copies, waits for them, and re-layouts: 1.89 us -> none  [the longest x1 1.31 us: device_body(): grad_in = jnp.transpose(back.reshape(head_blocks, micro_count, row_count,...]
    another operation x0 -> x1, other arithmetic: none -> 1.79 us  [device_body(): kv_own = jnp.stack([keys, values])]
  transfers between devices with their start and end apart: 9 -> 6, of which waited for: 6 -> 4; matrix products, arithmetic and copies ran while one was open for 5% -> 3% of each run, Pallas kernels for 5% -> 14%
where the time goes in v5:
time: 132 us; the launch traced here: 131 us
  Pallas kernels  37.9 us (29%)
  waiting for transfers between devices  33.1 us (25%)
  starting transfers between devices  25.7 us (19%)
  blocking collectives  20.4 us (15%)
  local copies, waits for them, and re-layouts  7.78 us (6%)
  other arithmetic  5.72 us (4%)
    pallas_call x2, Pallas kernels, layer_call(): pl.pallas_call(layer_kernel, grid=(1, kv_heads), in_specs=[q_spec, kv_spe...  23.4 us
    all_to_all x1, blocking collectives, device_body(): grad_t = lax.all_to_all(grads_above, 'pipe', 0, 0)  20.4 us
    ppermute x5, starting transfers between devices, from_behind(): return lax.ppermute(block, axis, route)  18.8 us
    all_to_all x1, waiting for transfers between devices, device_body(): lax.all_to_all(jnp.concatenate([query_send] + kv_send, axis=-1), 'pipe',...  17.2 us
    ppermute x5, waiting for transfers between devices, from_behind(): return lax.ppermute(block, axis, route)  15.9 us
    pallas_call x2, Pallas kernels, chain_call(): pl.pallas_call(functools.partial(chain_kernel, first=first), out_shape=(j...  14.5 us
    all_to_all x1, starting transfers between devices, device_body(): lax.all_to_all(jnp.concatenate([query_send] + kv_send, axis=-1), 'pipe',...  6.89 us
  transfers between devices with their start and end apart: 6, of which 4 were waited for; matrix products, arithmetic and copies ran while one was open for 3% of the time, Pallas kernels for 14%

profile of v5, /device:TPU:97, one launch (start us, length us, event | category | flops | bytes accessed | tf_op | source)
XLA Modules:
  0.0 131.5 jit_solution(18124118242033181995)
XLA Ops:
  0.6 0.0 copy-start
  0.6 1.6 %copy.13 = bf16[32,8,8,256]{3,2,1,0:T(8,128)(2,1)S(1)} copy(bf16[32,8,8,256]{3,1,2,0:T(8,128)(2,1)} %bitcast.50) | data formatting | bytes 2097152
  2.3 0.0 copy-start.3
  2.3 0.2 copy.10
  2.5 1.0 reshape_squeeze.10
  3.6 0.0 copy-done.3
  3.6 0.1 reshape_squeeze.11
  3.7 0.1 broadcast_in_dim.6
  3.8 0.1 broadcast_in_dim.7
  3.9 1.6 %pad_maximum_fusion = bf16[16,128,512]{2,1,0:T(8,128)(2,1)} fusion(bf16[16,128,128]{2,1,0:T(8,128)(2,1)S(1)} %bitcast.54, bf16[16,128,128]{2,1,0:T(8,128)(2,1)S(1)} %bitcast.53, bf16[16,128,256]{2,1,0:T(8,128)(2,1)S(1)} %bitcast.52), kind=kLoop, calls=%fused_computation | loop fusion | flops 6291456 | bytes 4194304 | tf_op jit(solution)/shard_map/concatenate | solution.py:189
  5.5 0.0 copy-start.7
  5.5 6.9 %all-to-all-start = ((bf16[16,128,512]{2,1,0:T(8,128)(2,1)}), bf16[16,128,512]{2,1,0:T(8,128)(2,1)S(1)}, u32[]{:S(2)}, u32[]{:S(2)}) async-start(bf16[16,128,512]{2,1,0:T(8,128)(2,1)} %pad_maximum_fusion), calls=%async_computation | async-start | bytes 4194304 | tf_op jit(solution)/shard_map/all_to_all | solution.py:189
  12.4 1.8 %pad_maximum_fusion.2.kvo_ref = bf16[2,1,2,128,512]{4,3,2,1,0:T(8,128)(2,1)} fusion(bf16[1,1,2,128,512]{4,3,2,1,0:T(8,128)(2,1)S(1)} %bitcast.57, bf16[1,1,2,128,512]{4,3,2,1,0:T(8,128)(2,1)} %bitcast.58), kind=kLoop, calls=%fused_computation.2 | loop fusion | flops 262144 | bytes 1048576 | tf_op jit(solution)/shard_map/stack | solution.py:159
  14.2 5.6 %collective-permute-start = (bf16[2,1,2,128,512]{4,3,2,1,0:T(8,128)(2,1)}, bf16[2,1,2,128,512]{4,3,2,1,0:T(8,128)(2,1)}, u32[]{:S(2)}, u32[]{:S(2)}) collective-permute-start(bf16[2,1,2,128,512]{4,3,2,1,0:T(8,128)(2,1)} %pad_maximum_fusion.2.kvo_ref), channel_id=1, source_target_pairs={{0,1},{1,2},{2,3},{3,4},{4,5},{5,6},{6,7},{7,8},{8,9},{9,10},{10,1... | collective-permute-start | bytes 1572872 | tf_op jit(solution)/shard_map/ppermute | solution.py:20
  19.8 0.0 copy-done.7
  19.9 0.0 copy-done
  19.9 0.6 fusion.11.g0_ref
  20.5 5.6 %collective-permute-done.kvh_ref = bf16[2,1,2,128,512]{4,3,2,1,0:T(8,128)(2,1)} collective-permute-done((bf16[2,1,2,128,512]{4,3,2,1,0:T(8,128)(2,1)}, bf16[2,1,2,128,512]{4,3,2,1,0:T(8,128)(2,1)}, u32[]{:S(2)}, u32[]{:S(2)}) %collective-permute-start) | collective-permute-done | bytes 524320 | tf_op jit(solution)/shard_map/ppermute | solution.py:20
  26.2 17.2 %all-to-all-done.x_ref = bf16[16,128,512]{2,1,0:T(8,128)(2,1)S(1)} async-done(((bf16[16,128,512]{2,1,0:T(8,128)(2,1)}), bf16[16,128,512]{2,1,0:T(8,128)(2,1)S(1)}, u32[]{:S(2)}, u32[]{:S(2)}) %all-to-all-start) | async-done | bytes 2097184 | tf_op jit(solution)/shard_map/all_to_all | solution.py:189
  43.3 0.0 copy-start.1
  43.3 1.0 fusion.10
  44.3 6.4 %collective-permute-start.2 = (bf16[8,128,256]{2,1,0:T(8,128)(2,1)S(1)}, bf16[8,128,256]{2,1,0:T(8,128)(2,1)}, u32[]{:S(2)}, u32[]{:S(2)}) collective-permute-start(bf16[8,128,256]{2,1,0:T(8,128)(2,1)S(1)} %get-tuple-element.30), channel_id=1, source_target_pairs={{0,1},{1,2},{2,3},{3,4},{4,5},{5,6},{6,7},{7,8},{8,9},{9,10},{10,1... | collective-permute-start | bytes 1572872 | tf_op jit(solution)/shard_map/ppermute | solution.py:20
  50.7 1.9 %collective-permute-start.1 = (bf16[8,128,256]{2,1,0:T(8,128)(2,1)}, bf16[8,128,256]{2,1,0:T(8,128)(2,1)}, u32[]{:S(2)}, u32[]{:S(2)}) collective-permute-start(bf16[8,128,256]{2,1,0:T(8,128)(2,1)} %get-tuple-element.29), channel_id=1, source_target_pairs={{0,1},{1,2},{2,3},{3,4},{4,5},{5,6},{6,7},{7,8},{8,9},{9,10},{10,1... | collective-permute-start | bytes 1572872 | tf_op jit(solution)/shard_map/ppermute | solution.py:20
  52.7 0.1 fusion.9
  52.8 0.1 and_convert_fusion.m_ref
  52.9 0.0 copy-start.2
  52.9 0.7 dynamic-slice_bitcast_fusion.m_ref
  53.6 3.2 %collective-permute-done.2.halo_ref = bf16[8,128,256]{2,1,0:T(8,128)(2,1)} collective-permute-done((bf16[8,128,256]{2,1,0:T(8,128)(2,1)S(1)}, bf16[8,128,256]{2,1,0:T(8,128)(2,1)}, u32[]{:S(2)}, u32[]{:S(2)}) %collective-permute-start.2) | collective-permute-done | bytes 524320 | tf_op jit(solution)/shard_map/ppermute | solution.py:20
  56.8 0.0 copy-done.1
  56.8 7.2 %shard_map.76 = (bf16[8,128,256]{2,1,0:T(8,128)(2,1)}, bf16[128,256]{1,0:T(8,128)(2,1)}) custom-call(bf16[16,128,512]{2,1,0:T(8,128)(2,1)} %copy-done.1, bf16[8,128,256]{2,1,0:T(8,128)(2,1)} %collective-permute-done.2.halo_ref, bf16[128,256]{1,0:T(8,128)(2,1)} %fusion.11.g0_ref, s32[128,256]{1,0:T(8,128)} %dynamic-slice_bitcast_fusion.m_ref), custom_call_target="tpu_custom_call" | custom-call | tf_op jit(solution)/shard_map/pallas_call | solution.py:70
  64.1 0.0 copy-start.4
  64.1 0.0 collective-permute-done.1.halo_ref
  64.1 7.3 %shard_map.77 = (bf16[8,128,256]{2,1,0:T(8,128)(2,1)}, bf16[128,256]{1,0:T(8,128)(2,1)}) custom-call(bf16[16,128,512]{2,1,0:T(8,128)(2,1)} %copy-done.1, bf16[8,128,256]{2,1,0:T(8,128)(2,1)} %collective-permute-done.1.halo_ref, bf16[128,256]{1,0:T(8,128)(2,1)} %get-tuple-element.18.g0_ref, s32[128,256]{1,0:T(8,128)} %dynamic-slice_bitcast_fusion.m_ref), custom_call_target="tpu_custom_call" | custom-call | tf_op jit(solution)/shard_map/pallas_call | solution.py:70
  71.3 0.0 copy-done.2
  71.3 1.0 slice.23
  72.4 0.0 copy-done.4
  72.4 0.1 pad_maximum_fusion.1
  72.5 20.4 %all_to_all.10.ga_ref.gb_ref = bf16[16,128,256]{2,1,0:T(8,128)(2,1)} all-to-all(bf16[16,128,256]{2,1,0:T(8,128)(2,1)S(1)} %pad_maximum_fusion.1), channel_id=1, replica_groups=mesh['pipe'=16,'seq'=32] {'pipe'}, dimensions={0} | all-to-all | bytes 2097152 | tf_op jit(solution)/shard_map/all_to_all | solution.py:201
  92.9 1.1 broadcast_in_dim.8.gi_ref
  94.0 11.7 %shard_map.78 = (f32[1,128,512]{2,1,0:T(8,128)}, f32[1,128,512]{2,1,0:T(8,128)}, bf16[2,1,128,512]{3,2,1,0:T(8,128)(2,1)}, bf16[1,2,128,2048]{3,2,1,0:T(8,128)(2,1)}) custom-call(bf16[1,2,128,2048]{3,2,1,0:T(8,128)(2,1)} %q_ref.3, bf16[2,1,2,128,512]{4,3,2,1,0:T(8,128)(2,1)} %pad_maximum_fusion.2.kvo_ref, ...), custom_call_target="tpu_custom_call", output_to_operand_aliasing={{3}: (6, {})} | custom-call | tf_op jit(solution)/shard_map/pallas_call | solution.py:124
  105.7 3.0 %collective-permute-start.3 = (bf16[2,1,128,512]{3,2,1,0:T(8,128)(2,1)}, bf16[2,1,128,512]{3,2,1,0:T(8,128)(2,1)S(1)}, u32[]{:S(2)}, u32[]{:S(2)}) collective-permute-start(bf16[2,1,128,512]{3,2,1,0:T(8,128)(2,1)} %get-tuple-element.24), channel_id=1, source_target_pairs={{1,0},{2,1},{3,2},{4,3},{5,4},{6,5},{7,6},{8,7},{9,8},{10,9},{11,1... | collective-permute-start | bytes 786440 | tf_op jit(solution)/shard_map/ppermute | solution.py:20
  108.7 0.0 copy-start.5
  108.7 0.0 copy-start.6
  108.7 11.7 %shard_map.79 = (f32[1,128,512]{2,1,0:T(8,128)}, f32[1,128,512]{2,1,0:T(8,128)}, bf16[2,1,128,512]{3,2,1,0:T(8,128)(2,1)}, bf16[1,2,128,2048]{3,2,1,0:T(8,128)(2,1)}) custom-call(bf16[1,2,128,2048]{3,2,1,0:T(8,128)(2,1)} %q_ref.3, bf16[2,1,2,128,512]{4,3,2,1,0:T(8,128)(2,1)} %pad_maximum_fusion.2.kvo_ref, ...), custom_call_target="tpu_custom_call", output_to_operand_aliasing={{3}: (6, {})} | custom-call | tf_op jit(solution)/shard_map/pallas_call | solution.py:124
  120.4 1.9 %collective-permute-start.4 = (bf16[2,1,128,512]{3,2,1,0:T(8,128)(2,1)}, bf16[2,1,128,512]{3,2,1,0:T(8,128)(2,1)S(1)}, u32[]{:S(2)}, u32[]{:S(2)}) collective-permute-start(bf16[2,1,128,512]{3,2,1,0:T(8,128)(2,1)} %get-tuple-element.26), channel_id=1, source_target_pairs={{1,0},{2,1},{3,2},{4,3},{5,4},{6,5},{7,6},{8,7},{9,8},{10,9},{11,1... | collective-permute-start | bytes 786440 | tf_op jit(solution)/shard_map/ppermute | solution.py:20
  122.4 0.0 collective-permute-done.3
  122.4 0.0 copy-done.5
  122.4 0.0 copy-done.6
  122.4 0.1 fusion.6
  122.5 7.1 %collective-permute-done.4 = bf16[2,1,128,512]{3,2,1,0:T(8,128)(2,1)S(1)} collective-permute-done((bf16[2,1,128,512]{3,2,1,0:T(8,128)(2,1)}, bf16[2,1,128,512]{3,2,1,0:T(8,128)(2,1)S(1)}, u32[]{:S(2)}, u32[]{:S(2)}) %collective-permute-start.4) | collective-permute-done | bytes 262176 | tf_op jit(solution)/shard_map/ppermute | solution.py:20
  129.5 1.1 fusion.7
  130.6 0.8 pad_maximum_fusion.3
  (8 shorter events, 0.1 us)
Async XLA Ops:
  0.6 19.2 %copy-start = (bf16[2,128,2048]{2,1,0:T(8,128)(2,1)S(1)}, bf16[2,128,2048]{2,1,0:T(8,128)(2,1)}, u32[]{:S(2)}) copy-start(bf16[2,128,2048]{2,1,0:T(8,128)(2,1)} %param.8) | copy-start | bytes 3145732
  2.3 1.3 copy-start.3
  5.5 14.4 %copy-start.7 = (s32[2,4096]{1,0:T(2,128)S(1)}, s32[2,4096]{1,0:T(2,128)}, u32[]{:S(2)}) copy-start(s32[2,4096]{1,0:T(2,128)} %param.9) | copy-start | bytes 98308
  5.5 37.9 %all-to-all-start = ((bf16[16,128,512]{2,1,0:T(8,128)(2,1)}), bf16[16,128,512]{2,1,0:T(8,128)(2,1)S(1)}, u32[]{:S(2)}, u32[]{:S(2)}) async-start(bf16[16,128,512]{2,1,0:T(8,128)(2,1)} %pad_maximum_fusion), calls=%async_computation | async-start | bytes 4194304 | tf_op jit(solution)/shard_map/all_to_all | solution.py:189
  14.2 12.0 %collective-permute-start = (bf16[2,1,2,128,512]{4,3,2,1,0:T(8,128)(2,1)}, bf16[2,1,2,128,512]{4,3,2,1,0:T(8,128)(2,1)}, u32[]{:S(2)}, u32[]{:S(2)}) collective-permute-start(bf16[2,1,2,128,512]{4,3,2,1,0:T(8,128)(2,1)} %pad_maximum_fusion.2.kvo_ref), channel_id=1, source_target_pairs={{0,1},{1,2},{2,3},{3,4},{4,5},{5,6},{6,7},{7,8},{8,9},{9,10},{10,1... | collective-permute-start | bytes 1572872 | tf_op jit(solution)/shard_map/ppermute | solution.py:20
  43.3 13.5 %copy-start.1 = (bf16[16,128,512]{2,1,0:T(8,128)(2,1)}, bf16[16,128,512]{2,1,0:T(8,128)(2,1)S(1)}, u32[]{:S(2)}) copy-start(bf16[16,128,512]{2,1,0:T(8,128)(2,1)S(1)} %all-to-all-done.x_ref) | copy-start | bytes 6291460
  44.3 12.5 %collective-permute-start.2 = (bf16[8,128,256]{2,1,0:T(8,128)(2,1)S(1)}, bf16[8,128,256]{2,1,0:T(8,128)(2,1)}, u32[]{:S(2)}, u32[]{:S(2)}) collective-permute-start(bf16[8,128,256]{2,1,0:T(8,128)(2,1)S(1)} %get-tuple-element.30), channel_id=1, source_target_pairs={{0,1},{1,2},{2,3},{3,4},{4,5},{5,6},{6,7},{7,8},{8,9},{9,10},{10,1... | collective-permute-start | bytes 1572872 | tf_op jit(solution)/shard_map/ppermute | solution.py:20
  50.7 13.3 %collective-permute-start.1 = (bf16[8,128,256]{2,1,0:T(8,128)(2,1)}, bf16[8,128,256]{2,1,0:T(8,128)(2,1)}, u32[]{:S(2)}, u32[]{:S(2)}) collective-permute-start(bf16[8,128,256]{2,1,0:T(8,128)(2,1)} %get-tuple-element.29), channel_id=1, source_target_pairs={{0,1},{1,2},{2,3},{3,4},{4,5},{5,6},{6,7},{7,8},{8,9},{9,10},{10,1... | collective-permute-start | bytes 1572872 | tf_op jit(solution)/shard_map/ppermute | solution.py:20
  52.9 18.4 %copy-start.2 = (s32[2,128,256]{2,1,0:T(8,128)}, s32[2,128,256]{2,1,0:T(8,128)S(1)}, u32[]{:S(2)}) copy-start(s32[2,128,256]{2,1,0:T(8,128)S(1)} %and_convert_fusion.m_ref) | copy-start | bytes 786436
  64.1 8.3 %copy-start.4 = (bf16[8,128,256]{2,1,0:T(8,128)(2,1)S(1)}, bf16[8,128,256]{2,1,0:T(8,128)(2,1)}, u32[]{:S(2)}) copy-start(bf16[8,128,256]{2,1,0:T(8,128)(2,1)} %get-tuple-element.20) | copy-start | bytes 1572868
  105.7 16.7 %collective-permute-start.3 = (bf16[2,1,128,512]{3,2,1,0:T(8,128)(2,1)}, bf16[2,1,128,512]{3,2,1,0:T(8,128)(2,1)S(1)}, u32[]{:S(2)}, u32[]{:S(2)}) collective-permute-start(bf16[2,1,128,512]{3,2,1,0:T(8,128)(2,1)} %get-tuple-element.24), channel_id=1, source_target_pairs={{1,0},{2,1},{3,2},{4,3},{5,4},{6,5},{7,6},{8,7},{9,8},{10,9},{11,1... | collective-permute-start | bytes 786440 | tf_op jit(solution)/shard_map/ppermute | solution.py:20
  108.7 13.7 %copy-start.5 = (f32[1,128,512]{2,1,0:T(8,128)S(1)}, f32[1,128,512]{2,1,0:T(8,128)}, u32[]{:S(2)}) copy-start(f32[1,128,512]{2,1,0:T(8,128)} %get-tuple-element.23) | copy-start | bytes 786436
  108.7 13.7 %copy-start.6 = (f32[1,128,512]{2,1,0:T(8,128)S(1)}, f32[1,128,512]{2,1,0:T(8,128)}, u32[]{:S(2)}) copy-start(f32[1,128,512]{2,1,0:T(8,128)} %get-tuple-element.27) | copy-start | bytes 786436
  120.4 9.1 %collective-permute-start.4 = (bf16[2,1,128,512]{3,2,1,0:T(8,128)(2,1)}, bf16[2,1,128,512]{3,2,1,0:T(8,128)(2,1)S(1)}, u32[]{:S(2)}, u32[]{:S(2)}) collective-permute-start(bf16[2,1,128,512]{3,2,1,0:T(8,128)(2,1)} %get-tuple-element.26), channel_id=1, source_target_pairs={{1,0},{2,1},{3,2},{4,3},{5,4},{6,5},{7,6},{8,7},{9,8},{10,9},{11,1... | collective-permute-start | bytes 786440 | tf_op jit(solution)/shard_map/ppermute | solution.py:20

commit v6 on v5

--- a/solution.py
+++ b/solution.py
@@ -77,12 +77,47 @@
     )(sent, halo, grad_top, allowed_i32)
 
 
-def layer_kernel(q_ref, kvo_ref, kvh_ref, ga_ref, gb_ref, m_ref, gi_ref,
-                 dk_ref, dv_ref, back_ref, gl_ref):
-    del gi_ref
+def layer_pre_kernel(q_ref, kvo_ref, kvh_ref, m_ref, p_ref, o_ref):
+    heads = q_ref.shape[3] // DH
+    allowed = m_ref[0] != 0
+    k = jnp.concatenate([kvh_ref[0, 0, 0], kvo_ref[0, 0, 0]], axis=0)
+    v = jnp.concatenate([kvh_ref[1, 0, 0], kvo_ref[1, 0, 0]], axis=0)
+    for h in range(heads):
+        q = q_ref[0, 0, :, h * DH:(h + 1) * DH]
+        scores = lax.dot_general(q, k, NT, preferred_element_type=jnp.float32) * SCALE
+        masked = jnp.where(allowed, scores, -jnp.inf)
+        row_max = jnp.max(masked, axis=-1, keepdims=True)
+        weights = jnp.exp(masked - row_max)
+        prob = weights / jnp.sum(weights, axis=-1, keepdims=True)
+        p_ref[0, h] = prob
+        o_ref[0, h] = jnp.dot(prob.astype(jnp.bfloat16), v, preferred_element_type=jnp.float32)
+
+
+def layer_pre_call(queries, kv_own, kv_halo, allowed_i32, interpret=False):
+    _, micro_count, rows, width = queries.shape
+    kv_heads = kv_own.shape[4] // DH
+    group = width // (kv_heads * DH)
+    kv_spec = pl.BlockSpec((2, 1, 1, rows, DH), lambda m, g: (0, 0, m, 0, g))
+    return pl.pallas_call(
+        layer_pre_kernel,
+        grid=(micro_count, kv_heads),
+        in_specs=[pl.BlockSpec((1, 1, rows, group * DH), lambda m, g: (0, m, 0, g)),
+                  kv_spec, kv_spec,
+                  pl.BlockSpec((1, rows, 2 * rows), lambda m, g: (m, 0, 0))],
+        out_specs=[pl.BlockSpec((1, group, rows, 2 * rows), lambda m, g: (m, g, 0, 0)),
+                   pl.BlockSpec((1, group, rows, DH), lambda m, g: (m, g, 0, 0))],
+        out_shape=[
+            jax.ShapeDtypeStruct((micro_count, kv_heads * group, rows, 2 * rows), jnp.float32),
+            jax.ShapeDtypeStruct((micro_count, kv_heads * group, rows, DH), jnp.float32),
+        ],
+        interpret=interpret,
+    )(queries, kv_own, kv_halo, allowed_i32)
+
+
+def layer_kernel(q_ref, kvo_ref, kvh_ref, ga_ref, gb_ref, p_ref, o_ref, *rest):
+    dk_ref, dv_ref, back_ref, gl_ref = rest[-4:]
     heads = q_ref.shape[3] // DH
     rows = q_ref.shape[2]
-    allowed = m_ref[0] != 0
     k = jnp.concatenate([kvh_ref[0, 0, 0], kvo_ref[0, 0, 0]], axis=0)
     v = jnp.concatenate([kvh_ref[1, 0, 0], kvo_ref[1, 0, 0]], axis=0)
     grad = jnp.concatenate([ga_ref[0], gb_ref[0]], axis=-1)
@@ -92,7 +127,11 @@
         cols = slice(h * DH, (h + 1) * DH)
         q = q_ref[0, 0, :, cols]
         g = grad[:, cols]
-        prob_low, grad_score = head_core(q, k, v, g, allowed)
+        prob = p_ref[0, h]
+        prob_low = prob.astype(jnp.bfloat16)
+        grad_prob = lax.dot_general(g, v, NT, preferred_element_type=jnp.float32)
+        grad_dot = jnp.sum(g.astype(jnp.float32) * o_ref[0, h], axis=-1, keepdims=True)
+        grad_score = (prob * (grad_prob - grad_dot)).astype(jnp.bfloat16)
         dq = jnp.dot(grad_score, k, preferred_element_type=jnp.float32) * SCALE
         gl_ref[0, 0, :, cols] = (g.astype(jnp.float32) + dq).astype(jnp.bfloat16)
         dk_h = lax.dot_general(grad_score, q, TN, preferred_element_type=jnp.float32)
@@ -106,7 +145,7 @@
     dv_ref[0] = dv[rows:]
 
 
-def layer_call(queries, kv_own, kv_halo, grad_t, allowed_i32, grad_prev, micro,
+def layer_call(queries, kv_own, kv_halo, grad_t, prob, out, grad_prev, micro,
                blocks_per_kv, interpret=False):
     _, micro_count, rows, width = queries.shape
     kv_heads = kv_own.shape[4] // DH
@@ -119,23 +158,30 @@
         (1, rows, bw), lambda i, g: ((g * blocks_per_kv) * micro_count + micro, 0, 0))
     gb_spec = pl.BlockSpec(
         (1, rows, bw), lambda i, g: ((g * blocks_per_kv + 1) * micro_count + micro, 0, 0))
+    p_spec = pl.BlockSpec((1, group, rows, 2 * rows), lambda i, g: (micro, g, 0, 0))
+    o_spec = pl.BlockSpec((1, group, rows, DH), lambda i, g: (micro, g, 0, 0))
     own_out = pl.BlockSpec((1, rows, DH), lambda i, g: (0, 0, g))
     own_shape = jax.ShapeDtypeStruct((1, rows, kv_heads * DH), jnp.float32)
+    in_specs = [q_spec, kv_spec, kv_spec, ga_spec, gb_spec, p_spec, o_spec]
+    operands = [queries, kv_own, kv_halo, grad_t, grad_t, prob, out]
+    aliases = {}
+    if grad_prev is not None:
+        in_specs.append(pl.BlockSpec(memory_space=pl.ANY))
+        operands.append(grad_prev)
+        aliases = {len(operands) - 1: 3}
     return pl.pallas_call(
         layer_kernel,
         grid=(1, kv_heads),
-        in_specs=[q_spec, kv_spec, kv_spec, ga_spec, gb_spec,
-                  pl.BlockSpec((1, rows, 2 * rows), lambda i, g: (micro, 0, 0)),
-                  pl.BlockSpec(memory_space=pl.ANY)],
+        in_specs=in_specs,
         out_specs=[own_out, own_out,
                    pl.BlockSpec((2, 1, rows, DH), lambda i, g: (0, 0, 0, g)),
                    q_spec],
         out_shape=[own_shape, own_shape,
                    jax.ShapeDtypeStruct((2, 1, rows, kv_heads * DH), jnp.bfloat16),
                    jax.ShapeDtypeStruct(queries.shape, jnp.bfloat16)],
-        input_output_aliases={6: 3},
+        input_output_aliases=aliases,
         interpret=interpret,
-    )(queries, kv_own, kv_halo, grad_t, grad_t, allowed_i32, grad_prev)
+    )(*operands)
 
 
 def device_body(queries, keys, values, out_grad, segments):
@@ -187,7 +233,7 @@
         )
         kv_send.append(split.reshape(section_count, row_count, DH))
     sent = lax.all_to_all(jnp.concatenate([query_send] + kv_send, axis=-1), "pipe", 0, 0)
-    sent, kv_halo = lax.optimization_barrier((sent, kv_halo))
+    prob, out = layer_pre_call(queries, kv_own, kv_halo, masks)
     split_at = section_count // 2
     halo_hi = from_behind(sent[split_at:, :, block_width:], "seq", 1)
     halo_lo = from_behind(sent[:split_at, :, block_width:], "seq", 1)
@@ -200,12 +246,12 @@
     grads_above = jnp.concatenate([grads_lo[1:], grads_hi, grad_top[None]], axis=0)
     grad_t = lax.all_to_all(grads_above, "pipe", 0, 0)
 
-    query_all = jnp.zeros(queries.shape, jnp.bfloat16)
+    query_all = None
     key_parts = []
     value_parts = []
     for micro in range(micro_count):
         key_own_grad, value_own_grad, kv_back, query_all = layer_call(
-            queries, kv_own, kv_halo, grad_t, masks, query_all, micro, blocks_per_kv
+            queries, kv_own, kv_halo, grad_t, prob, out, query_all, micro, blocks_per_kv
         )
         kv_next = from_behind(kv_back, "seq", -1)
         key_parts.append(key_own_grad + kv_next[0].astype(jnp.float32))

time: 132 us -> 129 us (0.977)
  the two profiles are of different devices: /device:TPU:97 before, /device:TPU:99 now
where the time goes in v6:
time: 129 us; the launch traced here: 128 us
  waiting for transfers between devices  43.6 us (34%)
  Pallas kernels  37.5 us (29%)
  starting transfers between devices  32.5 us (25%)
  local copies, waits for them, and re-layouts  8.18 us (6%)
  other arithmetic  4.99 us (4%)
    all_to_all x1, waiting for transfers between devices, device_body(): lax.all_to_all(jnp.concatenate([query_send] + kv_send, axis=-1), 'pipe',...  26.4 us
    ppermute x5, starting transfers between devices, from_behind(): return lax.ppermute(block, axis, route)  17.5 us
    ppermute x5, waiting for transfers between devices, from_behind(): return lax.ppermute(block, axis, route)  17.1 us
    pallas_call x2, Pallas kernels, chain_call(): pl.pallas_call(functools.partial(chain_kernel, first=first), out_shape=(j...  14.5 us
    pallas_call x2, Pallas kernels, layer_call(): pl.pallas_call(layer_kernel, grid=(1, kv_heads), in_specs=in_specs, out_s...  13.2 us
    pallas_call x1, Pallas kernels, layer_pre_call(): pl.pallas_call(layer_pre_kernel, grid=(micro_count, kv_heads), in_specs=[...  9.81 us
    all_to_all x1, starting transfers between devices, device_body(): grad_t = lax.all_to_all(grads_above, 'pipe', 0, 0)  7.92 us
    all_to_all x1, starting transfers between devices, device_body(): lax.all_to_all(jnp.concatenate([query_send] + kv_send, axis=-1), 'pipe',...  7.05 us
  transfers between devices with their start and end apart: 7, of which 4 were waited for; matrix products, arithmetic and copies ran while one was open for 1% of the time, Pallas kernels for 19%

profile of v6, /device:TPU:99, one launch (start us, length us, event | category | flops | bytes accessed | tf_op | source)
XLA Modules:
  0.0 127.7 jit_solution(694160617284173841)
XLA Ops:
  0.6 0.0 copy-start
  0.6 0.0 copy-start.8
  0.7 1.6 %copy.12 = bf16[32,8,8,256]{3,2,1,0:T(8,128)(2,1)S(1)} copy(bf16[32,8,8,256]{3,1,2,0:T(8,128)(2,1)} %bitcast.50) | data formatting | bytes 2097152
  2.3 0.0 copy-start.6
  2.3 0.2 copy.9
  2.5 0.0 copy-done.8
  2.5 0.1 reshape_squeeze.10
  2.7 0.6 copy-done.6
  3.2 0.1 reshape_squeeze.11
  3.4 0.1 broadcast_in_dim.4
  3.5 0.1 broadcast_in_dim.5
  3.6 1.6 %pad_maximum_fusion = bf16[16,128,512]{2,1,0:T(8,128)(2,1)} fusion(bf16[16,128,128]{2,1,0:T(8,128)(2,1)S(1)} %bitcast.54, bf16[16,128,128]{2,1,0:T(8,128)(2,1)S(1)} %bitcast.53, bf16[16,128,256]{2,1,0:T(8,128)(2,1)S(1)} %bitcast.52), kind=kLoop, calls=%fused_computation | loop fusion | flops 6291456 | bytes 4194304 | tf_op jit(solution)/shard_map/concatenate | solution.py:235
  5.2 0.0 copy-start.13
  5.2 7.0 %all-to-all-start = ((bf16[16,128,512]{2,1,0:T(8,128)(2,1)}), bf16[16,128,512]{2,1,0:T(8,128)(2,1)S(1)}, u32[]{:S(2)}, u32[]{:S(2)}) async-start(bf16[16,128,512]{2,1,0:T(8,128)(2,1)} %pad_maximum_fusion), calls=%async_computation | async-start | bytes 4194304 | tf_op jit(solution)/shard_map/all_to_all | solution.py:235
  12.2 0.0 copy-done.13
  12.3 0.0 copy-done
  12.3 0.7 fusion.11.g0_ref
  13.0 26.4 %all-to-all-done.x_ref = bf16[16,128,512]{2,1,0:T(8,128)(2,1)S(1)} async-done(((bf16[16,128,512]{2,1,0:T(8,128)(2,1)}), bf16[16,128,512]{2,1,0:T(8,128)(2,1)S(1)}, u32[]{:S(2)}, u32[]{:S(2)}) %all-to-all-start) | async-done | bytes 2097184 | tf_op jit(solution)/shard_map/all_to_all | solution.py:235
  39.4 0.0 copy-start.2
  39.4 1.0 fusion.10
  40.4 5.8 %collective-permute-start.2 = (bf16[8,128,256]{2,1,0:T(8,128)(2,1)S(1)}, bf16[8,128,256]{2,1,0:T(8,128)(2,1)}, u32[]{:S(2)}, u32[]{:S(2)}) collective-permute-start(bf16[8,128,256]{2,1,0:T(8,128)(2,1)S(1)} %get-tuple-element.30), channel_id=1, source_target_pairs={{0,1},{1,2},{2,3},{3,4},{4,5},{5,6},{6,7},{7,8},{8,9},{9,10},{10,1... | collective-permute-start | bytes 1572872 | tf_op jit(solution)/shard_map/ppermute | solution.py:20
  46.2 1.9 %collective-permute-start.1 = (bf16[8,128,256]{2,1,0:T(8,128)(2,1)}, bf16[8,128,256]{2,1,0:T(8,128)(2,1)}, u32[]{:S(2)}, u32[]{:S(2)}) collective-permute-start(bf16[8,128,256]{2,1,0:T(8,128)(2,1)} %get-tuple-element.29), channel_id=1, source_target_pairs={{0,1},{1,2},{2,3},{3,4},{4,5},{5,6},{6,7},{7,8},{8,9},{9,10},{10,1... | collective-permute-start | bytes 1572872 | tf_op jit(solution)/shard_map/ppermute | solution.py:20
  48.1 0.1 fusion.9
  48.2 0.1 and_convert_fusion.m_ref
  48.4 0.0 copy-start.5
  48.4 0.7 dynamic-slice_bitcast_fusion.m_ref
  49.1 3.2 %collective-permute-done.2.halo_ref = bf16[8,128,256]{2,1,0:T(8,128)(2,1)} collective-permute-done((bf16[8,128,256]{2,1,0:T(8,128)(2,1)S(1)}, bf16[8,128,256]{2,1,0:T(8,128)(2,1)}, u32[]{:S(2)}, u32[]{:S(2)}) %collective-permute-start.2) | collective-permute-done | bytes 524320 | tf_op jit(solution)/shard_map/ppermute | solution.py:20
  52.3 0.0 copy-done.2
  52.3 7.2 %shard_map.76 = (bf16[8,128,256]{2,1,0:T(8,128)(2,1)}, bf16[128,256]{1,0:T(8,128)(2,1)}) custom-call(bf16[16,128,512]{2,1,0:T(8,128)(2,1)} %copy-done.2, bf16[8,128,256]{2,1,0:T(8,128)(2,1)} %collective-permute-done.2.halo_ref, bf16[128,256]{1,0:T(8,128)(2,1)} %fusion.11.g0_ref, s32[128,256]{1,0:T(8,128)} %dynamic-slice_bitcast_fusion.m_ref), custom_call_target="tpu_custom_call" | custom-call | tf_op jit(solution)/shard_map/pallas_call | solution.py:70
  59.5 0.0 copy-start.10
  59.5 0.0 collective-permute-done.1.halo_ref
  59.6 7.2 %shard_map.77 = (bf16[8,128,256]{2,1,0:T(8,128)(2,1)}, bf16[128,256]{1,0:T(8,128)(2,1)}) custom-call(bf16[16,128,512]{2,1,0:T(8,128)(2,1)} %copy-done.2, bf16[8,128,256]{2,1,0:T(8,128)(2,1)} %collective-permute-done.1.halo_ref, bf16[128,256]{1,0:T(8,128)(2,1)} %get-tuple-element.16.g0_ref, s32[128,256]{1,0:T(8,128)} %dynamic-slice_bitcast_fusion.m_ref), custom_call_target="tpu_custom_call" | custom-call | tf_op jit(solution)/shard_map/pallas_call | solution.py:70
  66.8 0.0 copy-done.5
  66.8 1.0 slice.23
  67.9 0.0 copy-done.10
  67.9 0.0 copy-start.7
  67.9 0.0 copy-start.9
  67.9 1.1 pad_maximum_fusion.1
  69.0 7.9 %all-to-all-start.1 = ((bf16[16,128,256]{2,1,0:T(8,128)(2,1)}), bf16[16,128,256]{2,1,0:T(8,128)(2,1)S(1)}, u32[]{:S(2)}, u32[]{:S(2)}) async-start(bf16[16,128,256]{2,1,0:T(8,128)(2,1)} %pad_maximum_fusion.1), calls=%async_computation.1 | async-start | bytes 2097152 | tf_op jit(solution)/shard_map/all_to_all | solution.py:247
  76.9 0.0 copy-done.7
  76.9 0.0 copy-done.9
  76.9 0.1 pad_maximum_fusion.2.kvo_ref
  77.0 0.0 copy-start.3
  77.0 6.0 %collective-permute-start = (bf16[2,1,2,128,512]{4,3,2,1,0:T(8,128)(2,1)S(1)}, bf16[2,1,2,128,512]{4,3,2,1,0:T(8,128)(2,1)S(1)}, u32[]{:S(2)}, u32[]{:S(2)}) collective-permute-start(bf16[2,1,2,128,512]{4,3,2,1,0:T(8,128)(2,1)S(1)} %pad_maximum_fusion.2.kvo_ref), channel_id=1, source_target_pairs={{0,1},{1,2},{2,3},{3,4},{4,5},{5,6},{6,7},{7,8},{8,9},{9,10},{10,1... | collective-permute-start | bytes 1572872 | tf_op jit(solution)/shard_map/ppermute | solution.py:20
  83.0 6.1 %collective-permute-done.kvh_ref = bf16[2,1,2,128,512]{4,3,2,1,0:T(8,128)(2,1)S(1)} collective-permute-done((bf16[2,1,2,128,512]{4,3,2,1,0:T(8,128)(2,1)S(1)}, bf16[2,1,2,128,512]{4,3,2,1,0:T(8,128)(2,1)S(1)}, u32[]{:S(2)}, u32[]{:S(2)}) %collective-permute-start) | collective-permute-done | bytes 524320 | tf_op jit(solution)/shard_map/ppermute | solution.py:20
  89.1 0.0 copy-done.3
  89.1 0.0 copy-start.4
  89.1 0.8 copy-done.4
  89.9 9.8 %shard_map.78 = (f32[2,16,128,256]{3,2,1,0:T(8,128)}, f32[2,16,128,128]{3,2,1,0:T(8,128)}) custom-call(bf16[1,2,128,2048]{3,2,1,0:T(8,128)(2,1)} %q_ref.5, bf16[2,1,2,128,512]{4,3,2,1,0:T(8,128)(2,1)} %copy-done.3, bf16[2,1,2,128,512]{4,3,2,1,0:T(8,128)(2,1)} %copy-done.4, s32[2,128,256]{2,1,0:T(8,128)} %copy-done.5), custom_call_target="tpu_custom_call" | custom-call | tf_op jit(solution)/shard_map/pallas_call | solution.py:101
  99.7 0.0 all-to-all-done.1.ga_ref.gb_ref
  99.8 1.0 copy-done.1
  100.7 6.6 %shard_map.79 = (f32[1,128,512]{2,1,0:T(8,128)}, f32[1,128,512]{2,1,0:T(8,128)}, bf16[2,1,128,512]{3,2,1,0:T(8,128)(2,1)}, bf16[1,2,128,2048]{3,2,1,0:T(8,128)(2,1)}) custom-call(bf16[1,2,128,2048]{3,2,1,0:T(8,128)(2,1)} %q_ref.5, bf16[2,1,2,128,512]{4,3,2,1,0:T(8,128)(2,1)} %copy-done.3, bf16[2,1,2,128,512]{4,3,2,1,0:T(8,128)(2,1)} %copy-done.4, ...), custom_call_target="tpu_custom_call" | custom-call | tf_op jit(solution)/shard_map/pallas_call | solution.py:172
  107.3 1.9 %collective-permute-start.3 = (bf16[2,1,128,512]{3,2,1,0:T(8,128)(2,1)}, bf16[2,1,128,512]{3,2,1,0:T(8,128)(2,1)S(1)}, u32[]{:S(2)}, u32[]{:S(2)}) collective-permute-start(bf16[2,1,128,512]{3,2,1,0:T(8,128)(2,1)} %get-tuple-element.24), channel_id=1, source_target_pairs={{1,0},{2,1},{3,2},{4,3},{5,4},{6,5},{7,6},{8,7},{9,8},{10,9},{11,1... | collective-permute-start | bytes 786440 | tf_op jit(solution)/shard_map/ppermute | solution.py:20
  109.2 0.0 copy-start.11
  109.2 0.0 copy-start.12
  109.2 6.6 %shard_map.80 = (f32[1,128,512]{2,1,0:T(8,128)}, f32[1,128,512]{2,1,0:T(8,128)}, bf16[2,1,128,512]{3,2,1,0:T(8,128)(2,1)}, bf16[1,2,128,2048]{3,2,1,0:T(8,128)(2,1)}) custom-call(bf16[1,2,128,2048]{3,2,1,0:T(8,128)(2,1)} %q_ref.5, bf16[2,1,2,128,512]{4,3,2,1,0:T(8,128)(2,1)} %copy-done.3, ...), custom_call_target="tpu_custom_call", output_to_operand_aliasing={{3}: (7, {})} | custom-call | tf_op jit(solution)/shard_map/pallas_call | solution.py:172
  115.9 1.9 %collective-permute-start.4 = (bf16[2,1,128,512]{3,2,1,0:T(8,128)(2,1)}, bf16[2,1,128,512]{3,2,1,0:T(8,128)(2,1)S(1)}, u32[]{:S(2)}, u32[]{:S(2)}) collective-permute-start(bf16[2,1,128,512]{3,2,1,0:T(8,128)(2,1)} %get-tuple-element.26), channel_id=1, source_target_pairs={{1,0},{2,1},{3,2},{4,3},{5,4},{6,5},{7,6},{8,7},{9,8},{10,9},{11,1... | collective-permute-start | bytes 786440 | tf_op jit(solution)/shard_map/ppermute | solution.py:20
  117.8 0.0 collective-permute-done.3
  117.8 0.0 copy-done.11
  117.8 0.0 copy-done.12
  117.8 0.1 fusion.6
  117.9 7.8 %collective-permute-done.4 = bf16[2,1,128,512]{3,2,1,0:T(8,128)(2,1)S(1)} collective-permute-done((bf16[2,1,128,512]{3,2,1,0:T(8,128)(2,1)}, bf16[2,1,128,512]{3,2,1,0:T(8,128)(2,1)S(1)}, u32[]{:S(2)}, u32[]{:S(2)}) %collective-permute-start.4) | collective-permute-done | bytes 262176 | tf_op jit(solution)/shard_map/ppermute | solution.py:20
  125.7 1.1 fusion.7
  126.8 0.8 pad_maximum_fusion.3
  (9 shorter events, 0.1 us)
Async XLA Ops:
  0.6 11.7 %copy-start = (bf16[2,128,2048]{2,1,0:T(8,128)(2,1)S(1)}, bf16[2,128,2048]{2,1,0:T(8,128)(2,1)}, u32[]{:S(2)}) copy-start(bf16[2,128,2048]{2,1,0:T(8,128)(2,1)} %param.8) | copy-start | bytes 3145732
  0.6 1.9 %copy-start.8 = (bf16[1,2,128,512]{3,2,1,0:T(8,128)(2,1)S(1)}, bf16[1,2,128,512]{3,2,1,0:T(8,128)(2,1)}, u32[]{:S(2)}) copy-start(bf16[1,2,128,512]{3,2,1,0:T(8,128)(2,1)} %param.6) | copy-start | bytes 786436
  2.3 1.0 copy-start.6
  5.2 7.1 %copy-start.13 = (s32[2,4096]{1,0:T(2,128)S(1)}, s32[2,4096]{1,0:T(2,128)}, u32[]{:S(2)}) copy-start(s32[2,4096]{1,0:T(2,128)} %param.9) | copy-start | bytes 98308
  5.2 34.3 %all-to-all-start = ((bf16[16,128,512]{2,1,0:T(8,128)(2,1)}), bf16[16,128,512]{2,1,0:T(8,128)(2,1)S(1)}, u32[]{:S(2)}, u32[]{:S(2)}) async-start(bf16[16,128,512]{2,1,0:T(8,128)(2,1)} %pad_maximum_fusion), calls=%async_computation | async-start | bytes 4194304 | tf_op jit(solution)/shard_map/all_to_all | solution.py:235
  39.4 12.9 %copy-start.2 = (bf16[16,128,512]{2,1,0:T(8,128)(2,1)}, bf16[16,128,512]{2,1,0:T(8,128)(2,1)S(1)}, u32[]{:S(2)}) copy-start(bf16[16,128,512]{2,1,0:T(8,128)(2,1)S(1)} %all-to-all-done.x_ref) | copy-start | bytes 6291460
  40.4 11.9 %collective-permute-start.2 = (bf16[8,128,256]{2,1,0:T(8,128)(2,1)S(1)}, bf16[8,128,256]{2,1,0:T(8,128)(2,1)}, u32[]{:S(2)}, u32[]{:S(2)}) collective-permute-start(bf16[8,128,256]{2,1,0:T(8,128)(2,1)S(1)} %get-tuple-element.30), channel_id=1, source_target_pairs={{0,1},{1,2},{2,3},{3,4},{4,5},{5,6},{6,7},{7,8},{8,9},{9,10},{10,1... | collective-permute-start | bytes 1572872 | tf_op jit(solution)/shard_map/ppermute | solution.py:20
  46.2 13.3 %collective-permute-start.1 = (bf16[8,128,256]{2,1,0:T(8,128)(2,1)}, bf16[8,128,256]{2,1,0:T(8,128)(2,1)}, u32[]{:S(2)}, u32[]{:S(2)}) collective-permute-start(bf16[8,128,256]{2,1,0:T(8,128)(2,1)} %get-tuple-element.29), channel_id=1, source_target_pairs={{0,1},{1,2},{2,3},{3,4},{4,5},{5,6},{6,7},{7,8},{8,9},{9,10},{10,1... | collective-permute-start | bytes 1572872 | tf_op jit(solution)/shard_map/ppermute | solution.py:20
  48.4 18.4 %copy-start.5 = (s32[2,128,256]{2,1,0:T(8,128)}, s32[2,128,256]{2,1,0:T(8,128)S(1)}, u32[]{:S(2)}) copy-start(s32[2,128,256]{2,1,0:T(8,128)S(1)} %and_convert_fusion.m_ref) | copy-start | bytes 786436
  59.5 8.3 %copy-start.10 = (bf16[8,128,256]{2,1,0:T(8,128)(2,1)S(1)}, bf16[8,128,256]{2,1,0:T(8,128)(2,1)}, u32[]{:S(2)}) copy-start(bf16[8,128,256]{2,1,0:T(8,128)(2,1)} %get-tuple-element.18) | copy-start | bytes 1572868
  67.9 9.0 %copy-start.7 = (bf16[1,2,128,512]{3,2,1,0:T(8,128)(2,1)S(1)}, bf16[1,2,128,512]{3,2,1,0:T(8,128)(2,1)}, u32[]{:S(2)}) copy-start(bf16[1,2,128,512]{3,2,1,0:T(8,128)(2,1)} %param.7) | copy-start | bytes 786436
  67.9 9.0 %copy-start.9 = (bf16[1,2,128,512]{3,2,1,0:T(8,128)(2,1)S(1)}, bf16[1,2,128,512]{3,2,1,0:T(8,128)(2,1)}, u32[]{:S(2)}) copy-start(bf16[1,2,128,512]{3,2,1,0:T(8,128)(2,1)} %param.6) | copy-start | bytes 786436
  69.0 30.8 %all-to-all-start.1 = ((bf16[16,128,256]{2,1,0:T(8,128)(2,1)}), bf16[16,128,256]{2,1,0:T(8,128)(2,1)S(1)}, u32[]{:S(2)}, u32[]{:S(2)}) async-start(bf16[16,128,256]{2,1,0:T(8,128)(2,1)} %pad_maximum_fusion.1), calls=%async_computation.1 | async-start | bytes 2097152 | tf_op jit(solution)/shard_map/all_to_all | solution.py:247
  77.0 12.1 %copy-start.3 = (bf16[2,1,2,128,512]{4,3,2,1,0:T(8,128)(2,1)}, bf16[2,1,2,128,512]{4,3,2,1,0:T(8,128)(2,1)S(1)}, u32[]{:S(2)}) copy-start(bf16[2,1,2,128,512]{4,3,2,1,0:T(8,128)(2,1)S(1)} %pad_maximum_fusion.2.kvo_ref) | copy-start | bytes 1572868
  77.0 12.1 %collective-permute-start = (bf16[2,1,2,128,512]{4,3,2,1,0:T(8,128)(2,1)S(1)}, bf16[2,1,2,128,512]{4,3,2,1,0:T(8,128)(2,1)S(1)}, u32[]{:S(2)}, u32[]{:S(2)}) collective-permute-start(bf16[2,1,2,128,512]{4,3,2,1,0:T(8,128)(2,1)S(1)} %pad_maximum_fusion.2.kvo_ref), channel_id=1, source_target_pairs={{0,1},{1,2},{2,3},{3,4},{4,5},{5,6},{6,7},{7,8},{8,9},{9,10},{10,1... | collective-permute-start | bytes 1572872 | tf_op jit(solution)/shard_map/ppermute | solution.py:20
  89.1 0.8 copy-start.4
  99.7 1.0 copy-start.1
  107.3 10.5 %collective-permute-start.3 = (bf16[2,1,128,512]{3,2,1,0:T(8,128)(2,1)}, bf16[2,1,128,512]{3,2,1,0:T(8,128)(2,1)S(1)}, u32[]{:S(2)}, u32[]{:S(2)}) collective-permute-start(bf16[2,1,128,512]{3,2,1,0:T(8,128)(2,1)} %get-tuple-element.24), channel_id=1, source_target_pairs={{1,0},{2,1},{3,2},{4,3},{5,4},{6,5},{7,6},{8,7},{9,8},{10,9},{11,1... | collective-permute-start | bytes 786440 | tf_op jit(solution)/shard_map/ppermute | solution.py:20
  109.2 8.6 %copy-start.11 = (f32[1,128,512]{2,1,0:T(8,128)S(1)}, f32[1,128,512]{2,1,0:T(8,128)}, u32[]{:S(2)}) copy-start(f32[1,128,512]{2,1,0:T(8,128)} %get-tuple-element.23) | copy-start | bytes 786436
  109.2 8.6 %copy-start.12 = (f32[1,128,512]{2,1,0:T(8,128)S(1)}, f32[1,128,512]{2,1,0:T(8,128)}, u32[]{:S(2)}) copy-start(f32[1,128,512]{2,1,0:T(8,128)} %get-tuple-element.27) | copy-start | bytes 786436
  115.9 9.9 %collective-permute-start.4 = (bf16[2,1,128,512]{3,2,1,0:T(8,128)(2,1)}, bf16[2,1,128,512]{3,2,1,0:T(8,128)(2,1)S(1)}, u32[]{:S(2)}, u32[]{:S(2)}) collective-permute-start(bf16[2,1,128,512]{3,2,1,0:T(8,128)(2,1)} %get-tuple-element.26), channel_id=1, source_target_pairs={{1,0},{2,1},{3,2},{4,3},{5,4},{6,5},{7,6},{8,7},{9,8},{10,9},{11,1... | collective-permute-start | bytes 786440 | tf_op jit(solution)/shard_map/ppermute | solution.py:20

commit v7 on v6

--- a/solution.py
+++ b/solution.py
@@ -34,15 +34,25 @@
     return prob_low, grad_score
 
 
-def chain_kernel(x_ref, halo_ref, g0_ref, m_ref, o_ref, g_out_ref, *, first):
-    layers = halo_ref.shape[0]
+def chain_kernel(x_ref, halo_ref, g0_ref, m_ref, *rest, first, count):
+    if len(rest) == 3:
+        prev_ref, o_ref, g_out_ref = rest
+    else:
+        prev_ref = None
+        o_ref, g_out_ref = rest
     width = o_ref.shape[2]
     heads = width // DH
+    halo_first = first + count - halo_ref.shape[0]
     allowed = m_ref[...] != 0
+    if prev_ref is None:
+        o_ref[o_ref.shape[0] - 1] = g0_ref[...]
+    else:
+        top = first + count - 1
+        o_ref[top:] = prev_ref[top:]
 
     def step(i, g):
-        local = layers - 1 - i
-        layer = first + local
+        layer = first + count - 1 - i
+        local = layer - halo_first
         k = jnp.concatenate(
             [halo_ref[local, :, :DH], x_ref[layer, :, width:width + DH]], axis=0
         )
@@ -58,23 +68,60 @@
             dq = jnp.dot(grad_score, k, preferred_element_type=jnp.float32) * SCALE
             outs.append((gh.astype(jnp.float32) + dq).astype(jnp.bfloat16))
         g_new = jnp.concatenate(outs, axis=-1) if heads > 1 else outs[0]
-        o_ref[local] = g_new
+        o_ref[layer - 1] = g_new
         return g_new
 
-    g_out_ref[...] = lax.fori_loop(0, layers, step, g0_ref[...], unroll=True)
-
-
-def chain_call(sent, halo, grad_top, allowed_i32, first, interpret=False):
-    layers, rows, _ = halo.shape
+    g_out_ref[...] = lax.fori_loop(0, count, step, g0_ref[...], unroll=True)
+
+
+def chain_call(sent, halo, grad_top, allowed_i32, first, count, prev=None, interpret=False):
+    layers, rows, _ = sent.shape
     width = grad_top.shape[1]
+    operands = [sent, halo, grad_top, allowed_i32]
+    if prev is not None:
+        operands.append(prev)
     return pl.pallas_call(
-        functools.partial(chain_kernel, first=first),
+        functools.partial(chain_kernel, first=first, count=count),
         out_shape=(
             jax.ShapeDtypeStruct((layers, rows, width), jnp.bfloat16),
             jax.ShapeDtypeStruct((rows, width), jnp.bfloat16),
         ),
         interpret=interpret,
-    )(sent, halo, grad_top, allowed_i32)
+    )(*operands)
+
+
+def pack_kernel(q_ref, k_ref, v_ref, send_ref, kv_ref, *, blocks_per_kv):
+    blocks, _, total = send_ref.shape
+    bw = total - 2 * DH
+    q = q_ref[0, 0]
+    k = k_ref[0, 0]
+    v = v_ref[0, 0]
+    for b in range(blocks):
+        g = b // blocks_per_kv
+        send_ref[b, :, :bw] = q[:, b * bw:(b + 1) * bw]
+        send_ref[b, :, bw:bw + DH] = k[:, g * DH:(g + 1) * DH]
+        send_ref[b, :, bw + DH:] = v[:, g * DH:(g + 1) * DH]
+    kv_ref[0, 0, 0] = k
+    kv_ref[1, 0, 0] = v
+
+
+def pack_call(queries, keys, values, head_blocks, blocks_per_kv, interpret=False):
+    _, micro_count, rows, width = queries.shape
+    key_width = keys.shape[3]
+    bw = width // head_blocks
+    kv_in = pl.BlockSpec((1, 1, rows, key_width), lambda m: (0, m, 0, 0))
+    return pl.pallas_call(
+        functools.partial(pack_kernel, blocks_per_kv=blocks_per_kv),
+        grid=(micro_count,),
+        in_specs=[pl.BlockSpec((1, 1, rows, width), lambda m: (0, m, 0, 0)), kv_in, kv_in],
+        out_specs=[pl.BlockSpec((head_blocks, rows, bw + 2 * DH), lambda m: (m, 0, 0)),
+                   pl.BlockSpec((2, 1, 1, rows, key_width), lambda m: (0, 0, m, 0, 0))],
+        out_shape=[
+            jax.ShapeDtypeStruct((micro_count * head_blocks, rows, bw + 2 * DH), jnp.bfloat16),
+            jax.ShapeDtypeStruct((2,) + keys.shape, jnp.bfloat16),
+        ],
+        interpret=interpret,
+    )(queries, keys, values)
 
 
 def layer_pre_kernel(q_ref, kvo_ref, kvh_ref, m_ref, p_ref, o_ref):
@@ -147,17 +194,18 @@
 
 def layer_call(queries, kv_own, kv_halo, grad_t, prob, out, grad_prev, micro,
                blocks_per_kv, interpret=False):
-    _, micro_count, rows, width = queries.shape
+    _, _, rows, width = queries.shape
     kv_heads = kv_own.shape[4] // DH
     group = width // (kv_heads * DH)
     gw = group * DH
     bw = grad_t.shape[2]
     kv_spec = pl.BlockSpec((2, 1, 1, rows, DH), lambda i, g: (0, 0, micro, 0, g))
     q_spec = pl.BlockSpec((1, 1, rows, gw), lambda i, g: (0, micro, 0, g))
+    head_blocks = width // bw
     ga_spec = pl.BlockSpec(
-        (1, rows, bw), lambda i, g: ((g * blocks_per_kv) * micro_count + micro, 0, 0))
+        (1, rows, bw), lambda i, g: (micro * head_blocks + g * blocks_per_kv, 0, 0))
     gb_spec = pl.BlockSpec(
-        (1, rows, bw), lambda i, g: ((g * blocks_per_kv + 1) * micro_count + micro, 0, 0))
+        (1, rows, bw), lambda i, g: (micro * head_blocks + g * blocks_per_kv + 1, 0, 0))
     p_spec = pl.BlockSpec((1, group, rows, 2 * rows), lambda i, g: (micro, g, 0, 0))
     o_spec = pl.BlockSpec((1, group, rows, DH), lambda i, g: (micro, g, 0, 0))
     own_out = pl.BlockSpec((1, rows, DH), lambda i, g: (0, 0, g))
@@ -199,10 +247,7 @@
     block_heads = q_heads // head_blocks
     block_width = block_heads * DH
     blocks_per_kv = group_size // block_heads
-    own_query = queries[0]
-    own_key = keys[0]
-    own_value = values[0]
-    kv_own = jnp.stack([keys, values])
+    send, kv_own = pack_call(queries, keys, values, head_blocks, blocks_per_kv)
     seg_padded = jnp.concatenate(
         [jnp.full((micro_count, row_count), -1, jnp.int32), segments], axis=1
     )
@@ -220,30 +265,20 @@
     masks = (near[None] & (seg_query[:, :, None] == seg_key[:, None, :])).astype(jnp.int32)
     kv_halo = from_behind(kv_own, "seq", 1)
 
-    my_block = section_index // micro_count
-    my_micro = section_index % micro_count
-    query_send = jnp.transpose(
-        own_query.reshape(micro_count, row_count, head_blocks, block_width), (2, 0, 1, 3)
-    ).reshape(section_count, row_count, block_width)
-    kv_send = []
-    for rows in (own_key, own_value):
-        split = jnp.transpose(rows.reshape(micro_count, row_count, kv_heads, DH), (2, 0, 1, 3))
-        split = jnp.broadcast_to(
-            split[:, None], (kv_heads, blocks_per_kv, micro_count, row_count, DH)
-        )
-        kv_send.append(split.reshape(section_count, row_count, DH))
-    sent = lax.all_to_all(jnp.concatenate([query_send] + kv_send, axis=-1), "pipe", 0, 0)
+    my_block = section_index % head_blocks
+    my_micro = section_index // head_blocks
+    sent = lax.all_to_all(send, "pipe", 0, 0)
     prob, out = layer_pre_call(queries, kv_own, kv_halo, masks)
     split_at = section_count // 2
     halo_hi = from_behind(sent[split_at:, :, block_width:], "seq", 1)
-    halo_lo = from_behind(sent[:split_at, :, block_width:], "seq", 1)
+    halo_lo = from_behind(sent[1:split_at, :, block_width:], "seq", 1)
     grad_top = lax.dynamic_slice(
         out_grad, (my_micro, 0, my_block * block_width), (1, row_count, block_width)
     )[0]
     allowed = lax.dynamic_index_in_dim(masks, my_micro, 0, keepdims=False)
-    grads_hi, grad_mid = chain_call(sent, halo_hi, grad_top, allowed, split_at)
-    grads_lo, _ = chain_call(sent, halo_lo, grad_mid, allowed, 0)
-    grads_above = jnp.concatenate([grads_lo[1:], grads_hi, grad_top[None]], axis=0)
+    above_hi, grad_mid = chain_call(
+        sent, halo_hi, grad_top, allowed, split_at, section_count - split_at)
+    grads_above, _ = chain_call(sent, halo_lo, grad_mid, allowed, 1, split_at - 1, above_hi)
     grad_t = lax.all_to_all(grads_above, "pipe", 0, 0)
 
     query_all = None

time: 129 us -> 124 us (0.961)
  the two profiles are of different devices: /device:TPU:99 before, /device:TPU:227 now
where the time goes in v7:
time: 124 us; the launch traced here: 123 us
  waiting for transfers between devices  42.8 us (35%)
  Pallas kernels  40.5 us (33%)
  starting transfers between devices  32.5 us (26%)
  local copies, waits for them, and re-layouts  4.11 us (3%)
  other arithmetic  2.23 us (2%)
    all_to_all x1, waiting for transfers between devices, device_body(): sent = lax.all_to_all(send, 'pipe', 0, 0)  26.4 us
    ppermute x5, starting transfers between devices, from_behind(): return lax.ppermute(block, axis, route)  17.5 us
    ppermute x5, waiting for transfers between devices, from_behind(): return lax.ppermute(block, axis, route)  16.4 us
    pallas_call x2, Pallas kernels, chain_call(): pl.pallas_call(functools.partial(chain_kernel, first=first, count=count),...  14.6 us
    pallas_call x2, Pallas kernels, layer_call(): pl.pallas_call(layer_kernel, grid=(1, kv_heads), in_specs=in_specs, out_s...  13.2 us
    pallas_call x1, Pallas kernels, layer_pre_call(): pl.pallas_call(layer_pre_kernel, grid=(micro_count, kv_heads), in_specs=[...  9.77 us
    all_to_all x1, starting transfers between devices, device_body(): grad_t = lax.all_to_all(grads_above, 'pipe', 0, 0)  7.91 us
    all_to_all x1, starting transfers between devices, device_body(): sent = lax.all_to_all(send, 'pipe', 0, 0)  7.05 us
  transfers between devices with their start and end apart: 7, of which 4 were waited for; matrix products, arithmetic and copies ran while one was open for 2% of the time, Pallas kernels for 19%

profile of v7, /device:TPU:227, one launch (start us, length us, event | category | flops | bytes accessed | tf_op | source)
XLA Modules:
  0.0 122.9 jit_solution(253875021452850854)
XLA Ops:
  0.6 0.0 copy-start
  0.6 2.9 %shard_map.76 = (bf16[16,128,512]{2,1,0:T(8,128)(2,1)}, bf16[2,1,2,128,512]{4,3,2,1,0:T(8,128)(2,1)}) custom-call(bf16[1,2,128,2048]{3,2,1,0:T(8,128)(2,1)} %q_ref.7, bf16[1,2,128,512]{3,2,1,0:T(8,128)(2,1)} %k_ref.1, bf16[1,2,128,512]{3,2,1,0:T(8,128)(2,1)} %v_ref.1), custom_call_target="tpu_custom_call" | custom-call | tf_op jit(solution)/shard_map/pallas_call | solution.py:113
  3.6 0.0 copy-start.8
  3.6 7.0 %all-to-all-start = ((bf16[16,128,512]{2,1,0:T(8,128)(2,1)}), bf16[16,128,512]{2,1,0:T(8,128)(2,1)S(1)}, u32[]{:S(2)}, u32[]{:S(2)}) async-start(bf16[16,128,512]{2,1,0:T(8,128)(2,1)} %get-tuple-element.19), calls=%async_computation | async-start | bytes 4194304 | tf_op jit(solution)/shard_map/all_to_all | solution.py:270
  10.6 0.0 copy-done
  10.7 0.7 dynamic-slice_bitcast_fusion.1.g0_ref
  11.3 0.1 fusion.9
  11.4 26.4 %all-to-all-done.x_ref = bf16[16,128,512]{2,1,0:T(8,128)(2,1)S(1)} async-done(((bf16[16,128,512]{2,1,0:T(8,128)(2,1)}), bf16[16,128,512]{2,1,0:T(8,128)(2,1)S(1)}, u32[]{:S(2)}, u32[]{:S(2)}) %all-to-all-start) | async-done | bytes 2097184 | tf_op jit(solution)/shard_map/all_to_all | solution.py:270
  37.8 0.0 copy-start.2
  37.9 5.8 %collective-permute-start.2 = (bf16[8,128,256]{2,1,0:T(8,128)(2,1)S(1)}, bf16[8,128,256]{2,1,0:T(8,128)(2,1)}, u32[]{:S(2)}, u32[]{:S(2)}) collective-permute-start(bf16[8,128,256]{2,1,0:T(8,128)(2,1)S(1)} %slice.25), channel_id=1, source_target_pairs={{0,1},{1,2},{2,3},{3,4},{4,5},{5,6},{6,7},{7,8},{8,9},{9,10},{10,1... | collective-permute-start | bytes 1572872 | tf_op jit(solution)/shard_map/ppermute | solution.py:20
  43.7 0.0 copy-done.8
  43.7 0.8 slice.24
  44.5 1.9 %collective-permute-start.1 = (bf16[7,128,256]{2,1,0:T(8,128)(2,1)}, bf16[7,128,256]{2,1,0:T(8,128)(2,1)}, u32[]{:S(2)}, u32[]{:S(2)}) collective-permute-start(bf16[7,128,256]{2,1,0:T(8,128)(2,1)} %slice.24), channel_id=1, source_target_pairs={{0,1},{1,2},{2,3},{3,4},{4,5},{5,6},{6,7},{7,8},{8,9},{9,10},{10,1... | collective-permute-start | bytes 1376264 | tf_op jit(solution)/shard_map/ppermute | solution.py:20
  46.4 0.1 and_convert_fusion.m_ref
  46.5 0.0 copy-start.5
  46.5 0.7 dynamic-slice_bitcast_fusion.m_ref
  47.3 2.5 %collective-permute-done.2.halo_ref = bf16[8,128,256]{2,1,0:T(8,128)(2,1)} collective-permute-done((bf16[8,128,256]{2,1,0:T(8,128)(2,1)S(1)}, bf16[8,128,256]{2,1,0:T(8,128)(2,1)}, u32[]{:S(2)}, u32[]{:S(2)}) %collective-permute-start.2) | collective-permute-done | bytes 524320 | tf_op jit(solution)/shard_map/ppermute | solution.py:20
  49.8 0.0 copy-done.2
  49.8 7.4 %shard_map.77 = (bf16[16,128,256]{2,1,0:T(8,128)(2,1)}, bf16[128,256]{1,0:T(8,128)(2,1)}) custom-call(bf16[16,128,512]{2,1,0:T(8,128)(2,1)} %copy-done.2, bf16[8,128,256]{2,1,0:T(8,128)(2,1)} %collective-permute-done.2.halo_ref, bf16[128,256]{1,0:T(8,128)(2,1)} %dynamic-slice_bitcast_fusion.1.g0_ref, s32[128,256]{1,0:T(8,128)} %dynamic-slice_bitcast_fusion.m_ref), custom_call_target="tpu_custom_call" | custom-call | tf_op jit(solution)/shard_map/pallas_call | solution.py:83
  57.1 0.0 collective-permute-done.1.halo_ref
  57.1 0.0 copy-start.3
  57.1 7.2 %shard_map.78 = (bf16[16,128,256]{2,1,0:T(8,128)(2,1)}, bf16[128,256]{1,0:T(8,128)(2,1)}) custom-call(bf16[16,128,512]{2,1,0:T(8,128)(2,1)} %copy-done.2, bf16[7,128,256]{2,1,0:T(8,128)(2,1)} %collective-permute-done.1.halo_ref, bf16[128,256]{1,0:T(8,128)(2,1)} %get-tuple-element.20.g0_ref, s32[128,256]{1,0:T(8,128)} %dynamic-slice_bitcast_fusion.m_ref, ...), custom_call_target="tpu_custom_call" | custom-call | tf_op jit(solution)/shard_map/pallas_call | solution.py:83
  64.4 0.0 copy-done.5
  64.4 7.9 %all-to-all-start.1 = ((bf16[16,128,256]{2,1,0:T(8,128)(2,1)}), bf16[16,128,256]{2,1,0:T(8,128)(2,1)S(1)}, u32[]{:S(2)}, u32[]{:S(2)}) async-start(bf16[16,128,256]{2,1,0:T(8,128)(2,1)} %get-tuple-element.22), calls=%async_computation.1 | async-start | bytes 2097152 | tf_op jit(solution)/shard_map/all_to_all | solution.py:282
  72.3 0.0 copy-done.3
  72.3 6.0 %collective-permute-start = (bf16[2,1,2,128,512]{4,3,2,1,0:T(8,128)(2,1)S(1)}, bf16[2,1,2,128,512]{4,3,2,1,0:T(8,128)(2,1)S(1)}, u32[]{:S(2)}, u32[]{:S(2)}) collective-permute-start(bf16[2,1,2,128,512]{4,3,2,1,0:T(8,128)(2,1)S(1)} %copy-done.3), channel_id=1, source_target_pairs={{0,1},{1,2},{2,3},{3,4},{4,5},{5,6},{6,7},{7,8},{8,9},{9,10},{10,1... | collective-permute-start | bytes 1572872 | tf_op jit(solution)/shard_map/ppermute | solution.py:20
  78.3 6.1 %collective-permute-done.kvh_ref = bf16[2,1,2,128,512]{4,3,2,1,0:T(8,128)(2,1)S(1)} collective-permute-done((bf16[2,1,2,128,512]{4,3,2,1,0:T(8,128)(2,1)S(1)}, bf16[2,1,2,128,512]{4,3,2,1,0:T(8,128)(2,1)S(1)}, u32[]{:S(2)}, u32[]{:S(2)}) %collective-permute-start) | collective-permute-done | bytes 524320 | tf_op jit(solution)/shard_map/ppermute | solution.py:20
  84.4 0.0 copy-start.4
  84.4 0.9 copy-done.4
  85.3 9.8 %shard_map.79 = (f32[2,16,128,256]{3,2,1,0:T(8,128)}, f32[2,16,128,128]{3,2,1,0:T(8,128)}) custom-call(bf16[1,2,128,2048]{3,2,1,0:T(8,128)(2,1)} %q_ref.7, bf16[2,1,2,128,512]{4,3,2,1,0:T(8,128)(2,1)} %get-tuple-element.18.kvo_ref, bf16[2,1,2,128,512]{4,3,2,1,0:T(8,128)(2,1)} %copy-done.4, s32[2,128,256]{2,1,0:T(8,128)} %copy-done.5), custom_call_target="tpu_custom_call" | custom-call | tf_op jit(solution)/shard_map/pallas_call | solution.py:148
  95.0 0.0 all-to-all-done.1.ga_ref.gb_ref
  95.0 0.0 copy-start.1
  95.0 1.0 copy-done.1
  96.0 6.5 %shard_map.80 = (f32[1,128,512]{2,1,0:T(8,128)}, f32[1,128,512]{2,1,0:T(8,128)}, bf16[2,1,128,512]{3,2,1,0:T(8,128)(2,1)}, bf16[1,2,128,2048]{3,2,1,0:T(8,128)(2,1)}) custom-call(bf16[1,2,128,2048]{3,2,1,0:T(8,128)(2,1)} %q_ref.7, bf16[2,1,2,128,512]{4,3,2,1,0:T(8,128)(2,1)} %get-tuple-element.18.kvo_ref, bf16[2,1,2,128,512]{4,3,2,1,0:T(8,128)(2,1)} %copy-done.4, ...), custom_call_target="tpu_custom_call" | custom-call | tf_op jit(solution)/shard_map/pallas_call | solution.py:220
  102.5 1.9 %collective-permute-start.3 = (bf16[2,1,128,512]{3,2,1,0:T(8,128)(2,1)}, bf16[2,1,128,512]{3,2,1,0:T(8,128)(2,1)S(1)}, u32[]{:S(2)}, u32[]{:S(2)}) collective-permute-start(bf16[2,1,128,512]{3,2,1,0:T(8,128)(2,1)} %get-tuple-element.28), channel_id=1, source_target_pairs={{1,0},{2,1},{3,2},{4,3},{5,4},{6,5},{7,6},{8,7},{9,8},{10,9},{11,1... | collective-permute-start | bytes 786440 | tf_op jit(solution)/shard_map/ppermute | solution.py:20
  104.5 0.0 copy-start.6
  104.5 0.0 copy-start.7
  104.5 6.6 %shard_map.81 = (f32[1,128,512]{2,1,0:T(8,128)}, f32[1,128,512]{2,1,0:T(8,128)}, bf16[2,1,128,512]{3,2,1,0:T(8,128)(2,1)}, bf16[1,2,128,2048]{3,2,1,0:T(8,128)(2,1)}) custom-call(bf16[1,2,128,2048]{3,2,1,0:T(8,128)(2,1)} %q_ref.7, bf16[2,1,2,128,512]{4,3,2,1,0:T(8,128)(2,1)} %get-tuple-element.18.kvo_ref, ...), custom_call_target="tpu_custom_call", output_to_operand_aliasing={{3}: (7, {})} | custom-call | tf_op jit(solution)/shard_map/pallas_call | solution.py:220
  111.1 1.9 %collective-permute-start.4 = (bf16[2,1,128,512]{3,2,1,0:T(8,128)(2,1)}, bf16[2,1,128,512]{3,2,1,0:T(8,128)(2,1)S(1)}, u32[]{:S(2)}, u32[]{:S(2)}) collective-permute-start(bf16[2,1,128,512]{3,2,1,0:T(8,128)(2,1)} %get-tuple-element.30), channel_id=1, source_target_pairs={{1,0},{2,1},{3,2},{4,3},{5,4},{6,5},{7,6},{8,7},{9,8},{10,9},{11,1... | collective-permute-start | bytes 786440 | tf_op jit(solution)/shard_map/ppermute | solution.py:20
  113.0 0.0 collective-permute-done.3
  113.1 0.0 copy-done.6
  113.1 0.0 copy-done.7
  113.1 0.1 fusion.6
  113.2 7.8 %collective-permute-done.4 = bf16[2,1,128,512]{3,2,1,0:T(8,128)(2,1)S(1)} collective-permute-done((bf16[2,1,128,512]{3,2,1,0:T(8,128)(2,1)}, bf16[2,1,128,512]{3,2,1,0:T(8,128)(2,1)S(1)}, u32[]{:S(2)}, u32[]{:S(2)}) %collective-permute-start.4) | collective-permute-done | bytes 262176 | tf_op jit(solution)/shard_map/ppermute | solution.py:20
  121.0 1.1 fusion.7
  122.1 0.8 pad_maximum_fusion
  (6 shorter events, 0.1 us)
Async XLA Ops:
  0.6 10.0 %copy-start = (bf16[2,128,2048]{2,1,0:T(8,128)(2,1)S(1)}, bf16[2,128,2048]{2,1,0:T(8,128)(2,1)}, u32[]{:S(2)}) copy-start(bf16[2,128,2048]{2,1,0:T(8,128)(2,1)} %param.8) | copy-start | bytes 3145732
  3.6 40.1 %copy-start.8 = (s32[2,4096]{1,0:T(2,128)S(1)}, s32[2,4096]{1,0:T(2,128)}, u32[]{:S(2)}) copy-start(s32[2,4096]{1,0:T(2,128)} %param.9) | copy-start | bytes 98308
  3.6 34.3 %all-to-all-start = ((bf16[16,128,512]{2,1,0:T(8,128)(2,1)}), bf16[16,128,512]{2,1,0:T(8,128)(2,1)S(1)}, u32[]{:S(2)}, u32[]{:S(2)}) async-start(bf16[16,128,512]{2,1,0:T(8,128)(2,1)} %get-tuple-element.19), calls=%async_computation | async-start | bytes 4194304 | tf_op jit(solution)/shard_map/all_to_all | solution.py:270
  37.8 11.9 %copy-start.2 = (bf16[16,128,512]{2,1,0:T(8,128)(2,1)}, bf16[16,128,512]{2,1,0:T(8,128)(2,1)S(1)}, u32[]{:S(2)}) copy-start(bf16[16,128,512]{2,1,0:T(8,128)(2,1)S(1)} %all-to-all-done.x_ref) | copy-start | bytes 6291460
  37.9 11.9 %collective-permute-start.2 = (bf16[8,128,256]{2,1,0:T(8,128)(2,1)S(1)}, bf16[8,128,256]{2,1,0:T(8,128)(2,1)}, u32[]{:S(2)}, u32[]{:S(2)}) collective-permute-start(bf16[8,128,256]{2,1,0:T(8,128)(2,1)S(1)} %slice.25), channel_id=1, source_target_pairs={{0,1},{1,2},{2,3},{3,4},{4,5},{5,6},{6,7},{7,8},{8,9},{9,10},{10,1... | collective-permute-start | bytes 1572872 | tf_op jit(solution)/shard_map/ppermute | solution.py:20
  44.5 12.7 %collective-permute-start.1 = (bf16[7,128,256]{2,1,0:T(8,128)(2,1)}, bf16[7,128,256]{2,1,0:T(8,128)(2,1)}, u32[]{:S(2)}, u32[]{:S(2)}) collective-permute-start(bf16[7,128,256]{2,1,0:T(8,128)(2,1)} %slice.24), channel_id=1, source_target_pairs={{0,1},{1,2},{2,3},{3,4},{4,5},{5,6},{6,7},{7,8},{8,9},{9,10},{10,1... | collective-permute-start | bytes 1376264 | tf_op jit(solution)/shard_map/ppermute | solution.py:20
  46.5 17.9 %copy-start.5 = (s32[2,128,256]{2,1,0:T(8,128)}, s32[2,128,256]{2,1,0:T(8,128)S(1)}, u32[]{:S(2)}) copy-start(s32[2,128,256]{2,1,0:T(8,128)S(1)} %and_convert_fusion.m_ref) | copy-start | bytes 786436
  57.1 15.1 %copy-start.3 = (bf16[2,1,2,128,512]{4,3,2,1,0:T(8,128)(2,1)S(1)}, bf16[2,1,2,128,512]{4,3,2,1,0:T(8,128)(2,1)}, u32[]{:S(2)}) copy-start(bf16[2,1,2,128,512]{4,3,2,1,0:T(8,128)(2,1)} %get-tuple-element.18.kvo_ref) | copy-start | bytes 1572868
  64.4 30.7 %all-to-all-start.1 = ((bf16[16,128,256]{2,1,0:T(8,128)(2,1)}), bf16[16,128,256]{2,1,0:T(8,128)(2,1)S(1)}, u32[]{:S(2)}, u32[]{:S(2)}) async-start(bf16[16,128,256]{2,1,0:T(8,128)(2,1)} %get-tuple-element.22), calls=%async_computation.1 | async-start | bytes 2097152 | tf_op jit(solution)/shard_map/all_to_all | solution.py:282
  72.3 12.1 %collective-permute-start = (bf16[2,1,2,128,512]{4,3,2,1,0:T(8,128)(2,1)S(1)}, bf16[2,1,2,128,512]{4,3,2,1,0:T(8,128)(2,1)S(1)}, u32[]{:S(2)}, u32[]{:S(2)}) collective-permute-start(bf16[2,1,2,128,512]{4,3,2,1,0:T(8,128)(2,1)S(1)} %copy-done.3), channel_id=1, source_target_pairs={{0,1},{1,2},{2,3},{3,4},{4,5},{5,6},{6,7},{7,8},{8,9},{9,10},{10,1... | collective-permute-start | bytes 1572872 | tf_op jit(solution)/shard_map/ppermute | solution.py:20
  84.4 0.9 copy-start.4
  95.0 1.0 copy-start.1
  102.5 10.5 %collective-permute-start.3 = (bf16[2,1,128,512]{3,2,1,0:T(8,128)(2,1)}, bf16[2,1,128,512]{3,2,1,0:T(8,128)(2,1)S(1)}, u32[]{:S(2)}, u32[]{:S(2)}) collective-permute-start(bf16[2,1,128,512]{3,2,1,0:T(8,128)(2,1)} %get-tuple-element.28), channel_id=1, source_target_pairs={{1,0},{2,1},{3,2},{4,3},{5,4},{6,5},{7,6},{8,7},{9,8},{10,9},{11,1... | collective-permute-start | bytes 786440 | tf_op jit(solution)/shard_map/ppermute | solution.py:20
  104.5 8.6 %copy-start.6 = (f32[1,128,512]{2,1,0:T(8,128)S(1)}, f32[1,128,512]{2,1,0:T(8,128)}, u32[]{:S(2)}) copy-start(f32[1,128,512]{2,1,0:T(8,128)} %get-tuple-element.27) | copy-start | bytes 786436
  104.5 8.6 %copy-start.7 = (f32[1,128,512]{2,1,0:T(8,128)S(1)}, f32[1,128,512]{2,1,0:T(8,128)}, u32[]{:S(2)}) copy-start(f32[1,128,512]{2,1,0:T(8,128)} %get-tuple-element.31) | copy-start | bytes 786436
  111.1 9.9 %collective-permute-start.4 = (bf16[2,1,128,512]{3,2,1,0:T(8,128)(2,1)}, bf16[2,1,128,512]{3,2,1,0:T(8,128)(2,1)S(1)}, u32[]{:S(2)}, u32[]{:S(2)}) collective-permute-start(bf16[2,1,128,512]{3,2,1,0:T(8,128)(2,1)} %get-tuple-element.30), channel_id=1, source_target_pairs={{1,0},{2,1},{3,2},{4,3},{5,4},{6,5},{7,6},{8,7},{9,8},{10,9},{11,1... | collective-permute-start | bytes 786440 | tf_op jit(solution)/shard_map/ppermute | solution.py:20

commit v8 on v7

--- a/solution.py
+++ b/solution.py
@@ -34,7 +34,7 @@
     return prob_low, grad_score
 
 
-def chain_kernel(x_ref, halo_ref, g0_ref, m_ref, *rest, first, count):
+def chain_kernel(x_ref, g0_ref, m_ref, *rest, first, count):
     if len(rest) == 3:
         prev_ref, o_ref, g_out_ref = rest
     else:
@@ -42,7 +42,6 @@
         o_ref, g_out_ref = rest
     width = o_ref.shape[2]
     heads = width // DH
-    halo_first = first + count - halo_ref.shape[0]
     allowed = m_ref[...] != 0
     if prev_ref is None:
         o_ref[o_ref.shape[0] - 1] = g0_ref[...]
@@ -52,12 +51,13 @@
 
     def step(i, g):
         layer = first + count - 1 - i
-        local = layer - halo_first
         k = jnp.concatenate(
-            [halo_ref[local, :, :DH], x_ref[layer, :, width:width + DH]], axis=0
+            [x_ref[layer, :, width + 2 * DH:width + 3 * DH], x_ref[layer, :, width:width + DH]],
+            axis=0,
         )
         v = jnp.concatenate(
-            [halo_ref[local, :, DH:], x_ref[layer, :, width + DH:]], axis=0
+            [x_ref[layer, :, width + 3 * DH:], x_ref[layer, :, width + DH:width + 2 * DH]],
+            axis=0,
         )
         outs = []
         for h in range(heads):
@@ -74,10 +74,10 @@
     g_out_ref[...] = lax.fori_loop(0, count, step, g0_ref[...], unroll=True)
 
 
-def chain_call(sent, halo, grad_top, allowed_i32, first, count, prev=None, interpret=False):
+def chain_call(sent, grad_top, allowed_i32, first, count, prev=None, interpret=False):
     layers, rows, _ = sent.shape
     width = grad_top.shape[1]
-    operands = [sent, halo, grad_top, allowed_i32]
+    operands = [sent, grad_top, allowed_i32]
     if prev is not None:
         operands.append(prev)
     return pl.pallas_call(
@@ -90,38 +90,32 @@
     )(*operands)
 
 
-def pack_kernel(q_ref, k_ref, v_ref, send_ref, kv_ref, *, blocks_per_kv):
+def pack_kernel(q_ref, kv_ref, kvh_ref, send_ref, *, blocks_per_kv):
     blocks, _, total = send_ref.shape
-    bw = total - 2 * DH
+    bw = total - 4 * DH
     q = q_ref[0, 0]
-    k = k_ref[0, 0]
-    v = v_ref[0, 0]
+    parts = (kv_ref[0, 0, 0], kv_ref[1, 0, 0], kvh_ref[0, 0, 0], kvh_ref[1, 0, 0])
     for b in range(blocks):
         g = b // blocks_per_kv
         send_ref[b, :, :bw] = q[:, b * bw:(b + 1) * bw]
-        send_ref[b, :, bw:bw + DH] = k[:, g * DH:(g + 1) * DH]
-        send_ref[b, :, bw + DH:] = v[:, g * DH:(g + 1) * DH]
-    kv_ref[0, 0, 0] = k
-    kv_ref[1, 0, 0] = v
-
-
-def pack_call(queries, keys, values, head_blocks, blocks_per_kv, interpret=False):
+        for j, part in enumerate(parts):
+            send_ref[b, :, bw + j * DH:bw + (j + 1) * DH] = part[:, g * DH:(g + 1) * DH]
+
+
+def pack_call(queries, kv_own, kv_halo, head_blocks, blocks_per_kv, interpret=False):
     _, micro_count, rows, width = queries.shape
-    key_width = keys.shape[3]
+    key_width = kv_own.shape[4]
     bw = width // head_blocks
-    kv_in = pl.BlockSpec((1, 1, rows, key_width), lambda m: (0, m, 0, 0))
+    kv_in = pl.BlockSpec((2, 1, 1, rows, key_width), lambda m: (0, 0, m, 0, 0))
     return pl.pallas_call(
         functools.partial(pack_kernel, blocks_per_kv=blocks_per_kv),
         grid=(micro_count,),
         in_specs=[pl.BlockSpec((1, 1, rows, width), lambda m: (0, m, 0, 0)), kv_in, kv_in],
-        out_specs=[pl.BlockSpec((head_blocks, rows, bw + 2 * DH), lambda m: (m, 0, 0)),
-                   pl.BlockSpec((2, 1, 1, rows, key_width), lambda m: (0, 0, m, 0, 0))],
-        out_shape=[
-            jax.ShapeDtypeStruct((micro_count * head_blocks, rows, bw + 2 * DH), jnp.bfloat16),
-            jax.ShapeDtypeStruct((2,) + keys.shape, jnp.bfloat16),
-        ],
+        out_specs=pl.BlockSpec((head_blocks, rows, bw + 4 * DH), lambda m: (m, 0, 0)),
+        out_shape=jax.ShapeDtypeStruct(
+            (micro_count * head_blocks, rows, bw + 4 * DH), jnp.bfloat16),
         interpret=interpret,
-    )(queries, keys, values)
+    )(queries, kv_own, kv_halo)
 
 
 def layer_pre_kernel(q_ref, kvo_ref, kvh_ref, m_ref, p_ref, o_ref):
@@ -247,7 +241,7 @@
     block_heads = q_heads // head_blocks
     block_width = block_heads * DH
     blocks_per_kv = group_size // block_heads
-    send, kv_own = pack_call(queries, keys, values, head_blocks, blocks_per_kv)
+    kv_own = jnp.stack([keys, values])
     seg_padded = jnp.concatenate(
         [jnp.full((micro_count, row_count), -1, jnp.int32), segments], axis=1
     )
@@ -267,18 +261,14 @@
 
     my_block = section_index % head_blocks
     my_micro = section_index // head_blocks
+    send = pack_call(queries, kv_own, kv_halo, head_blocks, blocks_per_kv)
     sent = lax.all_to_all(send, "pipe", 0, 0)
     prob, out = layer_pre_call(queries, kv_own, kv_halo, masks)
-    split_at = section_count // 2
-    halo_hi = from_behind(sent[split_at:, :, block_width:], "seq", 1)
-    halo_lo = from_behind(sent[1:split_at, :, block_width:], "seq", 1)
     grad_top = lax.dynamic_slice(
         out_grad, (my_micro, 0, my_block * block_width), (1, row_count, block_width)
     )[0]
     allowed = lax.dynamic_index_in_dim(masks, my_micro, 0, keepdims=False)
-    above_hi, grad_mid = chain_call(
-        sent, halo_hi, grad_top, allowed, split_at, section_count - split_at)
-    grads_above, _ = chain_call(sent, halo_lo, grad_mid, allowed, 1, split_at - 1, above_hi)
+    grads_above, _ = chain_call(sent, grad_top, allowed, 1, section_count - 1)
     grad_t = lax.all_to_all(grads_above, "pipe", 0, 0)
 
     query_all = None

time: 124 us -> 135 us (1.089)
  the two profiles are of different devices: /device:TPU:227 before, /device:TPU:97 now
where the time goes in v8:
time: 135 us; the launch traced here: 134 us
  waiting for transfers between devices  66.6 us (49%)
  Pallas kernels  37.2 us (28%)
  starting transfers between devices  22.8 us (17%)
  other arithmetic  3.41 us (3%)
  local copies, waits for them, and re-layouts  3.26 us (2%)
    all_to_all x1, waiting for transfers between devices, device_body(): sent = lax.all_to_all(send, 'pipe', 0, 0)  47.4 us
    pallas_call x2, Pallas kernels, layer_call(): pl.pallas_call(layer_kernel, grid=(1, kv_heads), in_specs=in_specs, out_s...  13.2 us
    ppermute x3, waiting for transfers between devices, from_behind(): return lax.ppermute(block, axis, route)  13.2 us
    ppermute x3, starting transfers between devices, from_behind(): return lax.ppermute(block, axis, route)  11.9 us
    pallas_call x1, Pallas kernels, chain_call(): pl.pallas_call(functools.partial(chain_kernel, first=first, count=count),...  11.1 us
    pallas_call x1, Pallas kernels, layer_pre_call(): pl.pallas_call(layer_pre_kernel, grid=(micro_count, kv_heads), in_specs=[...  9.81 us
    all_to_all x1, starting transfers between devices, device_body(): sent = lax.all_to_all(send, 'pipe', 0, 0)  6.93 us
    all_to_all x1, waiting for transfers between devices, device_body(): grad_t = lax.all_to_all(grads_above, 'pipe', 0, 0)  6.02 us
  transfers between devices with their start and end apart: 5, of which 4 were waited for; matrix products, arithmetic and copies ran while one was open for 1% of the time, Pallas kernels for 12%

profile of v8, /device:TPU:97, one launch (start us, length us, event | category | flops | bytes accessed | tf_op | source)
XLA Modules:
  0.0 134.2 jit_solution(6079220242858084725)
XLA Ops:
  0.6 0.0 copy-start
  0.6 1.2 pad_maximum_fusion.kv_ref.kvo_ref
  1.8 0.0 copy-start.2
  1.8 5.3 %collective-permute-start = (bf16[2,1,2,128,512]{4,3,2,1,0:T(8,128)(2,1)S(1)}, bf16[2,1,2,128,512]{4,3,2,1,0:T(8,128)(2,1)S(1)}, u32[]{:S(2)}, u32[]{:S(2)}) collective-permute-start(bf16[2,1,2,128,512]{4,3,2,1,0:T(8,128)(2,1)S(1)} %pad_maximum_fusion.kv_ref.kvo_ref), channel_id=1, source_target_pairs={{0,1},{1,2},{2,3},{3,4},{4,5},{5,6},{6,7},{7,8},{8,9},{9,10},{10,1... | collective-permute-start | bytes 1572872 | tf_op jit(solution)/shard_map/ppermute | solution.py:20
  7.2 6.1 %collective-permute-done.kvh_ref = bf16[2,1,2,128,512]{4,3,2,1,0:T(8,128)(2,1)S(1)} collective-permute-done((bf16[2,1,2,128,512]{4,3,2,1,0:T(8,128)(2,1)S(1)}, bf16[2,1,2,128,512]{4,3,2,1,0:T(8,128)(2,1)S(1)}, u32[]{:S(2)}, u32[]{:S(2)}) %collective-permute-start) | collective-permute-done | bytes 524320 | tf_op jit(solution)/shard_map/ppermute | solution.py:20
  13.3 0.0 copy-done.2
  13.3 0.0 copy-start.3
  13.3 0.8 copy-done.3
  14.1 3.0 %shard_map.76 = bf16[16,128,768]{2,1,0:T(8,128)(2,1)} custom-call(bf16[1,2,128,2048]{3,2,1,0:T(8,128)(2,1)} %q_ref.7, bf16[2,1,2,128,512]{4,3,2,1,0:T(8,128)(2,1)} %copy-done.2, bf16[2,1,2,128,512]{4,3,2,1,0:T(8,128)(2,1)} %copy-done.3), custom_call_target="tpu_custom_call" | custom-call | tf_op jit(solution)/shard_map/pallas_call | solution.py:110
  17.1 0.0 copy-start.7
  17.1 6.9 %all-to-all-start = ((bf16[16,128,768]{2,1,0:T(8,128)(2,1)}), bf16[16,128,768]{2,1,0:T(8,128)(2,1)}, u32[]{:S(2)}, u32[]{:S(2)}) async-start(bf16[16,128,768]{2,1,0:T(8,128)(2,1)} %shard_map.76), calls=%async_computation | async-start | bytes 6291456 | tf_op jit(solution)/shard_map/all_to_all | solution.py:265
  24.2 0.0 copy-done.7
  24.2 0.0 copy-done
  24.2 0.6 dynamic-slice_bitcast_fusion.1.g0_ref
  24.9 0.1 fusion.9
  25.0 0.1 and_convert_fusion.m_ref
  25.1 0.0 copy-start.4
  25.1 0.7 dynamic-slice_bitcast_fusion.m_ref
  25.8 47.4 %all-to-all-done.x_ref = bf16[16,128,768]{2,1,0:T(8,128)(2,1)} async-done(((bf16[16,128,768]{2,1,0:T(8,128)(2,1)}), bf16[16,128,768]{2,1,0:T(8,128)(2,1)}, u32[]{:S(2)}, u32[]{:S(2)}) %all-to-all-start) | async-done | bytes 3145760 | tf_op jit(solution)/shard_map/all_to_all | solution.py:265
  73.3 11.1 %shard_map.77 = (bf16[16,128,256]{2,1,0:T(8,128)(2,1)}, bf16[128,256]{1,0:T(8,128)(2,1)}) custom-call(bf16[16,128,768]{2,1,0:T(8,128)(2,1)} %all-to-all-done.x_ref, bf16[128,256]{1,0:T(8,128)(2,1)} %dynamic-slice_bitcast_fusion.1.g0_ref, s32[128,256]{1,0:T(8,128)} %dynamic-slice_bitcast_fusion.m_ref), custom_call_target="tpu_custom_call" | custom-call | tf_op jit(solution)/shard_map/pallas_call | solution.py:83
  84.4 4.0 %all-to-all-start.1 = ((bf16[16,128,256]{2,1,0:T(8,128)(2,1)}), bf16[16,128,256]{2,1,0:T(8,128)(2,1)S(1)}, u32[]{:S(2)}, u32[]{:S(2)}) async-start(bf16[16,128,256]{2,1,0:T(8,128)(2,1)} %get-tuple-element.14), calls=%async_computation.1 | async-start | bytes 2097152 | tf_op jit(solution)/shard_map/all_to_all | solution.py:272
  88.4 0.0 copy-done.4
  88.4 9.8 %shard_map.78 = (f32[2,16,128,256]{3,2,1,0:T(8,128)}, f32[2,16,128,128]{3,2,1,0:T(8,128)}) custom-call(bf16[1,2,128,2048]{3,2,1,0:T(8,128)(2,1)} %q_ref.7, bf16[2,1,2,128,512]{4,3,2,1,0:T(8,128)(2,1)} %copy-done.2, bf16[2,1,2,128,512]{4,3,2,1,0:T(8,128)(2,1)} %copy-done.3, s32[2,128,256]{2,1,0:T(8,128)} %copy-done.4), custom_call_target="tpu_custom_call" | custom-call | tf_op jit(solution)/shard_map/pallas_call | solution.py:142
  98.2 6.0 %all-to-all-done.1.ga_ref.gb_ref = bf16[16,128,256]{2,1,0:T(8,128)(2,1)S(1)} async-done(((bf16[16,128,256]{2,1,0:T(8,128)(2,1)}), bf16[16,128,256]{2,1,0:T(8,128)(2,1)S(1)}, u32[]{:S(2)}, u32[]{:S(2)}) %all-to-all-start.1) | async-done | bytes 1048608 | tf_op jit(solution)/shard_map/all_to_all | solution.py:272
  104.2 0.0 copy-start.1
  104.2 1.0 copy-done.1
  105.2 6.5 %shard_map.79 = (f32[1,128,512]{2,1,0:T(8,128)}, f32[1,128,512]{2,1,0:T(8,128)}, bf16[2,1,128,512]{3,2,1,0:T(8,128)(2,1)}, bf16[1,2,128,2048]{3,2,1,0:T(8,128)(2,1)}) custom-call(bf16[1,2,128,2048]{3,2,1,0:T(8,128)(2,1)} %q_ref.7, bf16[2,1,2,128,512]{4,3,2,1,0:T(8,128)(2,1)} %copy-done.2, bf16[2,1,2,128,512]{4,3,2,1,0:T(8,128)(2,1)} %copy-done.3, ...), custom_call_target="tpu_custom_call" | custom-call | tf_op jit(solution)/shard_map/pallas_call | solution.py:214
  111.8 4.7 %collective-permute-start.1 = (bf16[2,1,128,512]{3,2,1,0:T(8,128)(2,1)}, bf16[2,1,128,512]{3,2,1,0:T(8,128)(2,1)S(1)}, u32[]{:S(2)}, u32[]{:S(2)}) collective-permute-start(bf16[2,1,128,512]{3,2,1,0:T(8,128)(2,1)} %get-tuple-element.20), channel_id=1, source_target_pairs={{1,0},{2,1},{3,2},{4,3},{5,4},{6,5},{7,6},{8,7},{9,8},{10,9},{11,1... | collective-permute-start | bytes 786440 | tf_op jit(solution)/shard_map/ppermute | solution.py:20
  116.5 0.0 copy-start.5
  116.5 0.0 copy-start.6
  116.5 6.6 %shard_map.80 = (f32[1,128,512]{2,1,0:T(8,128)}, f32[1,128,512]{2,1,0:T(8,128)}, bf16[2,1,128,512]{3,2,1,0:T(8,128)(2,1)}, bf16[1,2,128,2048]{3,2,1,0:T(8,128)(2,1)}) custom-call(bf16[1,2,128,2048]{3,2,1,0:T(8,128)(2,1)} %q_ref.7, bf16[2,1,2,128,512]{4,3,2,1,0:T(8,128)(2,1)} %copy-done.2, ...), custom_call_target="tpu_custom_call", output_to_operand_aliasing={{3}: (7, {})} | custom-call | tf_op jit(solution)/shard_map/pallas_call | solution.py:214
  123.1 1.9 %collective-permute-start.2 = (bf16[2,1,128,512]{3,2,1,0:T(8,128)(2,1)}, bf16[2,1,128,512]{3,2,1,0:T(8,128)(2,1)S(1)}, u32[]{:S(2)}, u32[]{:S(2)}) collective-permute-start(bf16[2,1,128,512]{3,2,1,0:T(8,128)(2,1)} %get-tuple-element.22), channel_id=1, source_target_pairs={{1,0},{2,1},{3,2},{4,3},{5,4},{6,5},{7,6},{8,7},{9,8},{10,9},{11,1... | collective-permute-start | bytes 786440 | tf_op jit(solution)/shard_map/ppermute | solution.py:20
  125.0 0.0 collective-permute-done.1
  125.1 0.0 copy-done.5
  125.1 0.0 copy-done.6
  125.1 0.1 fusion.6
  125.2 7.1 %collective-permute-done.2 = bf16[2,1,128,512]{3,2,1,0:T(8,128)(2,1)S(1)} collective-permute-done((bf16[2,1,128,512]{3,2,1,0:T(8,128)(2,1)}, bf16[2,1,128,512]{3,2,1,0:T(8,128)(2,1)S(1)}, u32[]{:S(2)}, u32[]{:S(2)}) %collective-permute-start.2) | collective-permute-done | bytes 262176 | tf_op jit(solution)/shard_map/ppermute | solution.py:20
  132.2 1.1 fusion.7
  133.3 0.8 pad_maximum_fusion.1
  (5 shorter events, 0.0 us)
Async XLA Ops:
  0.6 23.6 %copy-start = (bf16[2,128,2048]{2,1,0:T(8,128)(2,1)S(1)}, bf16[2,128,2048]{2,1,0:T(8,128)(2,1)}, u32[]{:S(2)}) copy-start(bf16[2,128,2048]{2,1,0:T(8,128)(2,1)} %param.8) | copy-start | bytes 3145732
  1.8 11.4 %copy-start.2 = (bf16[2,1,2,128,512]{4,3,2,1,0:T(8,128)(2,1)}, bf16[2,1,2,128,512]{4,3,2,1,0:T(8,128)(2,1)S(1)}, u32[]{:S(2)}) copy-start(bf16[2,1,2,128,512]{4,3,2,1,0:T(8,128)(2,1)S(1)} %pad_maximum_fusion.kv_ref.kvo_ref) | copy-start | bytes 1572868
  1.8 11.4 %collective-permute-start = (bf16[2,1,2,128,512]{4,3,2,1,0:T(8,128)(2,1)S(1)}, bf16[2,1,2,128,512]{4,3,2,1,0:T(8,128)(2,1)S(1)}, u32[]{:S(2)}, u32[]{:S(2)}) collective-permute-start(bf16[2,1,2,128,512]{4,3,2,1,0:T(8,128)(2,1)S(1)} %pad_maximum_fusion.kv_ref.kvo_ref), channel_id=1, source_target_pairs={{0,1},{1,2},{2,3},{3,4},{4,5},{5,6},{6,7},{7,8},{8,9},{9,10},{10,1... | collective-permute-start | bytes 1572872 | tf_op jit(solution)/shard_map/ppermute | solution.py:20
  13.3 0.8 copy-start.3
  17.1 7.0 %copy-start.7 = (s32[2,4096]{1,0:T(2,128)S(1)}, s32[2,4096]{1,0:T(2,128)}, u32[]{:S(2)}) copy-start(s32[2,4096]{1,0:T(2,128)} %param.9) | copy-start | bytes 98308
  17.1 56.1 %all-to-all-start = ((bf16[16,128,768]{2,1,0:T(8,128)(2,1)}), bf16[16,128,768]{2,1,0:T(8,128)(2,1)}, u32[]{:S(2)}, u32[]{:S(2)}) async-start(bf16[16,128,768]{2,1,0:T(8,128)(2,1)} %shard_map.76), calls=%async_computation | async-start | bytes 6291456 | tf_op jit(solution)/shard_map/all_to_all | solution.py:265
  25.1 63.3 %copy-start.4 = (s32[2,128,256]{2,1,0:T(8,128)}, s32[2,128,256]{2,1,0:T(8,128)S(1)}, u32[]{:S(2)}) copy-start(s32[2,128,256]{2,1,0:T(8,128)S(1)} %and_convert_fusion.m_ref) | copy-start | bytes 786436
  84.4 19.8 %all-to-all-start.1 = ((bf16[16,128,256]{2,1,0:T(8,128)(2,1)}), bf16[16,128,256]{2,1,0:T(8,128)(2,1)S(1)}, u32[]{:S(2)}, u32[]{:S(2)}) async-start(bf16[16,128,256]{2,1,0:T(8,128)(2,1)} %get-tuple-element.14), calls=%async_computation.1 | async-start | bytes 2097152 | tf_op jit(solution)/shard_map/all_to_all | solution.py:272
  104.2 1.0 copy-start.1
  111.8 13.3 %collective-permute-start.1 = (bf16[2,1,128,512]{3,2,1,0:T(8,128)(2,1)}, bf16[2,1,128,512]{3,2,1,0:T(8,128)(2,1)S(1)}, u32[]{:S(2)}, u32[]{:S(2)}) collective-permute-start(bf16[2,1,128,512]{3,2,1,0:T(8,128)(2,1)} %get-tuple-element.20), channel_id=1, source_target_pairs={{1,0},{2,1},{3,2},{4,3},{5,4},{6,5},{7,6},{8,7},{9,8},{10,9},{11,1... | collective-permute-start | bytes 786440 | tf_op jit(solution)/shard_map/ppermute | solution.py:20
  116.5 8.6 %copy-start.5 = (f32[1,128,512]{2,1,0:T(8,128)S(1)}, f32[1,128,512]{2,1,0:T(8,128)}, u32[]{:S(2)}) copy-start(f32[1,128,512]{2,1,0:T(8,128)} %get-tuple-element.19) | copy-start | bytes 786436
  116.5 8.6 %copy-start.6 = (f32[1,128,512]{2,1,0:T(8,128)S(1)}, f32[1,128,512]{2,1,0:T(8,128)}, u32[]{:S(2)}) copy-start(f32[1,128,512]{2,1,0:T(8,128)} %get-tuple-element.23) | copy-start | bytes 786436
  123.1 9.1 %collective-permute-start.2 = (bf16[2,1,128,512]{3,2,1,0:T(8,128)(2,1)}, bf16[2,1,128,512]{3,2,1,0:T(8,128)(2,1)S(1)}, u32[]{:S(2)}, u32[]{:S(2)}) collective-permute-start(bf16[2,1,128,512]{3,2,1,0:T(8,128)(2,1)} %get-tuple-element.22), channel_id=1, source_target_pairs={{1,0},{2,1},{3,2},{4,3},{5,4},{6,5},{7,6},{8,7},{9,8},{10,9},{11,1... | collective-permute-start | bytes 786440 | tf_op jit(solution)/shard_map/ppermute | solution.py:20

commit v9 on v7

--- a/solution.py
+++ b/solution.py
@@ -4,6 +4,7 @@
 import jax.numpy as jnp
 from jax import lax
 from jax.experimental import pallas as pl
+from jax.experimental.pallas import tpu as pltpu
 from jax.sharding import PartitionSpec as P
 
 
@@ -34,58 +35,77 @@
     return prob_low, grad_score
 
 
-def chain_kernel(x_ref, halo_ref, g0_ref, m_ref, *rest, first, count):
-    if len(rest) == 3:
-        prev_ref, o_ref, g_out_ref = rest
+def chain_kernel(x_hbm, halo_hbm, g0_ref, m_ref, *rest, first, count):
+    if len(rest) == 6:
+        prev_hbm, o_ref, g_out_ref, x_buf, h_buf, sems = rest
     else:
-        prev_ref = None
-        o_ref, g_out_ref = rest
+        prev_hbm = None
+        o_ref, g_out_ref, x_buf, h_buf, sems = rest
     width = o_ref.shape[2]
     heads = width // DH
-    halo_first = first + count - halo_ref.shape[0]
+    halo_first = first + count - halo_hbm.shape[0]
     allowed = m_ref[...] != 0
-    if prev_ref is None:
+    top = first + count - 1
+    copies = []
+    for i in range(count):
+        layer = top - i
+        cx = pltpu.make_async_copy(x_hbm.at[layer], x_buf.at[i], sems.at[0, i])
+        ch = pltpu.make_async_copy(halo_hbm.at[layer - halo_first], h_buf.at[i], sems.at[1, i])
+        cx.start()
+        ch.start()
+        copies.append((cx, ch))
+    if prev_hbm is None:
         o_ref[o_ref.shape[0] - 1] = g0_ref[...]
+        keep = None
     else:
-        top = first + count - 1
-        o_ref[top:] = prev_ref[top:]
-
-    def step(i, g):
-        layer = first + count - 1 - i
-        local = layer - halo_first
-        k = jnp.concatenate(
-            [halo_ref[local, :, :DH], x_ref[layer, :, width:width + DH]], axis=0
-        )
-        v = jnp.concatenate(
-            [halo_ref[local, :, DH:], x_ref[layer, :, width + DH:]], axis=0
-        )
+        keep = pltpu.make_async_copy(prev_hbm.at[top:], o_ref.at[top:], sems.at[2, 0])
+        keep.start()
+    g = g0_ref[...]
+    for i in range(count):
+        layer = top - i
+        cx, ch = copies[i]
+        cx.wait()
+        ch.wait()
+        k = jnp.concatenate([h_buf[i, :, :DH], x_buf[i, :, width:width + DH]], axis=0)
+        v = jnp.concatenate([h_buf[i, :, DH:], x_buf[i, :, width + DH:]], axis=0)
         outs = []
         for h in range(heads):
             cols = slice(h * DH, (h + 1) * DH)
-            q = x_ref[layer, :, cols]
+            q = x_buf[i, :, cols]
             gh = g[:, cols]
             _, grad_score = head_core(q, k, v, gh, allowed)
             dq = jnp.dot(grad_score, k, preferred_element_type=jnp.float32) * SCALE
             outs.append((gh.astype(jnp.float32) + dq).astype(jnp.bfloat16))
-        g_new = jnp.concatenate(outs, axis=-1) if heads > 1 else outs[0]
-        o_ref[layer - 1] = g_new
-        return g_new
-
-    g_out_ref[...] = lax.fori_loop(0, count, step, g0_ref[...], unroll=True)
+        g = jnp.concatenate(outs, axis=-1) if heads > 1 else outs[0]
+        o_ref[layer - 1] = g
+    g_out_ref[...] = g
+    if keep is not None:
+        keep.wait()
 
 
 def chain_call(sent, halo, grad_top, allowed_i32, first, count, prev=None, interpret=False):
-    layers, rows, _ = sent.shape
+    layers, rows, total = sent.shape
     width = grad_top.shape[1]
     operands = [sent, halo, grad_top, allowed_i32]
+    any_spec = pl.BlockSpec(memory_space=pl.ANY)
+    vmem_spec = pl.BlockSpec(memory_space=pltpu.VMEM)
+    in_specs = [any_spec, any_spec, vmem_spec, vmem_spec]
     if prev is not None:
         operands.append(prev)
+        in_specs.append(any_spec)
     return pl.pallas_call(
         functools.partial(chain_kernel, first=first, count=count),
+        in_specs=in_specs,
+        out_specs=(vmem_spec, vmem_spec),
         out_shape=(
             jax.ShapeDtypeStruct((layers, rows, width), jnp.bfloat16),
             jax.ShapeDtypeStruct((rows, width), jnp.bfloat16),
         ),
+        scratch_shapes=[
+            pltpu.VMEM((count, rows, total), sent.dtype),
+            pltpu.VMEM((count, rows, halo.shape[2]), halo.dtype),
+            pltpu.SemaphoreType.DMA((3, count)),
+        ],
         interpret=interpret,
     )(*operands)
 

time: 124 us -> 130 us (1.048)
  the two profiles are of different devices: /device:TPU:227 before, /device:TPU:99 now
where the time goes in v9:
time: 130 us; the launch traced here: 129 us
  Pallas kernels  46.2 us (36%)
  waiting for transfers between devices  42.8 us (33%)
  starting transfers between devices  32.5 us (25%)
  local copies, waits for them, and re-layouts  4.11 us (3%)
  other arithmetic  2.23 us (2%)
    all_to_all x1, waiting for transfers between devices, device_body(): sent = lax.all_to_all(send, 'pipe', 0, 0)  26.4 us
    pallas_call x2, Pallas kernels, chain_call(): pl.pallas_call(functools.partial(chain_kernel, first=first, count=count),...  20.4 us
    ppermute x5, starting transfers between devices, from_behind(): return lax.ppermute(block, axis, route)  17.5 us
    ppermute x5, waiting for transfers between devices, from_behind(): return lax.ppermute(block, axis, route)  16.4 us
    pallas_call x2, Pallas kernels, layer_call(): pl.pallas_call(layer_kernel, grid=(1, kv_heads), in_specs=in_specs, out_s...  13.2 us
    pallas_call x1, Pallas kernels, layer_pre_call(): pl.pallas_call(layer_pre_kernel, grid=(micro_count, kv_heads), in_specs=[...  9.78 us
    all_to_all x1, starting transfers between devices, device_body(): grad_t = lax.all_to_all(grads_above, 'pipe', 0, 0)  7.92 us
    all_to_all x1, starting transfers between devices, device_body(): sent = lax.all_to_all(send, 'pipe', 0, 0)  7.05 us
  transfers between devices with their start and end apart: 7, of which 4 were waited for; matrix products, arithmetic and copies ran while one was open for 2% of the time, Pallas kernels for 21%

profile of v9, /device:TPU:99, one launch (start us, length us, event | category | flops | bytes accessed | tf_op | source)
XLA Modules:
  0.0 128.7 jit_solution(1415841290473551396)
XLA Ops:
  0.6 0.0 copy-start
  0.6 2.9 %shard_map.76 = (bf16[16,128,512]{2,1,0:T(8,128)(2,1)}, bf16[2,1,2,128,512]{4,3,2,1,0:T(8,128)(2,1)}) custom-call(bf16[1,2,128,2048]{3,2,1,0:T(8,128)(2,1)} %q_ref.7, bf16[1,2,128,512]{3,2,1,0:T(8,128)(2,1)} %k_ref.1, bf16[1,2,128,512]{3,2,1,0:T(8,128)(2,1)} %v_ref.1), custom_call_target="tpu_custom_call" | custom-call | tf_op jit(solution)/shard_map/pallas_call | solution.py:133
  3.6 0.0 copy-start.8
  3.6 7.0 %all-to-all-start = ((bf16[16,128,512]{2,1,0:T(8,128)(2,1)}), bf16[16,128,512]{2,1,0:T(8,128)(2,1)S(1)}, u32[]{:S(2)}, u32[]{:S(2)}) async-start(bf16[16,128,512]{2,1,0:T(8,128)(2,1)} %get-tuple-element.19), calls=%async_computation | async-start | bytes 4194304 | tf_op jit(solution)/shard_map/all_to_all | solution.py:290
  10.6 0.0 copy-done
  10.7 0.7 dynamic-slice_bitcast_fusion.1.g0_ref
  11.3 0.1 fusion.9
  11.4 26.4 %all-to-all-done.x_hbm = bf16[16,128,512]{2,1,0:T(8,128)(2,1)S(1)} async-done(((bf16[16,128,512]{2,1,0:T(8,128)(2,1)}), bf16[16,128,512]{2,1,0:T(8,128)(2,1)S(1)}, u32[]{:S(2)}, u32[]{:S(2)}) %all-to-all-start) | async-done | bytes 2097184 | tf_op jit(solution)/shard_map/all_to_all | solution.py:290
  37.8 0.0 copy-start.2
  37.9 5.8 %collective-permute-start.2 = (bf16[8,128,256]{2,1,0:T(8,128)(2,1)S(1)}, bf16[8,128,256]{2,1,0:T(8,128)(2,1)}, u32[]{:S(2)}, u32[]{:S(2)}) collective-permute-start(bf16[8,128,256]{2,1,0:T(8,128)(2,1)S(1)} %slice.25), channel_id=1, source_target_pairs={{0,1},{1,2},{2,3},{3,4},{4,5},{5,6},{6,7},{7,8},{8,9},{9,10},{10,1... | collective-permute-start | bytes 1572872 | tf_op jit(solution)/shard_map/ppermute | solution.py:21
  43.7 0.0 copy-done.8
  43.7 0.8 slice.24
  44.5 1.9 %collective-permute-start.1 = (bf16[7,128,256]{2,1,0:T(8,128)(2,1)}, bf16[7,128,256]{2,1,0:T(8,128)(2,1)}, u32[]{:S(2)}, u32[]{:S(2)}) collective-permute-start(bf16[7,128,256]{2,1,0:T(8,128)(2,1)} %slice.24), channel_id=1, source_target_pairs={{0,1},{1,2},{2,3},{3,4},{4,5},{5,6},{6,7},{7,8},{8,9},{9,10},{10,1... | collective-permute-start | bytes 1376264 | tf_op jit(solution)/shard_map/ppermute | solution.py:21
  46.4 0.1 and_convert_fusion.m_ref
  46.5 0.0 copy-start.5
  46.5 0.7 dynamic-slice_bitcast_fusion.m_ref
  47.3 2.5 %collective-permute-done.2.halo_hbm = bf16[8,128,256]{2,1,0:T(8,128)(2,1)} collective-permute-done((bf16[8,128,256]{2,1,0:T(8,128)(2,1)S(1)}, bf16[8,128,256]{2,1,0:T(8,128)(2,1)}, u32[]{:S(2)}, u32[]{:S(2)}) %collective-permute-start.2) | collective-permute-done | bytes 524320 | tf_op jit(solution)/shard_map/ppermute | solution.py:21
  49.8 0.0 copy-done.2
  49.8 10.6 %shard_map.77 = (bf16[16,128,256]{2,1,0:T(8,128)(2,1)}, bf16[128,256]{1,0:T(8,128)(2,1)}) custom-call(bf16[16,128,512]{2,1,0:T(8,128)(2,1)} %copy-done.2, bf16[8,128,256]{2,1,0:T(8,128)(2,1)} %collective-permute-done.2.halo_hbm, bf16[128,256]{1,0:T(8,128)(2,1)} %dynamic-slice_bitcast_fusion.1.g0_ref, s32[128,256]{1,0:T(8,128)} %dynamic-slice_bitcast_fusion.m_ref), custom_call_target="tpu_custom_call" | custom-call | tf_op jit(solution)/shard_map/pallas_call | solution.py:96
  60.4 0.0 collective-permute-done.1.halo_hbm
  60.4 0.0 copy-start.3
  60.4 9.7 %shard_map.78 = (bf16[16,128,256]{2,1,0:T(8,128)(2,1)}, bf16[128,256]{1,0:T(8,128)(2,1)}) custom-call(bf16[16,128,512]{2,1,0:T(8,128)(2,1)} %copy-done.2, bf16[7,128,256]{2,1,0:T(8,128)(2,1)} %collective-permute-done.1.halo_hbm, bf16[128,256]{1,0:T(8,128)(2,1)} %get-tuple-element.20.g0_ref, s32[128,256]{1,0:T(8,128)} %dynamic-slice_bitcast_fusion.m_ref, ...), custom_call_target="tpu_custom_call" | custom-call | tf_op jit(solution)/shard_map/pallas_call | solution.py:96
  70.2 0.0 copy-done.5
  70.2 7.9 %all-to-all-start.1 = ((bf16[16,128,256]{2,1,0:T(8,128)(2,1)}), bf16[16,128,256]{2,1,0:T(8,128)(2,1)S(1)}, u32[]{:S(2)}, u32[]{:S(2)}) async-start(bf16[16,128,256]{2,1,0:T(8,128)(2,1)} %get-tuple-element.22), calls=%async_computation.1 | async-start | bytes 2097152 | tf_op jit(solution)/shard_map/all_to_all | solution.py:302
  78.1 0.0 copy-done.3
  78.1 6.0 %collective-permute-start = (bf16[2,1,2,128,512]{4,3,2,1,0:T(8,128)(2,1)S(1)}, bf16[2,1,2,128,512]{4,3,2,1,0:T(8,128)(2,1)S(1)}, u32[]{:S(2)}, u32[]{:S(2)}) collective-permute-start(bf16[2,1,2,128,512]{4,3,2,1,0:T(8,128)(2,1)S(1)} %copy-done.3), channel_id=1, source_target_pairs={{0,1},{1,2},{2,3},{3,4},{4,5},{5,6},{6,7},{7,8},{8,9},{9,10},{10,1... | collective-permute-start | bytes 1572872 | tf_op jit(solution)/shard_map/ppermute | solution.py:21
  84.1 6.1 %collective-permute-done.kvh_ref = bf16[2,1,2,128,512]{4,3,2,1,0:T(8,128)(2,1)S(1)} collective-permute-done((bf16[2,1,2,128,512]{4,3,2,1,0:T(8,128)(2,1)S(1)}, bf16[2,1,2,128,512]{4,3,2,1,0:T(8,128)(2,1)S(1)}, u32[]{:S(2)}, u32[]{:S(2)}) %collective-permute-start) | collective-permute-done | bytes 524320 | tf_op jit(solution)/shard_map/ppermute | solution.py:21
  90.2 0.0 copy-start.4
  90.2 0.9 copy-done.4
  91.1 9.8 %shard_map.79 = (f32[2,16,128,256]{3,2,1,0:T(8,128)}, f32[2,16,128,128]{3,2,1,0:T(8,128)}) custom-call(bf16[1,2,128,2048]{3,2,1,0:T(8,128)(2,1)} %q_ref.7, bf16[2,1,2,128,512]{4,3,2,1,0:T(8,128)(2,1)} %get-tuple-element.18.kvo_ref, bf16[2,1,2,128,512]{4,3,2,1,0:T(8,128)(2,1)} %copy-done.4, s32[2,128,256]{2,1,0:T(8,128)} %copy-done.5), custom_call_target="tpu_custom_call" | custom-call | tf_op jit(solution)/shard_map/pallas_call | solution.py:168
  100.8 0.0 all-to-all-done.1.ga_ref.gb_ref
  100.8 0.0 copy-start.1
  100.8 1.0 copy-done.1
  101.8 6.5 %shard_map.80 = (f32[1,128,512]{2,1,0:T(8,128)}, f32[1,128,512]{2,1,0:T(8,128)}, bf16[2,1,128,512]{3,2,1,0:T(8,128)(2,1)}, bf16[1,2,128,2048]{3,2,1,0:T(8,128)(2,1)}) custom-call(bf16[1,2,128,2048]{3,2,1,0:T(8,128)(2,1)} %q_ref.7, bf16[2,1,2,128,512]{4,3,2,1,0:T(8,128)(2,1)} %get-tuple-element.18.kvo_ref, bf16[2,1,2,128,512]{4,3,2,1,0:T(8,128)(2,1)} %copy-done.4, ...), custom_call_target="tpu_custom_call" | custom-call | tf_op jit(solution)/shard_map/pallas_call | solution.py:240
  108.3 1.9 %collective-permute-start.3 = (bf16[2,1,128,512]{3,2,1,0:T(8,128)(2,1)}, bf16[2,1,128,512]{3,2,1,0:T(8,128)(2,1)S(1)}, u32[]{:S(2)}, u32[]{:S(2)}) collective-permute-start(bf16[2,1,128,512]{3,2,1,0:T(8,128)(2,1)} %get-tuple-element.28), channel_id=1, source_target_pairs={{1,0},{2,1},{3,2},{4,3},{5,4},{6,5},{7,6},{8,7},{9,8},{10,9},{11,1... | collective-permute-start | bytes 786440 | tf_op jit(solution)/shard_map/ppermute | solution.py:21
  110.3 0.0 copy-start.6
  110.3 0.0 copy-start.7
  110.3 6.6 %shard_map.81 = (f32[1,128,512]{2,1,0:T(8,128)}, f32[1,128,512]{2,1,0:T(8,128)}, bf16[2,1,128,512]{3,2,1,0:T(8,128)(2,1)}, bf16[1,2,128,2048]{3,2,1,0:T(8,128)(2,1)}) custom-call(bf16[1,2,128,2048]{3,2,1,0:T(8,128)(2,1)} %q_ref.7, bf16[2,1,2,128,512]{4,3,2,1,0:T(8,128)(2,1)} %get-tuple-element.18.kvo_ref, ...), custom_call_target="tpu_custom_call", output_to_operand_aliasing={{3}: (7, {})} | custom-call | tf_op jit(solution)/shard_map/pallas_call | solution.py:240
  116.9 1.9 %collective-permute-start.4 = (bf16[2,1,128,512]{3,2,1,0:T(8,128)(2,1)}, bf16[2,1,128,512]{3,2,1,0:T(8,128)(2,1)S(1)}, u32[]{:S(2)}, u32[]{:S(2)}) collective-permute-start(bf16[2,1,128,512]{3,2,1,0:T(8,128)(2,1)} %get-tuple-element.30), channel_id=1, source_target_pairs={{1,0},{2,1},{3,2},{4,3},{5,4},{6,5},{7,6},{8,7},{9,8},{10,9},{11,1... | collective-permute-start | bytes 786440 | tf_op jit(solution)/shard_map/ppermute | solution.py:21
  118.8 0.0 collective-permute-done.3
  118.9 0.0 copy-done.6
  118.9 0.0 copy-done.7
  118.9 0.1 fusion.6
  119.0 7.8 %collective-permute-done.4 = bf16[2,1,128,512]{3,2,1,0:T(8,128)(2,1)S(1)} collective-permute-done((bf16[2,1,128,512]{3,2,1,0:T(8,128)(2,1)}, bf16[2,1,128,512]{3,2,1,0:T(8,128)(2,1)S(1)}, u32[]{:S(2)}, u32[]{:S(2)}) %collective-permute-start.4) | collective-permute-done | bytes 262176 | tf_op jit(solution)/shard_map/ppermute | solution.py:21
  126.8 1.1 fusion.7
  127.9 0.8 pad_maximum_fusion
  (6 shorter events, 0.1 us)
Async XLA Ops:
  0.6 10.0 %copy-start = (bf16[2,128,2048]{2,1,0:T(8,128)(2,1)S(1)}, bf16[2,128,2048]{2,1,0:T(8,128)(2,1)}, u32[]{:S(2)}) copy-start(bf16[2,128,2048]{2,1,0:T(8,128)(2,1)} %param.8) | copy-start | bytes 3145732
  3.6 40.1 %copy-start.8 = (s32[2,4096]{1,0:T(2,128)S(1)}, s32[2,4096]{1,0:T(2,128)}, u32[]{:S(2)}) copy-start(s32[2,4096]{1,0:T(2,128)} %param.9) | copy-start | bytes 98308
  3.6 34.3 %all-to-all-start = ((bf16[16,128,512]{2,1,0:T(8,128)(2,1)}), bf16[16,128,512]{2,1,0:T(8,128)(2,1)S(1)}, u32[]{:S(2)}, u32[]{:S(2)}) async-start(bf16[16,128,512]{2,1,0:T(8,128)(2,1)} %get-tuple-element.19), calls=%async_computation | async-start | bytes 4194304 | tf_op jit(solution)/shard_map/all_to_all | solution.py:290
  37.8 11.9 %copy-start.2 = (bf16[16,128,512]{2,1,0:T(8,128)(2,1)}, bf16[16,128,512]{2,1,0:T(8,128)(2,1)S(1)}, u32[]{:S(2)}) copy-start(bf16[16,128,512]{2,1,0:T(8,128)(2,1)S(1)} %all-to-all-done.x_hbm) | copy-start | bytes 6291460
  37.9 11.9 %collective-permute-start.2 = (bf16[8,128,256]{2,1,0:T(8,128)(2,1)S(1)}, bf16[8,128,256]{2,1,0:T(8,128)(2,1)}, u32[]{:S(2)}, u32[]{:S(2)}) collective-permute-start(bf16[8,128,256]{2,1,0:T(8,128)(2,1)S(1)} %slice.25), channel_id=1, source_target_pairs={{0,1},{1,2},{2,3},{3,4},{4,5},{5,6},{6,7},{7,8},{8,9},{9,10},{10,1... | collective-permute-start | bytes 1572872 | tf_op jit(solution)/shard_map/ppermute | solution.py:21
  44.5 15.9 %collective-permute-start.1 = (bf16[7,128,256]{2,1,0:T(8,128)(2,1)}, bf16[7,128,256]{2,1,0:T(8,128)(2,1)}, u32[]{:S(2)}, u32[]{:S(2)}) collective-permute-start(bf16[7,128,256]{2,1,0:T(8,128)(2,1)} %slice.24), channel_id=1, source_target_pairs={{0,1},{1,2},{2,3},{3,4},{4,5},{5,6},{6,7},{7,8},{8,9},{9,10},{10,1... | collective-permute-start | bytes 1376264 | tf_op jit(solution)/shard_map/ppermute | solution.py:21
  46.5 23.6 %copy-start.5 = (s32[2,128,256]{2,1,0:T(8,128)}, s32[2,128,256]{2,1,0:T(8,128)S(1)}, u32[]{:S(2)}) copy-start(s32[2,128,256]{2,1,0:T(8,128)S(1)} %and_convert_fusion.m_ref) | copy-start | bytes 786436
  60.4 17.7 %copy-start.3 = (bf16[2,1,2,128,512]{4,3,2,1,0:T(8,128)(2,1)S(1)}, bf16[2,1,2,128,512]{4,3,2,1,0:T(8,128)(2,1)}, u32[]{:S(2)}) copy-start(bf16[2,1,2,128,512]{4,3,2,1,0:T(8,128)(2,1)} %get-tuple-element.18.kvo_ref) | copy-start | bytes 1572868
  70.2 30.7 %all-to-all-start.1 = ((bf16[16,128,256]{2,1,0:T(8,128)(2,1)}), bf16[16,128,256]{2,1,0:T(8,128)(2,1)S(1)}, u32[]{:S(2)}, u32[]{:S(2)}) async-start(bf16[16,128,256]{2,1,0:T(8,128)(2,1)} %get-tuple-element.22), calls=%async_computation.1 | async-start | bytes 2097152 | tf_op jit(solution)/shard_map/all_to_all | solution.py:302
  78.1 12.1 %collective-permute-start = (bf16[2,1,2,128,512]{4,3,2,1,0:T(8,128)(2,1)S(1)}, bf16[2,1,2,128,512]{4,3,2,1,0:T(8,128)(2,1)S(1)}, u32[]{:S(2)}, u32[]{:S(2)}) collective-permute-start(bf16[2,1,2,128,512]{4,3,2,1,0:T(8,128)(2,1)S(1)} %copy-done.3), channel_id=1, source_target_pairs={{0,1},{1,2},{2,3},{3,4},{4,5},{5,6},{6,7},{7,8},{8,9},{9,10},{10,1... | collective-permute-start | bytes 1572872 | tf_op jit(solution)/shard_map/ppermute | solution.py:21
  90.2 0.9 copy-start.4
  100.8 1.0 copy-start.1
  108.3 10.5 %collective-permute-start.3 = (bf16[2,1,128,512]{3,2,1,0:T(8,128)(2,1)}, bf16[2,1,128,512]{3,2,1,0:T(8,128)(2,1)S(1)}, u32[]{:S(2)}, u32[]{:S(2)}) collective-permute-start(bf16[2,1,128,512]{3,2,1,0:T(8,128)(2,1)} %get-tuple-element.28), channel_id=1, source_target_pairs={{1,0},{2,1},{3,2},{4,3},{5,4},{6,5},{7,6},{8,7},{9,8},{10,9},{11,1... | collective-permute-start | bytes 786440 | tf_op jit(solution)/shard_map/ppermute | solution.py:21
  110.3 8.6 %copy-start.6 = (f32[1,128,512]{2,1,0:T(8,128)S(1)}, f32[1,128,512]{2,1,0:T(8,128)}, u32[]{:S(2)}) copy-start(f32[1,128,512]{2,1,0:T(8,128)} %get-tuple-element.27) | copy-start | bytes 786436
  110.3 8.6 %copy-start.7 = (f32[1,128,512]{2,1,0:T(8,128)S(1)}, f32[1,128,512]{2,1,0:T(8,128)}, u32[]{:S(2)}) copy-start(f32[1,128,512]{2,1,0:T(8,128)} %get-tuple-element.31) | copy-start | bytes 786436
  116.9 9.9 %collective-permute-start.4 = (bf16[2,1,128,512]{3,2,1,0:T(8,128)(2,1)}, bf16[2,1,128,512]{3,2,1,0:T(8,128)(2,1)S(1)}, u32[]{:S(2)}, u32[]{:S(2)}) collective-permute-start(bf16[2,1,128,512]{3,2,1,0:T(8,128)(2,1)} %get-tuple-element.30), channel_id=1, source_target_pairs={{1,0},{2,1},{3,2},{4,3},{5,4},{6,5},{7,6},{8,7},{9,8},{10,9},{11,1... | collective-permute-start | bytes 786440 | tf_op jit(solution)/shard_map/ppermute | solution.py:21

commit v10 on v7

--- a/solution.py
+++ b/solution.py
@@ -4,6 +4,7 @@
 import jax.numpy as jnp
 from jax import lax
 from jax.experimental import pallas as pl
+from jax.experimental.pallas import tpu as pltpu
 from jax.sharding import PartitionSpec as P
 
 
@@ -90,36 +91,45 @@
     )(*operands)
 
 
-def pack_kernel(q_ref, k_ref, v_ref, send_ref, kv_ref, *, blocks_per_kv):
-    blocks, _, total = send_ref.shape
+def pack_kernel(q_hbm, k_hbm, v_hbm, send_hbm, kv_hbm, sems, *, blocks_per_kv):
+    micro_count = q_hbm.shape[1]
+    total = send_hbm.shape[2]
     bw = total - 2 * DH
-    q = q_ref[0, 0]
-    k = k_ref[0, 0]
-    v = v_ref[0, 0]
-    for b in range(blocks):
-        g = b // blocks_per_kv
-        send_ref[b, :, :bw] = q[:, b * bw:(b + 1) * bw]
-        send_ref[b, :, bw:bw + DH] = k[:, g * DH:(g + 1) * DH]
-        send_ref[b, :, bw + DH:] = v[:, g * DH:(g + 1) * DH]
-    kv_ref[0, 0, 0] = k
-    kv_ref[1, 0, 0] = v
+    blocks = send_hbm.shape[0] // micro_count
+    copies = [
+        pltpu.make_async_copy(k_hbm.at[0], kv_hbm.at[0, 0], sems.at[0]),
+        pltpu.make_async_copy(v_hbm.at[0], kv_hbm.at[1, 0], sems.at[1]),
+    ]
+    for m in range(micro_count):
+        for b in range(blocks):
+            g = b // blocks_per_kv
+            dst = send_hbm.at[m * blocks + b]
+            parts = (
+                (q_hbm.at[0, m, :, pl.ds(b * bw, bw)], dst.at[:, pl.ds(0, bw)]),
+                (k_hbm.at[0, m, :, pl.ds(g * DH, DH)], dst.at[:, pl.ds(bw, DH)]),
+                (v_hbm.at[0, m, :, pl.ds(g * DH, DH)], dst.at[:, pl.ds(bw + DH, DH)]),
+            )
+            for src, to in parts:
+                copies.append(pltpu.make_async_copy(src, to, sems.at[len(copies)]))
+    for c in copies:
+        c.start()
+    for c in copies:
+        c.wait()
 
 
 def pack_call(queries, keys, values, head_blocks, blocks_per_kv, interpret=False):
     _, micro_count, rows, width = queries.shape
-    key_width = keys.shape[3]
     bw = width // head_blocks
-    kv_in = pl.BlockSpec((1, 1, rows, key_width), lambda m: (0, m, 0, 0))
+    any_spec = pl.BlockSpec(memory_space=pl.ANY)
     return pl.pallas_call(
         functools.partial(pack_kernel, blocks_per_kv=blocks_per_kv),
-        grid=(micro_count,),
-        in_specs=[pl.BlockSpec((1, 1, rows, width), lambda m: (0, m, 0, 0)), kv_in, kv_in],
-        out_specs=[pl.BlockSpec((head_blocks, rows, bw + 2 * DH), lambda m: (m, 0, 0)),
-                   pl.BlockSpec((2, 1, 1, rows, key_width), lambda m: (0, 0, m, 0, 0))],
+        in_specs=[any_spec, any_spec, any_spec],
+        out_specs=[any_spec, any_spec],
         out_shape=[
             jax.ShapeDtypeStruct((micro_count * head_blocks, rows, bw + 2 * DH), jnp.bfloat16),
             jax.ShapeDtypeStruct((2,) + keys.shape, jnp.bfloat16),
         ],
+        scratch_shapes=[pltpu.SemaphoreType.DMA((2 + 3 * micro_count * head_blocks,))],
         interpret=interpret,
     )(queries, keys, values)
 

time: 124 us -> 202 us (1.63)
  the two profiles are of different devices: /device:TPU:227 before, /device:TPU:99 now
where the time goes in v10:
time: 202 us; the launch traced here: 201 us
  Pallas kernels  119 us (59%)
  waiting for transfers between devices  42.8 us (21%)
  starting transfers between devices  32.4 us (16%)
  local copies, waits for them, and re-layouts  4.12 us (2%)
  other arithmetic  2.23 us (1%)
    pallas_call x1, Pallas kernels, pack_call(): pl.pallas_call(functools.partial(pack_kernel, blocks_per_kv=blocks_per_kv...  81 us
    all_to_all x1, waiting for transfers between devices, device_body(): sent = lax.all_to_all(send, 'pipe', 0, 0)  26.4 us
    ppermute x5, starting transfers between devices, from_behind(): return lax.ppermute(block, axis, route)  17.5 us
    ppermute x5, waiting for transfers between devices, from_behind(): return lax.ppermute(block, axis, route)  16.4 us
    pallas_call x2, Pallas kernels, chain_call(): pl.pallas_call(functools.partial(chain_kernel, first=first, count=count),...  14.6 us
    pallas_call x2, Pallas kernels, layer_call(): pl.pallas_call(layer_kernel, grid=(1, kv_heads), in_specs=in_specs, out_s...  13.2 us
    pallas_call x1, Pallas kernels, layer_pre_call(): pl.pallas_call(layer_pre_kernel, grid=(micro_count, kv_heads), in_specs=[...  9.77 us
    all_to_all x1, starting transfers between devices, device_body(): grad_t = lax.all_to_all(grads_above, 'pipe', 0, 0)  7.91 us
  transfers between devices with their start and end apart: 7, of which 4 were waited for; matrix products, arithmetic and copies ran while one was open for 1% of the time, Pallas kernels for 12%

profile of v10, /device:TPU:99, one launch (start us, length us, event | category | flops | bytes accessed | tf_op | source)
XLA Modules:
  0.0 200.9 jit_solution(14116512716705794811)
XLA Ops:
  0.6 0.0 copy-start
  0.6 81.0 %shard_map.76 = (bf16[16,128,512]{2,1,0:T(8,128)(2,1)}, bf16[2,1,2,128,512]{4,3,2,1,0:T(8,128)(2,1)}) custom-call(bf16[1,2,128,2048]{3,2,1,0:T(8,128)(2,1)} %q_ref.5, bf16[1,2,128,512]{3,2,1,0:T(8,128)(2,1)} %k_hbm.1, bf16[1,2,128,512]{3,2,1,0:T(8,128)(2,1)} %v_hbm.1), custom_call_target="tpu_custom_call" | custom-call | tf_op jit(solution)/shard_map/pallas_call | solution.py:124
  81.6 0.0 copy-start.8
  81.6 6.9 %all-to-all-start = ((bf16[16,128,512]{2,1,0:T(8,128)(2,1)}), bf16[16,128,512]{2,1,0:T(8,128)(2,1)S(1)}, u32[]{:S(2)}, u32[]{:S(2)}) async-start(bf16[16,128,512]{2,1,0:T(8,128)(2,1)} %get-tuple-element.19), calls=%async_computation | async-start | bytes 4194304 | tf_op jit(solution)/shard_map/all_to_all | solution.py:280
  88.6 0.0 copy-done
  88.6 0.7 dynamic-slice_bitcast_fusion.1.g0_ref
  89.3 0.1 fusion.9
  89.4 26.4 %all-to-all-done.x_ref = bf16[16,128,512]{2,1,0:T(8,128)(2,1)S(1)} async-done(((bf16[16,128,512]{2,1,0:T(8,128)(2,1)}), bf16[16,128,512]{2,1,0:T(8,128)(2,1)S(1)}, u32[]{:S(2)}, u32[]{:S(2)}) %all-to-all-start) | async-done | bytes 2097184 | tf_op jit(solution)/shard_map/all_to_all | solution.py:280
  115.8 0.0 copy-start.2
  115.8 5.8 %collective-permute-start.2 = (bf16[8,128,256]{2,1,0:T(8,128)(2,1)S(1)}, bf16[8,128,256]{2,1,0:T(8,128)(2,1)}, u32[]{:S(2)}, u32[]{:S(2)}) collective-permute-start(bf16[8,128,256]{2,1,0:T(8,128)(2,1)S(1)} %slice.25), channel_id=1, source_target_pairs={{0,1},{1,2},{2,3},{3,4},{4,5},{5,6},{6,7},{7,8},{8,9},{9,10},{10,1... | collective-permute-start | bytes 1572872 | tf_op jit(solution)/shard_map/ppermute | solution.py:21
  121.6 0.0 copy-done.8
  121.6 0.8 slice.24
  122.4 1.9 collective-permute-start.1
  124.4 0.1 and_convert_fusion.m_ref
  124.5 0.0 copy-start.5
  124.5 0.7 dynamic-slice_bitcast_fusion.m_ref
  125.2 2.5 %collective-permute-done.2.halo_ref = bf16[8,128,256]{2,1,0:T(8,128)(2,1)} collective-permute-done((bf16[8,128,256]{2,1,0:T(8,128)(2,1)S(1)}, bf16[8,128,256]{2,1,0:T(8,128)(2,1)}, u32[]{:S(2)}, u32[]{:S(2)}) %collective-permute-start.2) | collective-permute-done | bytes 524320 | tf_op jit(solution)/shard_map/ppermute | solution.py:21
  127.7 0.0 copy-done.2
  127.7 7.4 %shard_map.77 = (bf16[16,128,256]{2,1,0:T(8,128)(2,1)}, bf16[128,256]{1,0:T(8,128)(2,1)}) custom-call(bf16[16,128,512]{2,1,0:T(8,128)(2,1)} %copy-done.2, bf16[8,128,256]{2,1,0:T(8,128)(2,1)} %collective-permute-done.2.halo_ref, bf16[128,256]{1,0:T(8,128)(2,1)} %dynamic-slice_bitcast_fusion.1.g0_ref, s32[128,256]{1,0:T(8,128)} %dynamic-slice_bitcast_fusion.m_ref), custom_call_target="tpu_custom_call" | custom-call | tf_op jit(solution)/shard_map/pallas_call | solution.py:84
  135.1 0.0 collective-permute-done.1.halo_ref
  135.1 0.0 copy-start.3
  135.1 7.2 %shard_map.78 = (bf16[16,128,256]{2,1,0:T(8,128)(2,1)}, bf16[128,256]{1,0:T(8,128)(2,1)}) custom-call(bf16[16,128,512]{2,1,0:T(8,128)(2,1)} %copy-done.2, bf16[7,128,256]{2,1,0:T(8,128)(2,1)} %collective-permute-done.1.halo_ref, bf16[128,256]{1,0:T(8,128)(2,1)} %get-tuple-element.20.g0_ref, s32[128,256]{1,0:T(8,128)} %dynamic-slice_bitcast_fusion.m_ref, ...), custom_call_target="tpu_custom_call" | custom-call | tf_op jit(solution)/shard_map/pallas_call | solution.py:84
  142.3 0.0 copy-done.5
  142.3 7.9 %all-to-all-start.1 = ((bf16[16,128,256]{2,1,0:T(8,128)(2,1)}), bf16[16,128,256]{2,1,0:T(8,128)(2,1)S(1)}, u32[]{:S(2)}, u32[]{:S(2)}) async-start(bf16[16,128,256]{2,1,0:T(8,128)(2,1)} %get-tuple-element.22), calls=%async_computation.1 | async-start | bytes 2097152 | tf_op jit(solution)/shard_map/all_to_all | solution.py:292
  150.2 0.0 copy-done.3
  150.2 6.0 %collective-permute-start = (bf16[2,1,2,128,512]{4,3,2,1,0:T(8,128)(2,1)S(1)}, bf16[2,1,2,128,512]{4,3,2,1,0:T(8,128)(2,1)S(1)}, u32[]{:S(2)}, u32[]{:S(2)}) collective-permute-start(bf16[2,1,2,128,512]{4,3,2,1,0:T(8,128)(2,1)S(1)} %copy-done.3), channel_id=1, source_target_pairs={{0,1},{1,2},{2,3},{3,4},{4,5},{5,6},{6,7},{7,8},{8,9},{9,10},{10,1... | collective-permute-start | bytes 1572872 | tf_op jit(solution)/shard_map/ppermute | solution.py:21
  156.2 6.1 %collective-permute-done.kvh_ref = bf16[2,1,2,128,512]{4,3,2,1,0:T(8,128)(2,1)S(1)} collective-permute-done((bf16[2,1,2,128,512]{4,3,2,1,0:T(8,128)(2,1)S(1)}, bf16[2,1,2,128,512]{4,3,2,1,0:T(8,128)(2,1)S(1)}, u32[]{:S(2)}, u32[]{:S(2)}) %collective-permute-start) | collective-permute-done | bytes 524320 | tf_op jit(solution)/shard_map/ppermute | solution.py:21
  162.3 0.0 copy-start.4
  162.3 0.9 copy-done.4
  163.2 9.8 %shard_map.79 = (f32[2,16,128,256]{3,2,1,0:T(8,128)}, f32[2,16,128,128]{3,2,1,0:T(8,128)}) custom-call(bf16[1,2,128,2048]{3,2,1,0:T(8,128)(2,1)} %q_ref.5, bf16[2,1,2,128,512]{4,3,2,1,0:T(8,128)(2,1)} %get-tuple-element.18.kvo_ref, bf16[2,1,2,128,512]{4,3,2,1,0:T(8,128)(2,1)} %copy-done.4, s32[2,128,256]{2,1,0:T(8,128)} %copy-done.5), custom_call_target="tpu_custom_call" | custom-call | tf_op jit(solution)/shard_map/pallas_call | solution.py:158
  173.0 0.0 all-to-all-done.1.ga_ref.gb_ref
  173.0 0.0 copy-start.1
  173.0 1.0 copy-done.1
  173.9 6.5 %shard_map.80 = (f32[1,128,512]{2,1,0:T(8,128)}, f32[1,128,512]{2,1,0:T(8,128)}, bf16[2,1,128,512]{3,2,1,0:T(8,128)(2,1)}, bf16[1,2,128,2048]{3,2,1,0:T(8,128)(2,1)}) custom-call(bf16[1,2,128,2048]{3,2,1,0:T(8,128)(2,1)} %q_ref.5, bf16[2,1,2,128,512]{4,3,2,1,0:T(8,128)(2,1)} %get-tuple-element.18.kvo_ref, bf16[2,1,2,128,512]{4,3,2,1,0:T(8,128)(2,1)} %copy-done.4, ...), custom_call_target="tpu_custom_call" | custom-call | tf_op jit(solution)/shard_map/pallas_call | solution.py:230
  180.5 1.9 collective-permute-start.3
  182.4 0.0 copy-start.6
  182.4 0.0 copy-start.7
  182.4 6.6 %shard_map.81 = (f32[1,128,512]{2,1,0:T(8,128)}, f32[1,128,512]{2,1,0:T(8,128)}, bf16[2,1,128,512]{3,2,1,0:T(8,128)(2,1)}, bf16[1,2,128,2048]{3,2,1,0:T(8,128)(2,1)}) custom-call(bf16[1,2,128,2048]{3,2,1,0:T(8,128)(2,1)} %q_ref.5, bf16[2,1,2,128,512]{4,3,2,1,0:T(8,128)(2,1)} %get-tuple-element.18.kvo_ref, ...), custom_call_target="tpu_custom_call", output_to_operand_aliasing={{3}: (7, {})} | custom-call | tf_op jit(solution)/shard_map/pallas_call | solution.py:230
  189.1 1.9 collective-permute-start.4
  191.0 0.0 collective-permute-done.3
  191.0 0.0 copy-done.6
  191.0 0.0 copy-done.7
  191.0 0.1 fusion.6
  191.1 7.8 %collective-permute-done.4 = bf16[2,1,128,512]{3,2,1,0:T(8,128)(2,1)S(1)} collective-permute-done((bf16[2,1,128,512]{3,2,1,0:T(8,128)(2,1)}, bf16[2,1,128,512]{3,2,1,0:T(8,128)(2,1)S(1)}, u32[]{:S(2)}, u32[]{:S(2)}) %collective-permute-start.4) | collective-permute-done | bytes 262176 | tf_op jit(solution)/shard_map/ppermute | solution.py:21
  198.9 1.1 fusion.7
  200.0 0.8 pad_maximum_fusion
  (6 shorter events, 0.1 us)
Async XLA Ops:
  0.6 88.0 %copy-start = (bf16[2,128,2048]{2,1,0:T(8,128)(2,1)S(1)}, bf16[2,128,2048]{2,1,0:T(8,128)(2,1)}, u32[]{:S(2)}) copy-start(bf16[2,128,2048]{2,1,0:T(8,128)(2,1)} %param.8) | copy-start | bytes 3145732
  81.6 40.0 %copy-start.8 = (s32[2,4096]{1,0:T(2,128)S(1)}, s32[2,4096]{1,0:T(2,128)}, u32[]{:S(2)}) copy-start(s32[2,4096]{1,0:T(2,128)} %param.9) | copy-start | bytes 98308
  81.6 34.1 %all-to-all-start = ((bf16[16,128,512]{2,1,0:T(8,128)(2,1)}), bf16[16,128,512]{2,1,0:T(8,128)(2,1)S(1)}, u32[]{:S(2)}, u32[]{:S(2)}) async-start(bf16[16,128,512]{2,1,0:T(8,128)(2,1)} %get-tuple-element.19), calls=%async_computation | async-start | bytes 4194304 | tf_op jit(solution)/shard_map/all_to_all | solution.py:280
  115.8 11.9 %copy-start.2 = (bf16[16,128,512]{2,1,0:T(8,128)(2,1)}, bf16[16,128,512]{2,1,0:T(8,128)(2,1)S(1)}, u32[]{:S(2)}) copy-start(bf16[16,128,512]{2,1,0:T(8,128)(2,1)S(1)} %all-to-all-done.x_ref) | copy-start | bytes 6291460
  115.8 11.9 %collective-permute-start.2 = (bf16[8,128,256]{2,1,0:T(8,128)(2,1)S(1)}, bf16[8,128,256]{2,1,0:T(8,128)(2,1)}, u32[]{:S(2)}, u32[]{:S(2)}) collective-permute-start(bf16[8,128,256]{2,1,0:T(8,128)(2,1)S(1)} %slice.25), channel_id=1, source_target_pairs={{0,1},{1,2},{2,3},{3,4},{4,5},{5,6},{6,7},{7,8},{8,9},{9,10},{10,1... | collective-permute-start | bytes 1572872 | tf_op jit(solution)/shard_map/ppermute | solution.py:21
  122.4 12.7 %collective-permute-start.1 = (bf16[7,128,256]{2,1,0:T(8,128)(2,1)}, bf16[7,128,256]{2,1,0:T(8,128)(2,1)}, u32[]{:S(2)}, u32[]{:S(2)}) collective-permute-start(bf16[7,128,256]{2,1,0:T(8,128)(2,1)} %slice.24), channel_id=1, source_target_pairs={{0,1},{1,2},{2,3},{3,4},{4,5},{5,6},{6,7},{7,8},{8,9},{9,10},{10,1... | collective-permute-start | bytes 1376264 | tf_op jit(solution)/shard_map/ppermute | solution.py:21
  124.5 17.8 %copy-start.5 = (s32[2,128,256]{2,1,0:T(8,128)}, s32[2,128,256]{2,1,0:T(8,128)S(1)}, u32[]{:S(2)}) copy-start(s32[2,128,256]{2,1,0:T(8,128)S(1)} %and_convert_fusion.m_ref) | copy-start | bytes 786436
  135.1 15.1 %copy-start.3 = (bf16[2,1,2,128,512]{4,3,2,1,0:T(8,128)(2,1)S(1)}, bf16[2,1,2,128,512]{4,3,2,1,0:T(8,128)(2,1)}, u32[]{:S(2)}) copy-start(bf16[2,1,2,128,512]{4,3,2,1,0:T(8,128)(2,1)} %get-tuple-element.18.kvo_ref) | copy-start | bytes 1572868
  142.3 30.7 %all-to-all-start.1 = ((bf16[16,128,256]{2,1,0:T(8,128)(2,1)}), bf16[16,128,256]{2,1,0:T(8,128)(2,1)S(1)}, u32[]{:S(2)}, u32[]{:S(2)}) async-start(bf16[16,128,256]{2,1,0:T(8,128)(2,1)} %get-tuple-element.22), calls=%async_computation.1 | async-start | bytes 2097152 | tf_op jit(solution)/shard_map/all_to_all | solution.py:292
  150.2 12.1 %collective-permute-start = (bf16[2,1,2,128,512]{4,3,2,1,0:T(8,128)(2,1)S(1)}, bf16[2,1,2,128,512]{4,3,2,1,0:T(8,128)(2,1)S(1)}, u32[]{:S(2)}, u32[]{:S(2)}) collective-permute-start(bf16[2,1,2,128,512]{4,3,2,1,0:T(8,128)(2,1)S(1)} %copy-done.3), channel_id=1, source_target_pairs={{0,1},{1,2},{2,3},{3,4},{4,5},{5,6},{6,7},{7,8},{8,9},{9,10},{10,1... | collective-permute-start | bytes 1572872 | tf_op jit(solution)/shard_map/ppermute | solution.py:21
  162.3 0.9 copy-start.4
  173.0 1.0 copy-start.1
  180.5 10.5 %collective-permute-start.3 = (bf16[2,1,128,512]{3,2,1,0:T(8,128)(2,1)}, bf16[2,1,128,512]{3,2,1,0:T(8,128)(2,1)S(1)}, u32[]{:S(2)}, u32[]{:S(2)}) collective-permute-start(bf16[2,1,128,512]{3,2,1,0:T(8,128)(2,1)} %get-tuple-element.28), channel_id=1, source_target_pairs={{1,0},{2,1},{3,2},{4,3},{5,4},{6,5},{7,6},{8,7},{9,8},{10,9},{11,1... | collective-permute-start | bytes 786440 | tf_op jit(solution)/shard_map/ppermute | solution.py:21
  182.4 8.6 %copy-start.6 = (f32[1,128,512]{2,1,0:T(8,128)S(1)}, f32[1,128,512]{2,1,0:T(8,128)}, u32[]{:S(2)}) copy-start(f32[1,128,512]{2,1,0:T(8,128)} %get-tuple-element.27) | copy-start | bytes 786436
  182.4 8.6 %copy-start.7 = (f32[1,128,512]{2,1,0:T(8,128)S(1)}, f32[1,128,512]{2,1,0:T(8,128)}, u32[]{:S(2)}) copy-start(f32[1,128,512]{2,1,0:T(8,128)} %get-tuple-element.31) | copy-start | bytes 786436
  189.1 9.9 %collective-permute-start.4 = (bf16[2,1,128,512]{3,2,1,0:T(8,128)(2,1)}, bf16[2,1,128,512]{3,2,1,0:T(8,128)(2,1)S(1)}, u32[]{:S(2)}, u32[]{:S(2)}) collective-permute-start(bf16[2,1,128,512]{3,2,1,0:T(8,128)(2,1)} %get-tuple-element.30), channel_id=1, source_target_pairs={{1,0},{2,1},{3,2},{4,3},{5,4},{6,5},{7,6},{8,7},{9,8},{10,9},{11,1... | collective-permute-start | bytes 786440 | tf_op jit(solution)/shard_map/ppermute | solution.py:21

commit v11 on v7

--- a/solution.py
+++ b/solution.py
@@ -34,7 +34,7 @@
     return prob_low, grad_score
 
 
-def chain_kernel(x_ref, halo_ref, g0_ref, m_ref, *rest, first, count):
+def chain_kernel(x_ref, halo_ref, g0_ref, m_ref, *rest, first, count, x_first):
     if len(rest) == 3:
         prev_ref, o_ref, g_out_ref = rest
     else:
@@ -44,25 +44,27 @@
     heads = width // DH
     halo_first = first + count - halo_ref.shape[0]
     allowed = m_ref[...] != 0
+    top = first + count - 1
     if prev_ref is None:
         o_ref[o_ref.shape[0] - 1] = g0_ref[...]
     else:
-        top = first + count - 1
-        o_ref[top:] = prev_ref[top:]
+        o_ref[top] = g0_ref[...]
+        o_ref[top + 1:] = prev_ref[top + 1 - (o_ref.shape[0] - prev_ref.shape[0]):]
 
     def step(i, g):
-        layer = first + count - 1 - i
+        layer = top - i
         local = layer - halo_first
+        xl = layer - x_first
         k = jnp.concatenate(
-            [halo_ref[local, :, :DH], x_ref[layer, :, width:width + DH]], axis=0
+            [halo_ref[local, :, :DH], x_ref[xl, :, width:width + DH]], axis=0
         )
         v = jnp.concatenate(
-            [halo_ref[local, :, DH:], x_ref[layer, :, width + DH:]], axis=0
+            [halo_ref[local, :, DH:], x_ref[xl, :, width + DH:]], axis=0
         )
         outs = []
         for h in range(heads):
             cols = slice(h * DH, (h + 1) * DH)
-            q = x_ref[layer, :, cols]
+            q = x_ref[xl, :, cols]
             gh = g[:, cols]
             _, grad_score = head_core(q, k, v, gh, allowed)
             dq = jnp.dot(grad_score, k, preferred_element_type=jnp.float32) * SCALE
@@ -75,13 +77,23 @@
 
 
 def chain_call(sent, halo, grad_top, allowed_i32, first, count, prev=None, interpret=False):
-    layers, rows, _ = sent.shape
+    layers, rows, total = sent.shape
     width = grad_top.shape[1]
+    half = layers // 2
+    x_block = (first + count - 1) // half
+    x_spec = pl.BlockSpec((half, rows, total), lambda i: (x_block, 0, 0))
     operands = [sent, halo, grad_top, allowed_i32]
+    full_specs = [pl.BlockSpec(a.shape, lambda i, n=a.ndim: (0,) * n) for a in operands[1:]]
+    in_specs = [x_spec] + full_specs
     if prev is not None:
         operands.append(prev)
+        in_specs.append(pl.BlockSpec((half, rows, width), lambda i: (1, 0, 0)))
     return pl.pallas_call(
-        functools.partial(chain_kernel, first=first, count=count),
+        functools.partial(chain_kernel, first=first, count=count, x_first=x_block * half),
+        in_specs=in_specs,
+        grid=(1,),
+        out_specs=(pl.BlockSpec((layers, rows, width), lambda i: (0, 0, 0)),
+                   pl.BlockSpec((rows, width), lambda i: (0, 0))),
         out_shape=(
             jax.ShapeDtypeStruct((layers, rows, width), jnp.bfloat16),
             jax.ShapeDtypeStruct((rows, width), jnp.bfloat16),

time: 124 us -> 123 us (level)
  the two profiles are of different devices: /device:TPU:227 before, /device:TPU:99 now
where the time goes in v11:
time: 123 us; the launch traced here: 122 us
  waiting for transfers between devices  42.8 us (35%)
  Pallas kernels  39.6 us (32%)
  starting transfers between devices  32.5 us (26%)
  local copies, waits for them, and re-layouts  4.11 us (3%)
  other arithmetic  2.23 us (2%)
    all_to_all x1, waiting for transfers between devices, device_body(): sent = lax.all_to_all(send, 'pipe', 0, 0)  26.4 us
    ppermute x5, starting transfers between devices, from_behind(): return lax.ppermute(block, axis, route)  17.5 us
    ppermute x5, waiting for transfers between devices, from_behind(): return lax.ppermute(block, axis, route)  16.4 us
    pallas_call x2, Pallas kernels, chain_call(): pl.pallas_call(functools.partial(chain_kernel, first=first, count=count,...  13.7 us
    pallas_call x2, Pallas kernels, layer_call(): pl.pallas_call(layer_kernel, grid=(1, kv_heads), in_specs=in_specs, out_s...  13.2 us
    pallas_call x1, Pallas kernels, layer_pre_call(): pl.pallas_call(layer_pre_kernel, grid=(micro_count, kv_heads), in_specs=[...  9.77 us
    all_to_all x1, starting transfers between devices, device_body(): grad_t = lax.all_to_all(grads_above, 'pipe', 0, 0)  7.91 us
    all_to_all x1, starting transfers between devices, device_body(): sent = lax.all_to_all(send, 'pipe', 0, 0)  7.05 us
  transfers between devices with their start and end apart: 7, of which 4 were waited for; matrix products, arithmetic and copies ran while one was open for 2% of the time, Pallas kernels for 19%

profile of v11, /device:TPU:99, one launch (start us, length us, event | category | flops | bytes accessed | tf_op | source)
XLA Modules:
  0.0 122.0 jit_solution(17506966522207594448)
XLA Ops:
  0.6 0.0 copy-start
  0.6 2.9 %shard_map.76 = (bf16[16,128,512]{2,1,0:T(8,128)(2,1)}, bf16[2,1,2,128,512]{4,3,2,1,0:T(8,128)(2,1)}) custom-call(bf16[1,2,128,2048]{3,2,1,0:T(8,128)(2,1)} %q_ref.7, bf16[1,2,128,512]{3,2,1,0:T(8,128)(2,1)} %k_ref.1, bf16[1,2,128,512]{3,2,1,0:T(8,128)(2,1)} %v_ref.1), custom_call_target="tpu_custom_call" | custom-call | tf_op jit(solution)/shard_map/pallas_call | solution.py:125
  3.6 0.0 copy-start.8
  3.6 7.0 %all-to-all-start = ((bf16[16,128,512]{2,1,0:T(8,128)(2,1)}), bf16[16,128,512]{2,1,0:T(8,128)(2,1)S(1)}, u32[]{:S(2)}, u32[]{:S(2)}) async-start(bf16[16,128,512]{2,1,0:T(8,128)(2,1)} %get-tuple-element.19), calls=%async_computation | async-start | bytes 4194304 | tf_op jit(solution)/shard_map/all_to_all | solution.py:282
  10.6 0.0 copy-done
  10.7 0.7 dynamic-slice_bitcast_fusion.1.g0_ref
  11.3 0.1 fusion.9
  11.4 26.4 %all-to-all-done.x_ref = bf16[16,128,512]{2,1,0:T(8,128)(2,1)S(1)} async-done(((bf16[16,128,512]{2,1,0:T(8,128)(2,1)}), bf16[16,128,512]{2,1,0:T(8,128)(2,1)S(1)}, u32[]{:S(2)}, u32[]{:S(2)}) %all-to-all-start) | async-done | bytes 2097184 | tf_op jit(solution)/shard_map/all_to_all | solution.py:282
  37.8 0.0 copy-start.2
  37.9 5.8 %collective-permute-start.2 = (bf16[8,128,256]{2,1,0:T(8,128)(2,1)S(1)}, bf16[8,128,256]{2,1,0:T(8,128)(2,1)}, u32[]{:S(2)}, u32[]{:S(2)}) collective-permute-start(bf16[8,128,256]{2,1,0:T(8,128)(2,1)S(1)} %slice.25), channel_id=1, source_target_pairs={{0,1},{1,2},{2,3},{3,4},{4,5},{5,6},{6,7},{7,8},{8,9},{9,10},{10,1... | collective-permute-start | bytes 1572872 | tf_op jit(solution)/shard_map/ppermute | solution.py:20
  43.7 0.0 copy-done.8
  43.7 0.8 slice.24
  44.5 1.9 %collective-permute-start.1 = (bf16[7,128,256]{2,1,0:T(8,128)(2,1)}, bf16[7,128,256]{2,1,0:T(8,128)(2,1)}, u32[]{:S(2)}, u32[]{:S(2)}) collective-permute-start(bf16[7,128,256]{2,1,0:T(8,128)(2,1)} %slice.24), channel_id=1, source_target_pairs={{0,1},{1,2},{2,3},{3,4},{4,5},{5,6},{6,7},{7,8},{8,9},{9,10},{10,1... | collective-permute-start | bytes 1376264 | tf_op jit(solution)/shard_map/ppermute | solution.py:20
  46.4 0.1 and_convert_fusion.m_ref
  46.5 0.0 copy-start.5
  46.5 0.7 dynamic-slice_bitcast_fusion.m_ref
  47.3 2.5 %collective-permute-done.2.halo_ref = bf16[8,128,256]{2,1,0:T(8,128)(2,1)} collective-permute-done((bf16[8,128,256]{2,1,0:T(8,128)(2,1)S(1)}, bf16[8,128,256]{2,1,0:T(8,128)(2,1)}, u32[]{:S(2)}, u32[]{:S(2)}) %collective-permute-start.2) | collective-permute-done | bytes 524320 | tf_op jit(solution)/shard_map/ppermute | solution.py:20
  49.8 0.0 copy-done.2
  49.8 7.0 %shard_map.77 = (bf16[16,128,256]{2,1,0:T(8,128)(2,1)}, bf16[128,256]{1,0:T(8,128)(2,1)}) custom-call(bf16[16,128,512]{2,1,0:T(8,128)(2,1)} %copy-done.2, bf16[8,128,256]{2,1,0:T(8,128)(2,1)} %collective-permute-done.2.halo_ref, bf16[128,256]{1,0:T(8,128)(2,1)} %dynamic-slice_bitcast_fusion.1.g0_ref, s32[128,256]{1,0:T(8,128)} %dynamic-slice_bitcast_fusion.m_ref), custom_call_target="tpu_custom_call" | custom-call | tf_op jit(solution)/shard_map/pallas_call | solution.py:91
  56.8 0.0 collective-permute-done.1.halo_ref
  56.8 0.0 copy-start.3
  56.8 6.7 %shard_map.78 = (bf16[16,128,256]{2,1,0:T(8,128)(2,1)}, bf16[128,256]{1,0:T(8,128)(2,1)}) custom-call(bf16[16,128,512]{2,1,0:T(8,128)(2,1)} %copy-done.2, bf16[7,128,256]{2,1,0:T(8,128)(2,1)} %collective-permute-done.1.halo_ref, bf16[128,256]{1,0:T(8,128)(2,1)} %get-tuple-element.20.g0_ref, s32[128,256]{1,0:T(8,128)} %dynamic-slice_bitcast_fusion.m_ref, ...), custom_call_target="tpu_custom_call" | custom-call | tf_op jit(solution)/shard_map/pallas_call | solution.py:91
  63.5 0.0 copy-done.5
  63.5 7.9 %all-to-all-start.1 = ((bf16[16,128,256]{2,1,0:T(8,128)(2,1)}), bf16[16,128,256]{2,1,0:T(8,128)(2,1)S(1)}, u32[]{:S(2)}, u32[]{:S(2)}) async-start(bf16[16,128,256]{2,1,0:T(8,128)(2,1)} %get-tuple-element.22), calls=%async_computation.1 | async-start | bytes 2097152 | tf_op jit(solution)/shard_map/all_to_all | solution.py:294
  71.4 0.0 copy-done.3
  71.4 6.0 %collective-permute-start = (bf16[2,1,2,128,512]{4,3,2,1,0:T(8,128)(2,1)S(1)}, bf16[2,1,2,128,512]{4,3,2,1,0:T(8,128)(2,1)S(1)}, u32[]{:S(2)}, u32[]{:S(2)}) collective-permute-start(bf16[2,1,2,128,512]{4,3,2,1,0:T(8,128)(2,1)S(1)} %copy-done.3), channel_id=1, source_target_pairs={{0,1},{1,2},{2,3},{3,4},{4,5},{5,6},{6,7},{7,8},{8,9},{9,10},{10,1... | collective-permute-start | bytes 1572872 | tf_op jit(solution)/shard_map/ppermute | solution.py:20
  77.4 6.1 %collective-permute-done.kvh_ref = bf16[2,1,2,128,512]{4,3,2,1,0:T(8,128)(2,1)S(1)} collective-permute-done((bf16[2,1,2,128,512]{4,3,2,1,0:T(8,128)(2,1)S(1)}, bf16[2,1,2,128,512]{4,3,2,1,0:T(8,128)(2,1)S(1)}, u32[]{:S(2)}, u32[]{:S(2)}) %collective-permute-start) | collective-permute-done | bytes 524320 | tf_op jit(solution)/shard_map/ppermute | solution.py:20
  83.5 0.0 copy-start.4
  83.5 0.9 copy-done.4
  84.4 9.8 %shard_map.79 = (f32[2,16,128,256]{3,2,1,0:T(8,128)}, f32[2,16,128,128]{3,2,1,0:T(8,128)}) custom-call(bf16[1,2,128,2048]{3,2,1,0:T(8,128)(2,1)} %q_ref.7, bf16[2,1,2,128,512]{4,3,2,1,0:T(8,128)(2,1)} %get-tuple-element.18.kvo_ref, bf16[2,1,2,128,512]{4,3,2,1,0:T(8,128)(2,1)} %copy-done.4, s32[2,128,256]{2,1,0:T(8,128)} %copy-done.5), custom_call_target="tpu_custom_call" | custom-call | tf_op jit(solution)/shard_map/pallas_call | solution.py:160
  94.2 0.0 all-to-all-done.1.ga_ref.gb_ref
  94.2 0.0 copy-start.1
  94.2 1.0 copy-done.1
  95.1 6.5 %shard_map.80 = (f32[1,128,512]{2,1,0:T(8,128)}, f32[1,128,512]{2,1,0:T(8,128)}, bf16[2,1,128,512]{3,2,1,0:T(8,128)(2,1)}, bf16[1,2,128,2048]{3,2,1,0:T(8,128)(2,1)}) custom-call(bf16[1,2,128,2048]{3,2,1,0:T(8,128)(2,1)} %q_ref.7, bf16[2,1,2,128,512]{4,3,2,1,0:T(8,128)(2,1)} %get-tuple-element.18.kvo_ref, bf16[2,1,2,128,512]{4,3,2,1,0:T(8,128)(2,1)} %copy-done.4, ...), custom_call_target="tpu_custom_call" | custom-call | tf_op jit(solution)/shard_map/pallas_call | solution.py:232
  101.7 1.9 %collective-permute-start.3 = (bf16[2,1,128,512]{3,2,1,0:T(8,128)(2,1)}, bf16[2,1,128,512]{3,2,1,0:T(8,128)(2,1)S(1)}, u32[]{:S(2)}, u32[]{:S(2)}) collective-permute-start(bf16[2,1,128,512]{3,2,1,0:T(8,128)(2,1)} %get-tuple-element.28), channel_id=1, source_target_pairs={{1,0},{2,1},{3,2},{4,3},{5,4},{6,5},{7,6},{8,7},{9,8},{10,9},{11,1... | collective-permute-start | bytes 786440 | tf_op jit(solution)/shard_map/ppermute | solution.py:20
  103.6 0.0 copy-start.6
  103.6 0.0 copy-start.7
  103.6 6.6 %shard_map.81 = (f32[1,128,512]{2,1,0:T(8,128)}, f32[1,128,512]{2,1,0:T(8,128)}, bf16[2,1,128,512]{3,2,1,0:T(8,128)(2,1)}, bf16[1,2,128,2048]{3,2,1,0:T(8,128)(2,1)}) custom-call(bf16[1,2,128,2048]{3,2,1,0:T(8,128)(2,1)} %q_ref.7, bf16[2,1,2,128,512]{4,3,2,1,0:T(8,128)(2,1)} %get-tuple-element.18.kvo_ref, ...), custom_call_target="tpu_custom_call", output_to_operand_aliasing={{3}: (7, {})} | custom-call | tf_op jit(solution)/shard_map/pallas_call | solution.py:232
  110.2 1.9 %collective-permute-start.4 = (bf16[2,1,128,512]{3,2,1,0:T(8,128)(2,1)}, bf16[2,1,128,512]{3,2,1,0:T(8,128)(2,1)S(1)}, u32[]{:S(2)}, u32[]{:S(2)}) collective-permute-start(bf16[2,1,128,512]{3,2,1,0:T(8,128)(2,1)} %get-tuple-element.30), channel_id=1, source_target_pairs={{1,0},{2,1},{3,2},{4,3},{5,4},{6,5},{7,6},{8,7},{9,8},{10,9},{11,1... | collective-permute-start | bytes 786440 | tf_op jit(solution)/shard_map/ppermute | solution.py:20
  112.2 0.0 collective-permute-done.3
  112.2 0.0 copy-done.6
  112.2 0.0 copy-done.7
  112.2 0.1 fusion.6
  112.3 7.8 %collective-permute-done.4 = bf16[2,1,128,512]{3,2,1,0:T(8,128)(2,1)S(1)} collective-permute-done((bf16[2,1,128,512]{3,2,1,0:T(8,128)(2,1)}, bf16[2,1,128,512]{3,2,1,0:T(8,128)(2,1)S(1)}, u32[]{:S(2)}, u32[]{:S(2)}) %collective-permute-start.4) | collective-permute-done | bytes 262176 | tf_op jit(solution)/shard_map/ppermute | solution.py:20
  120.1 1.1 fusion.7
  121.2 0.8 pad_maximum_fusion
  (6 shorter events, 0.1 us)
Async XLA Ops:
  0.6 10.0 %copy-start = (bf16[2,128,2048]{2,1,0:T(8,128)(2,1)S(1)}, bf16[2,128,2048]{2,1,0:T(8,128)(2,1)}, u32[]{:S(2)}) copy-start(bf16[2,128,2048]{2,1,0:T(8,128)(2,1)} %param.8) | copy-start | bytes 3145732
  3.6 40.1 %copy-start.8 = (s32[2,4096]{1,0:T(2,128)S(1)}, s32[2,4096]{1,0:T(2,128)}, u32[]{:S(2)}) copy-start(s32[2,4096]{1,0:T(2,128)} %param.9) | copy-start | bytes 98308
  3.6 34.3 %all-to-all-start = ((bf16[16,128,512]{2,1,0:T(8,128)(2,1)}), bf16[16,128,512]{2,1,0:T(8,128)(2,1)S(1)}, u32[]{:S(2)}, u32[]{:S(2)}) async-start(bf16[16,128,512]{2,1,0:T(8,128)(2,1)} %get-tuple-element.19), calls=%async_computation | async-start | bytes 4194304 | tf_op jit(solution)/shard_map/all_to_all | solution.py:282
  37.8 11.9 %copy-start.2 = (bf16[16,128,512]{2,1,0:T(8,128)(2,1)}, bf16[16,128,512]{2,1,0:T(8,128)(2,1)S(1)}, u32[]{:S(2)}) copy-start(bf16[16,128,512]{2,1,0:T(8,128)(2,1)S(1)} %all-to-all-done.x_ref) | copy-start | bytes 6291460
  37.9 11.9 %collective-permute-start.2 = (bf16[8,128,256]{2,1,0:T(8,128)(2,1)S(1)}, bf16[8,128,256]{2,1,0:T(8,128)(2,1)}, u32[]{:S(2)}, u32[]{:S(2)}) collective-permute-start(bf16[8,128,256]{2,1,0:T(8,128)(2,1)S(1)} %slice.25), channel_id=1, source_target_pairs={{0,1},{1,2},{2,3},{3,4},{4,5},{5,6},{6,7},{7,8},{8,9},{9,10},{10,1... | collective-permute-start | bytes 1572872 | tf_op jit(solution)/shard_map/ppermute | solution.py:20
  44.5 12.3 %collective-permute-start.1 = (bf16[7,128,256]{2,1,0:T(8,128)(2,1)}, bf16[7,128,256]{2,1,0:T(8,128)(2,1)}, u32[]{:S(2)}, u32[]{:S(2)}) collective-permute-start(bf16[7,128,256]{2,1,0:T(8,128)(2,1)} %slice.24), channel_id=1, source_target_pairs={{0,1},{1,2},{2,3},{3,4},{4,5},{5,6},{6,7},{7,8},{8,9},{9,10},{10,1... | collective-permute-start | bytes 1376264 | tf_op jit(solution)/shard_map/ppermute | solution.py:20
  46.5 17.0 %copy-start.5 = (s32[2,128,256]{2,1,0:T(8,128)}, s32[2,128,256]{2,1,0:T(8,128)S(1)}, u32[]{:S(2)}) copy-start(s32[2,128,256]{2,1,0:T(8,128)S(1)} %and_convert_fusion.m_ref) | copy-start | bytes 786436
  56.8 14.7 %copy-start.3 = (bf16[2,1,2,128,512]{4,3,2,1,0:T(8,128)(2,1)S(1)}, bf16[2,1,2,128,512]{4,3,2,1,0:T(8,128)(2,1)}, u32[]{:S(2)}) copy-start(bf16[2,1,2,128,512]{4,3,2,1,0:T(8,128)(2,1)} %get-tuple-element.18.kvo_ref) | copy-start | bytes 1572868
  63.5 30.7 %all-to-all-start.1 = ((bf16[16,128,256]{2,1,0:T(8,128)(2,1)}), bf16[16,128,256]{2,1,0:T(8,128)(2,1)S(1)}, u32[]{:S(2)}, u32[]{:S(2)}) async-start(bf16[16,128,256]{2,1,0:T(8,128)(2,1)} %get-tuple-element.22), calls=%async_computation.1 | async-start | bytes 2097152 | tf_op jit(solution)/shard_map/all_to_all | solution.py:294
  71.4 12.1 %collective-permute-start = (bf16[2,1,2,128,512]{4,3,2,1,0:T(8,128)(2,1)S(1)}, bf16[2,1,2,128,512]{4,3,2,1,0:T(8,128)(2,1)S(1)}, u32[]{:S(2)}, u32[]{:S(2)}) collective-permute-start(bf16[2,1,2,128,512]{4,3,2,1,0:T(8,128)(2,1)S(1)} %copy-done.3), channel_id=1, source_target_pairs={{0,1},{1,2},{2,3},{3,4},{4,5},{5,6},{6,7},{7,8},{8,9},{9,10},{10,1... | collective-permute-start | bytes 1572872 | tf_op jit(solution)/shard_map/ppermute | solution.py:20
  83.5 0.9 copy-start.4
  94.2 1.0 copy-start.1
  101.7 10.5 %collective-permute-start.3 = (bf16[2,1,128,512]{3,2,1,0:T(8,128)(2,1)}, bf16[2,1,128,512]{3,2,1,0:T(8,128)(2,1)S(1)}, u32[]{:S(2)}, u32[]{:S(2)}) collective-permute-start(bf16[2,1,128,512]{3,2,1,0:T(8,128)(2,1)} %get-tuple-element.28), channel_id=1, source_target_pairs={{1,0},{2,1},{3,2},{4,3},{5,4},{6,5},{7,6},{8,7},{9,8},{10,9},{11,1... | collective-permute-start | bytes 786440 | tf_op jit(solution)/shard_map/ppermute | solution.py:20
  103.6 8.6 %copy-start.6 = (f32[1,128,512]{2,1,0:T(8,128)S(1)}, f32[1,128,512]{2,1,0:T(8,128)}, u32[]{:S(2)}) copy-start(f32[1,128,512]{2,1,0:T(8,128)} %get-tuple-element.27) | copy-start | bytes 786436
  103.6 8.6 %copy-start.7 = (f32[1,128,512]{2,1,0:T(8,128)S(1)}, f32[1,128,512]{2,1,0:T(8,128)}, u32[]{:S(2)}) copy-start(f32[1,128,512]{2,1,0:T(8,128)} %get-tuple-element.31) | copy-start | bytes 786436
  110.2 9.9 %collective-permute-start.4 = (bf16[2,1,128,512]{3,2,1,0:T(8,128)(2,1)}, bf16[2,1,128,512]{3,2,1,0:T(8,128)(2,1)S(1)}, u32[]{:S(2)}, u32[]{:S(2)}) collective-permute-start(bf16[2,1,128,512]{3,2,1,0:T(8,128)(2,1)} %get-tuple-element.30), channel_id=1, source_target_pairs={{1,0},{2,1},{3,2},{4,3},{5,4},{6,5},{7,6},{8,7},{9,8},{10,9},{11,1... | collective-permute-start | bytes 786440 | tf_op jit(solution)/shard_map/ppermute | solution.py:20

commit v12 on v11

--- a/solution.py
+++ b/solution.py
@@ -173,16 +173,26 @@
     )(queries, kv_own, kv_halo, allowed_i32)
 
 
-def layer_kernel(q_ref, kvo_ref, kvh_ref, ga_ref, gb_ref, p_ref, o_ref, *rest):
+def layer_kernel(q_ref, kvo_ref, kvh_ref, g_ref, p_ref, o_ref, *rest):
     dk_ref, dv_ref, back_ref, gl_ref = rest[-4:]
-    heads = q_ref.shape[3] // DH
+    pairs = kvo_ref.shape[4] // DH
+    heads = q_ref.shape[3] // (DH * pairs)
     rows = q_ref.shape[2]
-    k = jnp.concatenate([kvh_ref[0, 0, 0], kvo_ref[0, 0, 0]], axis=0)
-    v = jnp.concatenate([kvh_ref[1, 0, 0], kvo_ref[1, 0, 0]], axis=0)
-    grad = jnp.concatenate([ga_ref[0], gb_ref[0]], axis=-1)
+    grad = jnp.concatenate([g_ref[j] for j in range(g_ref.shape[0])], axis=-1)
+    for c in range(pairs):
+        kc = slice(c * DH, (c + 1) * DH)
+        layer_group(q_ref, kvo_ref, kvh_ref, grad, p_ref, o_ref, dk_ref, dv_ref, back_ref,
+                    gl_ref, c, kc, heads, rows)
+
+
+def layer_group(q_ref, kvo_ref, kvh_ref, grad, p_ref, o_ref, dk_ref, dv_ref, back_ref,
+                gl_ref, c, kc, heads, rows):
+    k = jnp.concatenate([kvh_ref[0, 0, 0, :, kc], kvo_ref[0, 0, 0, :, kc]], axis=0)
+    v = jnp.concatenate([kvh_ref[1, 0, 0, :, kc], kvo_ref[1, 0, 0, :, kc]], axis=0)
     dk = None
     dv = None
-    for h in range(heads):
+    for hh in range(heads):
+        h = c * heads + hh
         cols = slice(h * DH, (h + 1) * DH)
         q = q_ref[0, 0, :, cols]
         g = grad[:, cols]
@@ -198,10 +208,10 @@
         dk = dk_h if dk is None else dk + dk_h
         dv = dv_h if dv is None else dv + dv_h
     dk = dk * SCALE
-    back_ref[0, 0] = dk[:rows].astype(back_ref.dtype)
-    back_ref[1, 0] = dv[:rows].astype(back_ref.dtype)
-    dk_ref[0] = dk[rows:]
-    dv_ref[0] = dv[rows:]
+    back_ref[0, 0, :, kc] = dk[:rows].astype(back_ref.dtype)
+    back_ref[1, 0, :, kc] = dv[:rows].astype(back_ref.dtype)
+    dk_ref[0, :, kc] = dk[rows:]
+    dv_ref[0, :, kc] = dv[rows:]
 
 
 def layer_call(queries, kv_own, kv_halo, grad_t, prob, out, grad_prev, micro,
@@ -211,19 +221,18 @@
     group = width // (kv_heads * DH)
     gw = group * DH
     bw = grad_t.shape[2]
-    kv_spec = pl.BlockSpec((2, 1, 1, rows, DH), lambda i, g: (0, 0, micro, 0, g))
-    q_spec = pl.BlockSpec((1, 1, rows, gw), lambda i, g: (0, micro, 0, g))
-    head_blocks = width // bw
-    ga_spec = pl.BlockSpec(
-        (1, rows, bw), lambda i, g: (micro * head_blocks + g * blocks_per_kv, 0, 0))
-    gb_spec = pl.BlockSpec(
-        (1, rows, bw), lambda i, g: (micro * head_blocks + g * blocks_per_kv + 1, 0, 0))
-    p_spec = pl.BlockSpec((1, group, rows, 2 * rows), lambda i, g: (micro, g, 0, 0))
-    o_spec = pl.BlockSpec((1, group, rows, DH), lambda i, g: (micro, g, 0, 0))
-    own_out = pl.BlockSpec((1, rows, DH), lambda i, g: (0, 0, g))
+    pairs = 2
+    kv_spec = pl.BlockSpec((2, 1, 1, rows, pairs * DH), lambda i, g: (0, 0, micro, 0, g))
+    q_spec = pl.BlockSpec((1, 1, rows, pairs * gw), lambda i, g: (0, micro, 0, g))
+    steps = kv_heads // pairs
+    g_spec = pl.BlockSpec(
+        (pairs * blocks_per_kv, rows, bw), lambda i, g: (micro * steps + g, 0, 0))
+    p_spec = pl.BlockSpec((1, pairs * group, rows, 2 * rows), lambda i, g: (micro, g, 0, 0))
+    o_spec = pl.BlockSpec((1, pairs * group, rows, DH), lambda i, g: (micro, g, 0, 0))
+    own_out = pl.BlockSpec((1, rows, pairs * DH), lambda i, g: (0, 0, g))
     own_shape = jax.ShapeDtypeStruct((1, rows, kv_heads * DH), jnp.float32)
-    in_specs = [q_spec, kv_spec, kv_spec, ga_spec, gb_spec, p_spec, o_spec]
-    operands = [queries, kv_own, kv_halo, grad_t, grad_t, prob, out]
+    in_specs = [q_spec, kv_spec, kv_spec, g_spec, p_spec, o_spec]
+    operands = [queries, kv_own, kv_halo, grad_t, prob, out]
     aliases = {}
     if grad_prev is not None:
         in_specs.append(pl.BlockSpec(memory_space=pl.ANY))
@@ -231,10 +240,10 @@
         aliases = {len(operands) - 1: 3}
     return pl.pallas_call(
         layer_kernel,
-        grid=(1, kv_heads),
+        grid=(1, steps),
         in_specs=in_specs,
         out_specs=[own_out, own_out,
-                   pl.BlockSpec((2, 1, rows, DH), lambda i, g: (0, 0, 0, g)),
+                   pl.BlockSpec((2, 1, rows, pairs * DH), lambda i, g: (0, 0, 0, g)),
                    q_spec],
         out_shape=[own_shape, own_shape,
                    jax.ShapeDtypeStruct((2, 1, rows, kv_heads * DH), jnp.bfloat16),

time: 123 us -> 122 us (level)
  no operation moved by 1% of the time
where the time goes in v12:
time: 122 us; the launch traced here: 121 us
  waiting for transfers between devices  42.8 us (35%)
  Pallas kernels  38.6 us (32%)
  starting transfers between devices  32.5 us (27%)
  local copies, waits for them, and re-layouts  4.11 us (3%)
  other arithmetic  2.23 us (2%)
    all_to_all x1, waiting for transfers between devices, device_body(): sent = lax.all_to_all(send, 'pipe', 0, 0)  26.4 us
    ppermute x5, starting transfers between devices, from_behind(): return lax.ppermute(block, axis, route)  17.5 us
    ppermute x5, waiting for transfers between devices, from_behind(): return lax.ppermute(block, axis, route)  16.4 us
    pallas_call x2, Pallas kernels, chain_call(): pl.pallas_call(functools.partial(chain_kernel, first=first, count=count,...  13.7 us
    pallas_call x2, Pallas kernels, layer_call(): pl.pallas_call(layer_kernel, grid=(1, steps), in_specs=in_specs, out_spec...  12.2 us
    pallas_call x1, Pallas kernels, layer_pre_call(): pl.pallas_call(layer_pre_kernel, grid=(micro_count, kv_heads), in_specs=[...  9.77 us
    all_to_all x1, starting transfers between devices, device_body(): grad_t = lax.all_to_all(grads_above, 'pipe', 0, 0)  7.91 us
    all_to_all x1, starting transfers between devices, device_body(): sent = lax.all_to_all(send, 'pipe', 0, 0)  7.05 us
  transfers between devices with their start and end apart: 7, of which 4 were waited for; matrix products, arithmetic and copies ran while one was open for 2% of the time, Pallas kernels for 19%

profile of v12, /device:TPU:99, one launch (start us, length us, event | category | flops | bytes accessed | tf_op | source)
XLA Modules:
  0.0 121.0 jit_solution(12994101928643084152)
XLA Ops:
  0.6 0.0 copy-start
  0.6 2.9 %shard_map.76 = (bf16[16,128,512]{2,1,0:T(8,128)(2,1)}, bf16[2,1,2,128,512]{4,3,2,1,0:T(8,128)(2,1)}) custom-call(bf16[1,2,128,2048]{3,2,1,0:T(8,128)(2,1)} %q_ref.7, bf16[1,2,128,512]{3,2,1,0:T(8,128)(2,1)} %k_ref.1, bf16[1,2,128,512]{3,2,1,0:T(8,128)(2,1)} %v_ref.1), custom_call_target="tpu_custom_call" | custom-call | tf_op jit(solution)/shard_map/pallas_call | solution.py:125
  3.6 0.0 copy-start.8
  3.6 7.0 %all-to-all-start = ((bf16[16,128,512]{2,1,0:T(8,128)(2,1)}), bf16[16,128,512]{2,1,0:T(8,128)(2,1)S(1)}, u32[]{:S(2)}, u32[]{:S(2)}) async-start(bf16[16,128,512]{2,1,0:T(8,128)(2,1)} %get-tuple-element.19), calls=%async_computation | async-start | bytes 4194304 | tf_op jit(solution)/shard_map/all_to_all | solution.py:291
  10.6 0.0 copy-done
  10.7 0.7 dynamic-slice_bitcast_fusion.1.g0_ref
  11.3 0.1 fusion.9
  11.4 26.4 %all-to-all-done.x_ref = bf16[16,128,512]{2,1,0:T(8,128)(2,1)S(1)} async-done(((bf16[16,128,512]{2,1,0:T(8,128)(2,1)}), bf16[16,128,512]{2,1,0:T(8,128)(2,1)S(1)}, u32[]{:S(2)}, u32[]{:S(2)}) %all-to-all-start) | async-done | bytes 2097184 | tf_op jit(solution)/shard_map/all_to_all | solution.py:291
  37.8 0.0 copy-start.1
  37.9 5.8 %collective-permute-start.2 = (bf16[8,128,256]{2,1,0:T(8,128)(2,1)S(1)}, bf16[8,128,256]{2,1,0:T(8,128)(2,1)}, u32[]{:S(2)}, u32[]{:S(2)}) collective-permute-start(bf16[8,128,256]{2,1,0:T(8,128)(2,1)S(1)} %slice.25), channel_id=1, source_target_pairs={{0,1},{1,2},{2,3},{3,4},{4,5},{5,6},{6,7},{7,8},{8,9},{9,10},{10,1... | collective-permute-start | bytes 1572872 | tf_op jit(solution)/shard_map/ppermute | solution.py:20
  43.7 0.0 copy-done.8
  43.7 0.8 slice.24
  44.5 1.9 %collective-permute-start.1 = (bf16[7,128,256]{2,1,0:T(8,128)(2,1)}, bf16[7,128,256]{2,1,0:T(8,128)(2,1)}, u32[]{:S(2)}, u32[]{:S(2)}) collective-permute-start(bf16[7,128,256]{2,1,0:T(8,128)(2,1)} %slice.24), channel_id=1, source_target_pairs={{0,1},{1,2},{2,3},{3,4},{4,5},{5,6},{6,7},{7,8},{8,9},{9,10},{10,1... | collective-permute-start | bytes 1376264 | tf_op jit(solution)/shard_map/ppermute | solution.py:20
  46.4 0.1 and_convert_fusion.m_ref
  46.5 0.0 copy-start.5
  46.5 0.7 dynamic-slice_bitcast_fusion.m_ref
  47.3 2.5 %collective-permute-done.2.halo_ref = bf16[8,128,256]{2,1,0:T(8,128)(2,1)} collective-permute-done((bf16[8,128,256]{2,1,0:T(8,128)(2,1)S(1)}, bf16[8,128,256]{2,1,0:T(8,128)(2,1)}, u32[]{:S(2)}, u32[]{:S(2)}) %collective-permute-start.2) | collective-permute-done | bytes 524320 | tf_op jit(solution)/shard_map/ppermute | solution.py:20
  49.8 0.0 copy-done.1
  49.8 7.0 %shard_map.77 = (bf16[16,128,256]{2,1,0:T(8,128)(2,1)}, bf16[128,256]{1,0:T(8,128)(2,1)}) custom-call(bf16[16,128,512]{2,1,0:T(8,128)(2,1)} %copy-done.1, bf16[8,128,256]{2,1,0:T(8,128)(2,1)} %collective-permute-done.2.halo_ref, bf16[128,256]{1,0:T(8,128)(2,1)} %dynamic-slice_bitcast_fusion.1.g0_ref, s32[128,256]{1,0:T(8,128)} %dynamic-slice_bitcast_fusion.m_ref), custom_call_target="tpu_custom_call" | custom-call | tf_op jit(solution)/shard_map/pallas_call | solution.py:91
  56.8 0.0 collective-permute-done.1.halo_ref
  56.8 0.0 copy-start.3
  56.8 6.7 %shard_map.78 = (bf16[16,128,256]{2,1,0:T(8,128)(2,1)}, bf16[128,256]{1,0:T(8,128)(2,1)}) custom-call(bf16[16,128,512]{2,1,0:T(8,128)(2,1)} %copy-done.1, bf16[7,128,256]{2,1,0:T(8,128)(2,1)} %collective-permute-done.1.halo_ref, bf16[128,256]{1,0:T(8,128)(2,1)} %get-tuple-element.20.g0_ref, s32[128,256]{1,0:T(8,128)} %dynamic-slice_bitcast_fusion.m_ref, ...), custom_call_target="tpu_custom_call" | custom-call | tf_op jit(solution)/shard_map/pallas_call | solution.py:91
  63.5 0.0 copy-done.5
  63.5 7.9 %all-to-all-start.1 = ((bf16[16,128,256]{2,1,0:T(8,128)(2,1)}), bf16[16,128,256]{2,1,0:T(8,128)(2,1)S(1)}, u32[]{:S(2)}, u32[]{:S(2)}) async-start(bf16[16,128,256]{2,1,0:T(8,128)(2,1)} %get-tuple-element.22), calls=%async_computation.1 | async-start | bytes 2097152 | tf_op jit(solution)/shard_map/all_to_all | solution.py:303
  71.4 0.0 copy-done.3
  71.4 6.0 %collective-permute-start = (bf16[2,1,2,128,512]{4,3,2,1,0:T(8,128)(2,1)S(1)}, bf16[2,1,2,128,512]{4,3,2,1,0:T(8,128)(2,1)S(1)}, u32[]{:S(2)}, u32[]{:S(2)}) collective-permute-start(bf16[2,1,2,128,512]{4,3,2,1,0:T(8,128)(2,1)S(1)} %copy-done.3), channel_id=1, source_target_pairs={{0,1},{1,2},{2,3},{3,4},{4,5},{5,6},{6,7},{7,8},{8,9},{9,10},{10,1... | collective-permute-start | bytes 1572872 | tf_op jit(solution)/shard_map/ppermute | solution.py:20
  77.4 6.1 %collective-permute-done.kvh_ref = bf16[2,1,2,128,512]{4,3,2,1,0:T(8,128)(2,1)S(1)} collective-permute-done((bf16[2,1,2,128,512]{4,3,2,1,0:T(8,128)(2,1)S(1)}, bf16[2,1,2,128,512]{4,3,2,1,0:T(8,128)(2,1)S(1)}, u32[]{:S(2)}, u32[]{:S(2)}) %collective-permute-start) | collective-permute-done | bytes 524320 | tf_op jit(solution)/shard_map/ppermute | solution.py:20
  83.5 0.0 copy-start.4
  83.5 0.9 copy-done.4
  84.4 9.8 %shard_map.79 = (f32[2,16,128,256]{3,2,1,0:T(8,128)}, f32[2,16,128,128]{3,2,1,0:T(8,128)}) custom-call(bf16[1,2,128,2048]{3,2,1,0:T(8,128)(2,1)} %q_ref.7, bf16[2,1,2,128,512]{4,3,2,1,0:T(8,128)(2,1)} %get-tuple-element.18.kvo_ref, bf16[2,1,2,128,512]{4,3,2,1,0:T(8,128)(2,1)} %copy-done.4, s32[2,128,256]{2,1,0:T(8,128)} %copy-done.5), custom_call_target="tpu_custom_call" | custom-call | tf_op jit(solution)/shard_map/pallas_call | solution.py:160
  94.2 0.0 all-to-all-done.1.g_ref
  94.2 0.0 copy-start.2
  94.2 1.0 copy-done.2
  95.1 6.0 %shard_map.80 = (f32[1,128,512]{2,1,0:T(8,128)}, f32[1,128,512]{2,1,0:T(8,128)}, bf16[2,1,128,512]{3,2,1,0:T(8,128)(2,1)}, bf16[1,2,128,2048]{3,2,1,0:T(8,128)(2,1)}) custom-call(bf16[1,2,128,2048]{3,2,1,0:T(8,128)(2,1)} %q_ref.7, bf16[2,1,2,128,512]{4,3,2,1,0:T(8,128)(2,1)} %get-tuple-element.18.kvo_ref, bf16[2,1,2,128,512]{4,3,2,1,0:T(8,128)(2,1)} %copy-done.4, ...), custom_call_target="tpu_custom_call" | custom-call | tf_op jit(solution)/shard_map/pallas_call | solution.py:241
  101.2 1.9 %collective-permute-start.3 = (bf16[2,1,128,512]{3,2,1,0:T(8,128)(2,1)}, bf16[2,1,128,512]{3,2,1,0:T(8,128)(2,1)S(1)}, u32[]{:S(2)}, u32[]{:S(2)}) collective-permute-start(bf16[2,1,128,512]{3,2,1,0:T(8,128)(2,1)} %get-tuple-element.28), channel_id=1, source_target_pairs={{1,0},{2,1},{3,2},{4,3},{5,4},{6,5},{7,6},{8,7},{9,8},{10,9},{11,1... | collective-permute-start | bytes 786440 | tf_op jit(solution)/shard_map/ppermute | solution.py:20
  103.1 0.0 copy-start.6
  103.1 0.0 copy-start.7
  103.1 6.1 %shard_map.81 = (f32[1,128,512]{2,1,0:T(8,128)}, f32[1,128,512]{2,1,0:T(8,128)}, bf16[2,1,128,512]{3,2,1,0:T(8,128)(2,1)}, bf16[1,2,128,2048]{3,2,1,0:T(8,128)(2,1)}) custom-call(bf16[1,2,128,2048]{3,2,1,0:T(8,128)(2,1)} %q_ref.7, bf16[2,1,2,128,512]{4,3,2,1,0:T(8,128)(2,1)} %get-tuple-element.18.kvo_ref, ...), custom_call_target="tpu_custom_call", output_to_operand_aliasing={{3}: (6, {})} | custom-call | tf_op jit(solution)/shard_map/pallas_call | solution.py:241
  109.2 1.9 %collective-permute-start.4 = (bf16[2,1,128,512]{3,2,1,0:T(8,128)(2,1)}, bf16[2,1,128,512]{3,2,1,0:T(8,128)(2,1)S(1)}, u32[]{:S(2)}, u32[]{:S(2)}) collective-permute-start(bf16[2,1,128,512]{3,2,1,0:T(8,128)(2,1)} %get-tuple-element.30), channel_id=1, source_target_pairs={{1,0},{2,1},{3,2},{4,3},{5,4},{6,5},{7,6},{8,7},{9,8},{10,9},{11,1... | collective-permute-start | bytes 786440 | tf_op jit(solution)/shard_map/ppermute | solution.py:20
  111.2 0.0 collective-permute-done.3
  111.2 0.0 copy-done.6
  111.2 0.0 copy-done.7
  111.2 0.1 fusion.6
  111.3 7.8 %collective-permute-done.4 = bf16[2,1,128,512]{3,2,1,0:T(8,128)(2,1)S(1)} collective-permute-done((bf16[2,1,128,512]{3,2,1,0:T(8,128)(2,1)}, bf16[2,1,128,512]{3,2,1,0:T(8,128)(2,1)S(1)}, u32[]{:S(2)}, u32[]{:S(2)}) %collective-permute-start.4) | collective-permute-done | bytes 262176 | tf_op jit(solution)/shard_map/ppermute | solution.py:20
  119.1 1.1 fusion.7
  120.2 0.8 pad_maximum_fusion
  (6 shorter events, 0.1 us)
Async XLA Ops:
  0.6 10.0 %copy-start = (bf16[2,128,2048]{2,1,0:T(8,128)(2,1)S(1)}, bf16[2,128,2048]{2,1,0:T(8,128)(2,1)}, u32[]{:S(2)}) copy-start(bf16[2,128,2048]{2,1,0:T(8,128)(2,1)} %param.8) | copy-start | bytes 3145732
  3.6 40.1 %copy-start.8 = (s32[2,4096]{1,0:T(2,128)S(1)}, s32[2,4096]{1,0:T(2,128)}, u32[]{:S(2)}) copy-start(s32[2,4096]{1,0:T(2,128)} %param.9) | copy-start | bytes 98308
  3.6 34.3 %all-to-all-start = ((bf16[16,128,512]{2,1,0:T(8,128)(2,1)}), bf16[16,128,512]{2,1,0:T(8,128)(2,1)S(1)}, u32[]{:S(2)}, u32[]{:S(2)}) async-start(bf16[16,128,512]{2,1,0:T(8,128)(2,1)} %get-tuple-element.19), calls=%async_computation | async-start | bytes 4194304 | tf_op jit(solution)/shard_map/all_to_all | solution.py:291
  37.8 11.9 %copy-start.1 = (bf16[16,128,512]{2,1,0:T(8,128)(2,1)}, bf16[16,128,512]{2,1,0:T(8,128)(2,1)S(1)}, u32[]{:S(2)}) copy-start(bf16[16,128,512]{2,1,0:T(8,128)(2,1)S(1)} %all-to-all-done.x_ref) | copy-start | bytes 6291460
  37.9 11.9 %collective-permute-start.2 = (bf16[8,128,256]{2,1,0:T(8,128)(2,1)S(1)}, bf16[8,128,256]{2,1,0:T(8,128)(2,1)}, u32[]{:S(2)}, u32[]{:S(2)}) collective-permute-start(bf16[8,128,256]{2,1,0:T(8,128)(2,1)S(1)} %slice.25), channel_id=1, source_target_pairs={{0,1},{1,2},{2,3},{3,4},{4,5},{5,6},{6,7},{7,8},{8,9},{9,10},{10,1... | collective-permute-start | bytes 1572872 | tf_op jit(solution)/shard_map/ppermute | solution.py:20
  44.5 12.3 %collective-permute-start.1 = (bf16[7,128,256]{2,1,0:T(8,128)(2,1)}, bf16[7,128,256]{2,1,0:T(8,128)(2,1)}, u32[]{:S(2)}, u32[]{:S(2)}) collective-permute-start(bf16[7,128,256]{2,1,0:T(8,128)(2,1)} %slice.24), channel_id=1, source_target_pairs={{0,1},{1,2},{2,3},{3,4},{4,5},{5,6},{6,7},{7,8},{8,9},{9,10},{10,1... | collective-permute-start | bytes 1376264 | tf_op jit(solution)/shard_map/ppermute | solution.py:20
  46.5 17.0 %copy-start.5 = (s32[2,128,256]{2,1,0:T(8,128)}, s32[2,128,256]{2,1,0:T(8,128)S(1)}, u32[]{:S(2)}) copy-start(s32[2,128,256]{2,1,0:T(8,128)S(1)} %and_convert_fusion.m_ref) | copy-start | bytes 786436
  56.8 14.7 %copy-start.3 = (bf16[2,1,2,128,512]{4,3,2,1,0:T(8,128)(2,1)S(1)}, bf16[2,1,2,128,512]{4,3,2,1,0:T(8,128)(2,1)}, u32[]{:S(2)}) copy-start(bf16[2,1,2,128,512]{4,3,2,1,0:T(8,128)(2,1)} %get-tuple-element.18.kvo_ref) | copy-start | bytes 1572868
  63.5 30.7 %all-to-all-start.1 = ((bf16[16,128,256]{2,1,0:T(8,128)(2,1)}), bf16[16,128,256]{2,1,0:T(8,128)(2,1)S(1)}, u32[]{:S(2)}, u32[]{:S(2)}) async-start(bf16[16,128,256]{2,1,0:T(8,128)(2,1)} %get-tuple-element.22), calls=%async_computation.1 | async-start | bytes 2097152 | tf_op jit(solution)/shard_map/all_to_all | solution.py:303
  71.4 12.1 %collective-permute-start = (bf16[2,1,2,128,512]{4,3,2,1,0:T(8,128)(2,1)S(1)}, bf16[2,1,2,128,512]{4,3,2,1,0:T(8,128)(2,1)S(1)}, u32[]{:S(2)}, u32[]{:S(2)}) collective-permute-start(bf16[2,1,2,128,512]{4,3,2,1,0:T(8,128)(2,1)S(1)} %copy-done.3), channel_id=1, source_target_pairs={{0,1},{1,2},{2,3},{3,4},{4,5},{5,6},{6,7},{7,8},{8,9},{9,10},{10,1... | collective-permute-start | bytes 1572872 | tf_op jit(solution)/shard_map/ppermute | solution.py:20
  83.5 0.9 copy-start.4
  94.2 1.0 copy-start.2
  101.2 10.0 %collective-permute-start.3 = (bf16[2,1,128,512]{3,2,1,0:T(8,128)(2,1)}, bf16[2,1,128,512]{3,2,1,0:T(8,128)(2,1)S(1)}, u32[]{:S(2)}, u32[]{:S(2)}) collective-permute-start(bf16[2,1,128,512]{3,2,1,0:T(8,128)(2,1)} %get-tuple-element.28), channel_id=1, source_target_pairs={{1,0},{2,1},{3,2},{4,3},{5,4},{6,5},{7,6},{8,7},{9,8},{10,9},{11,1... | collective-permute-start | bytes 786440 | tf_op jit(solution)/shard_map/ppermute | solution.py:20
  103.1 8.1 %copy-start.6 = (f32[1,128,512]{2,1,0:T(8,128)S(1)}, f32[1,128,512]{2,1,0:T(8,128)}, u32[]{:S(2)}) copy-start(f32[1,128,512]{2,1,0:T(8,128)} %get-tuple-element.27) | copy-start | bytes 786436
  103.1 8.1 %copy-start.7 = (f32[1,128,512]{2,1,0:T(8,128)S(1)}, f32[1,128,512]{2,1,0:T(8,128)}, u32[]{:S(2)}) copy-start(f32[1,128,512]{2,1,0:T(8,128)} %get-tuple-element.31) | copy-start | bytes 786436
  109.2 9.9 %collective-permute-start.4 = (bf16[2,1,128,512]{3,2,1,0:T(8,128)(2,1)}, bf16[2,1,128,512]{3,2,1,0:T(8,128)(2,1)S(1)}, u32[]{:S(2)}, u32[]{:S(2)}) collective-permute-start(bf16[2,1,128,512]{3,2,1,0:T(8,128)(2,1)} %get-tuple-element.30), channel_id=1, source_target_pairs={{1,0},{2,1},{3,2},{4,3},{5,4},{6,5},{7,6},{8,7},{9,8},{10,9},{11,1... | collective-permute-start | bytes 786440 | tf_op jit(solution)/shard_map/ppermute | solution.py:20
